TPU v7x, 32 devices: a whole 2x2x4 slice. The times are simulated.
32 devices in a mesh: req: 8 (over z, x), head: 4 (over y, core).
Axes of the slice: x: 2, y: 2, z: 4, core: 2. Of those that a mesh axis runs over, the one named last changes fastest.
Arguments:
- tokens: bfloat16 [256, 2048], P('req'), may hold values from -6 to 6
- norm_gain: float32 [2048], replicated, may hold values from 0.1 to 1.9
- key_value_weight: bfloat16 [2048, 16, 2, 128], P(None, 'head'), may hold values from -0.125 to 0.125
- query_weight: bfloat16 [32, 2048, 512], P('req', None, 'head'), may hold values from -0.125 to 0.125
- output_weight: bfloat16 [32, 512, 2048], P('req', 'head'), may hold values from -0.5 to 0.5
- cache_keys: bfloat16 [512, 128, 16, 128], P('req', None, 'head'), may hold values from -552 to 552
- cache_values: bfloat16 [512, 128, 16, 128], P('req', None, 'head'), may hold values from -6 to 6
- cache_length: int32 [256], P('req'), may hold values from 16 to 4096, as said below
- page_table: int32 [256, 32], P('req'), may hold values from 0 to 511, as said below
- expert_choice: int32 [256, 2], P('req'), may hold values from 0 to 7, all different within a row; in each aligned block of 32 rows (0 to 31, 32 to 63, ...) at most 12 rows name the same one
- expert_gate: float32 [256, 2], P('req'), may hold values from 0.1 to 1
- live_mask: int32 [256], P('req'), may hold values 0 or 1
Outputs:
- attention_out: bfloat16 [256, 2048], P('req', 'head')
Inputs may be any that keep to these rules, and one draw needn't show every extreme that they name: `cache_length`: request group g holds requests g * 32 to (g+1) * 32 - 1. Every request holds 16 to 64 cached tokens, except that in 3 * (number of groups) // 4 groups exactly one request holds 2048 to 4096; some request holds exactly 4096. `page_table`: group g owns pages g * 64 to (g+1) * 64 - 1, and row r lists, in order, the ceil(cache_length[r] / 128) distinct pages of request r, all owned by its group; no page serves two requests; later entries repeat the request's first page. A group uses at most 63 pages, and some group uses exactly that many. `expert_choice`: among the tokens of one request group, no attention expert is chosen more than 12 times, and in some group one expert is chosen exactly 12 times; a token's choices differ.
All inputs are finite; a program needn't handle non-finite values. No bound on the sum of `live_mask` on one device may be relied on, other than what follows from the above.
Results may differ from a plain program's by a relative error of at most 0.007.
The roundings to bfloat16 on the way count: a program that leaves them out, or rounds other values in their place, can miss the bound.
Values may be sent and summed in bfloat16 or wider, within the bound.
No kernel may reach another device: no remote copies, remote signals or barrier semaphores. Data moves between devices by JAX's collectives and lax.ppermute only.
A program may use at most 128 MiB of HBM per device.

v0:
```python
import jax
import jax.numpy as jnp
from jax import lax
from jax.sharding import PartitionSpec as P

AEXP = 8
CAP = 12


eps = 1e-06
theta = 10000.0


def rotate(vectors, positions):
    half_width = vectors.shape[-1] // 2
    frequency = theta ** (-(jnp.arange(half_width, dtype=jnp.float32) * 2.0) / vectors.shape[-1])
    angles = positions.astype(jnp.float32)[..., None] * frequency
    cosine = jnp.cos(angles)
    sine_part = jnp.sin(angles)
    first_half = vectors[..., :half_width]
    second = vectors[..., half_width:]
    return jnp.concatenate(
        [first_half * cosine - second * sine_part, second * cosine + first_half * sine_part],
        axis=-1,
    )


def body(
    tokens,
    norm_gain,
    key_value_weight,
    query_weight,
    output_weight,
    cache_keys,
    cache_values,
    cache_length,
    page_table,
    expert_choice,
    expert_gate,
    live_mask,
):
    groups = lax.axis_size("req")
    group_index = lax.axis_index("req")
    row_count = tokens.shape[0]
    model_width = tokens.shape[1]
    choices_each = expert_choice.shape[1]
    heads_here = key_value_weight.shape[1]
    head_dim = key_value_weight.shape[3]
    pairs_here = query_weight.shape[0]
    pages_here = cache_keys.shape[0]
    page_len = cache_keys.shape[1]
    max_pages = page_table.shape[1]
    experts = AEXP
    capacity = CAP
    as_float = tokens.astype(jnp.float32)
    normed = (
        as_float
        * lax.rsqrt(jnp.mean(as_float * as_float, axis=-1, keepdims=True) + eps)
        * norm_gain
    ).astype(jnp.bfloat16)
    flat_expert = expert_choice.reshape(-1)
    onehot = (flat_expert[:, None] == jnp.arange(experts)[None, :]).astype(jnp.int32)
    before = jnp.cumsum(onehot, axis=0) - onehot
    slot_index = jnp.sum(before * onehot, axis=1)
    target = flat_expert * capacity + slot_index
    select = target[None, :] == jnp.arange(experts * capacity)[:, None]
    select_rows = select.astype(jnp.bfloat16)
    repeated = jnp.repeat(normed, choices_each, axis=0)
    sendbuf = jnp.dot(select_rows, repeated, preferred_element_type=jnp.float32).astype(
        jnp.bfloat16
    )
    sendbuf = jnp.broadcast_to(
        sendbuf.reshape(experts, 1, capacity, model_width),
        (experts, heads_here, capacity, model_width),
    )
    sendbuf = sendbuf.reshape(groups, pairs_here, capacity, model_width)
    queries_far = jnp.einsum(
        "spnd,pdh->spnh",
        lax.all_to_all(sendbuf, "req", split_axis=0, concat_axis=0, tiled=True),
        query_weight,
        preferred_element_type=jnp.float32,
    ).astype(jnp.bfloat16)
    key_value = jnp.dot(
        normed,
        key_value_weight.reshape(model_width, heads_here * 2 * head_dim),
        preferred_element_type=jnp.float32,
    )
    key_value = key_value.reshape(row_count, heads_here, 2, head_dim)
    key_new = rotate(key_value[:, :, 0], cache_length[:, None]).astype(jnp.bfloat16)
    value_new = key_value[:, :, 1].astype(jnp.bfloat16)
    local_ids = page_table - group_index * pages_here
    page_used = jnp.arange(max_pages)[None, :] * page_len < cache_length[:, None]
    page_match = page_used[:, :, None] & (
        local_ids[:, :, None] == jnp.arange(pages_here)[None, None, :]
    )
    owned_pages = jnp.any(page_match, axis=1)
    page_taken = jnp.any(owned_pages, axis=0)
    page_owner = jnp.sum(
        owned_pages.astype(jnp.int32) * jnp.arange(row_count, dtype=jnp.int32)[:, None], axis=0
    )
    page_start = jnp.sum(
        page_match.astype(jnp.int32)
        * (jnp.arange(max_pages, dtype=jnp.int32) * page_len)[None, :, None],
        axis=(0, 1),
    )
    page_limit = cache_length[page_owner]
    in_range = page_taken[:, None] & (
        page_start[:, None] + jnp.arange(page_len)[None, :] < page_limit[:, None]
    )
    queries = lax.all_to_all(queries_far, "req", split_axis=0, concat_axis=0, tiled=True)
    queries = (
        queries.reshape(experts, heads_here, capacity, head_dim)
        .transpose(0, 2, 1, 3)
        .reshape(experts * capacity, heads_here, head_dim)
    )
    raw_query = queries[target].reshape(row_count, choices_each, heads_here, head_dim)
    query_rot = rotate(raw_query.astype(jnp.float32), cache_length[:, None, None]).astype(
        jnp.bfloat16
    )
    score_scale = 1.0 / head_dim**0.5
    page_queries = query_rot[page_owner]
    scores = (
        jnp.einsum("pkhd,pthd->pkht", page_queries, cache_keys, preferred_element_type=jnp.float32)
        * score_scale
    )
    scores = jnp.where(in_range[:, None, None, :], scores, -jnp.inf)
    fresh_score = (
        jnp.einsum("rkhd,rhd->rkh", query_rot, key_new, preferred_element_type=jnp.float32)
        * score_scale
    )
    page_top = jnp.max(scores, axis=3)
    owned_top = jnp.max(jnp.where(owned_pages[:, :, None, None], page_top[None], -jnp.inf), axis=1)
    row_top = jnp.maximum(owned_top, fresh_score)
    weights = jnp.exp(scores - row_top[page_owner][..., None])
    fresh_weight = jnp.exp(fresh_score - row_top)
    owned_float = owned_pages.astype(jnp.float32)
    denominator = (
        jnp.einsum(
            "rp,pkh->rkh", owned_float, jnp.sum(weights, axis=3), precision=lax.Precision.HIGHEST
        )
        + fresh_weight
    )
    weights_rounded = weights.astype(jnp.bfloat16)
    fresh_rounded = lax.optimization_barrier(fresh_weight.astype(jnp.bfloat16)).astype(jnp.float32)
    page_context = jnp.einsum(
        "pkht,pthd->pkhd", weights_rounded, cache_values, preferred_element_type=jnp.float32
    )
    accumulated = jnp.einsum(
        "rp,pkhd->rkhd", owned_float, page_context, precision=lax.Precision.HIGHEST
    )
    accumulated = accumulated + fresh_rounded[..., None] * value_new.astype(jnp.float32)[:, None]
    context = (accumulated / denominator[..., None]).astype(jnp.bfloat16)
    context_flat = context.reshape(row_count * choices_each, heads_here * head_dim)
    context_buf = jnp.dot(select_rows, context_flat, preferred_element_type=jnp.float32).astype(
        jnp.bfloat16
    )
    context_buf = context_buf.reshape(experts, capacity, heads_here, head_dim).transpose(0, 2, 1, 3)
    context_buf = context_buf.reshape(groups, pairs_here, capacity, head_dim)
    partial_far = jnp.einsum(
        "spnh,phd->spnd",
        lax.all_to_all(context_buf, "req", split_axis=0, concat_axis=0, tiled=True),
        output_weight,
        preferred_element_type=jnp.float32,
    )
    gate_flat = expert_gate.reshape(-1)
    spread = (
        jnp.where(select, gate_flat[None, :], jnp.float32(0.0))
        .reshape(experts * capacity, row_count, choices_each)
        .sum(axis=2)
        .T
    )
    alive_rows = live_mask.astype(jnp.float32)[:, None]
    returned = lax.all_to_all(partial_far, "req", split_axis=0, concat_axis=0, tiled=True)
    summed = returned.reshape(experts, heads_here, capacity, model_width).sum(axis=1)
    own_sum = jnp.dot(
        spread, summed.reshape(experts * capacity, model_width), precision=lax.Precision.HIGHEST
    )
    result = lax.psum_scatter(own_sum, "head", scatter_dimension=1, tiled=True)
    return (result * alive_rows).astype(jnp.bfloat16)


def solution(mesh):
    return jax.shard_map(
        body,
        mesh=mesh,
        in_specs=(
            P("req", None),
            P(),
            P(None, "head", None, None),
            P("req", None, "head"),
            P("req", "head", None),
            P("req", None, "head", None),
            P("req", None, "head", None),
            P("req"),
            P("req", None),
            P("req", None),
            P("req", None),
            P("req"),
        ),
        out_specs=P("req", "head"),
        check_vma=False,
    )
```

profile of v0, /device:TPU:0, one launch (start us, length us, event | category | flops | bytes accessed | tf_op | source)
XLA Modules:
  0.0 213.2 jit_solution(9936694887595753030)
XLA Ops:
  6.5 0.9 copy.60
  7.9 1.0 fusion.35
  9.0 1.0 fusion.37
  10.6 1.9 broadcast_in_dim.44
  12.6 7.3 %all-to-all-start = ((bf16[8,4,12,2048]{3,1,2,0:T(4,128)(2,1)}), bf16[8,4,12,2048]{3,1,2,0:T(4,128)(2,1)}, u32[]{:S(2)}, u32[]{:S(2)}) async-start(bf16[8,4,12,2048]{3,1,2,0:T(4,128)(2,1)} %broadcast_in_dim.44), calls=%async_computation | async-start | bytes 3145728 | tf_op jit(solution)/shard_map/all_to_all | solution.py:79
  20.2 0.4 fusion.33
  20.6 0.8 gather_fusion
  21.4 7.7 %reshape.323 = bf16[2048,1024]{1,0:T(8,128)(2,1)} reshape(bf16[2048,4,2,128]{3,2,1,0:T(2,128)(2,1)} %param.14) | data formatting | bytes 8388608 | tf_op jit(solution)/shard_map/reshape | solution.py:85
  29.1 6.5 %copy.68 = bf16[1024,2048]{1,0:T(8,128)(2,1)} copy(bf16[1024,2048]{0,1:T(8,128)(2,1)} %bitcast.100) | data formatting | bytes 8388608 | tf_op jit(solution)/shard_map/dot_general | solution.py:83
  35.8 3.5 %fusion.42 = f32[32,4,2,128]{3,0,2,1:T(8,128)S(1)} fusion(bf16[4,2,128,2048]{3,2,1,0:T(8,128)(2,1)} %bitcast.99, bf16[32,2048]{1,0:T(8,128)(2,1)S(1)} %fusion.37), kind=kOutput, calls=%fused_computation.38 | convolution fusion | flops 134217728 | bytes 4456448 | tf_op jit(solution)/shard_map/dot_general | solution.py:83
  39.9 17.1 %all-to-all-done = bf16[8,4,12,2048]{3,1,2,0:T(4,128)(2,1)} async-done(((bf16[8,4,12,2048]{3,1,2,0:T(4,128)(2,1)}), bf16[8,4,12,2048]{3,1,2,0:T(4,128)(2,1)}, u32[]{:S(2)}, u32[]{:S(2)}) %all-to-all-start) | async-done | bytes 1572896 | tf_op jit(solution)/shard_map/all_to_all | solution.py:79
  56.9 4.0 %fusion.19 = bf16[8,4,12,128]{3,2,0,1:T(8,128)(2,1)S(1)} fusion(bf16[4,2048,128]{2,1,0:T(8,128)(2,1)} %param.15, bf16[8,4,12,2048]{3,1,2,0:T(4,128)(2,1)} %all-to-all-done), kind=kOutput, calls=%fused_computation.18 | convolution fusion | flops 201375744 | bytes 3768320 | tf_op jit(solution)/shard_map/spnd,pdh->spnh/dot_general | solution.py:77
  60.9 0.7 copy.64
  61.7 3.6 %all-to-all-start.1 = ((bf16[8,4,12,128]{3,1,2,0:T(4,128)(2,1)}), bf16[8,4,12,128]{3,1,2,0:T(4,128)(2,1)S(1)}, u32[]{:S(2)}, u32[]{:S(2)}) async-start(bf16[8,4,12,128]{3,1,2,0:T(4,128)(2,1)} %copy.64), calls=%async_computation.1 | async-start | bytes 196608 | tf_op jit(solution)/shard_map/all_to_all | solution.py:110
  65.4 7.0 %all-to-all-done.1 = bf16[8,4,12,128]{3,1,2,0:T(4,128)(2,1)S(1)} async-done(((bf16[8,4,12,128]{3,1,2,0:T(4,128)(2,1)}), bf16[8,4,12,128]{3,1,2,0:T(4,128)(2,1)S(1)}, u32[]{:S(2)}, u32[]{:S(2)}) %all-to-all-start.1) | async-done | bytes 98336 | tf_op jit(solution)/shard_map/all_to_all | solution.py:110
  72.4 0.7 gather_fusion.1
  73.4 0.7 gather_fusion.2
  74.1 7.9 %fusion.65 = (f32[64,2,4]{1,2,0:T(4,128)S(1)}, f32[64,2,4,128]{3,1,2,0:T(2,128)S(1)}) fusion(bf16[64,128,4,128]{3,2,1,0:T(4,128)(2,1)} %param.17, bf16[64,2,4,128]{3,2,1,0:T(4,128)(2,1)S(1)} %gather_fusion.2, pred[64,128]{1,0:T(8,128)(4,1)S(1)} %fusion.55), kind=kOutput, calls=%fused_computation.95 | convolution fusion | flops 16973312 | bytes 8792064 | tf_op jit(solution)/shard_map/pkhd,pthd->pkht/dot_general | solution.py:123
  82.8 0.7 gather_fusion.3
  83.4 0.5 copy.70
  83.9 0.7 fusion.39
  84.7 5.7 %fusion.8 = f32[64,2,4,128]{3,1,2,0:T(2,128)S(1)} fusion(bf16[64,128,4,128]{3,2,1,0:T(4,128)(2,1)} %param.18, f32[64,2,4,128]{3,1,2,0:T(2,128)S(1)} %get-tuple-element.18, f32[64,2,4]{1,2,0:T(4,128)S(1)} %copy.70), kind=kOutput, calls=%fused_computation.14 | convolution fusion | flops 16908288 | bytes 8914944 | tf_op jit(solution)/shard_map/pkht,pthd->pkhd/dot_general | solution.py:145
  91.2 9.5 %all_to_all.20 = bf16[8,4,12,128]{3,1,2,0:T(4,128)(2,1)S(1)} all-to-all(bf16[8,4,12,128]{3,1,2,0:T(4,128)(2,1)S(1)} %bitcast.101), channel_id=1, replica_groups=mesh['req'=8,'head'=4] {'req'}, dimensions={0} | all-to-all | bytes 196608 | tf_op jit(solution)/shard_map/all_to_all | solution.py:161
  100.7 0.7 convolution_bitcast_fusion
  101.4 3.7 %copy.76 = f32[8,4,12,2048]{3,1,2,0:T(4,128)} copy(f32[8,4,12,2048]{3,2,0,1:T(8,128)S(1)} %convolution_bitcast_fusion) | data formatting | bytes 6291456 | tf_op jit(solution)/shard_map/spnh,phd->spnd/transpose | solution.py:159
  105.2 4.6 %all-to-all-start.3 = ((f32[8,4,12,2048]{3,1,2,0:T(4,128)}), f32[8,4,12,2048]{3,1,2,0:T(4,128)}, u32[]{:S(2)}, u32[]{:S(2)}) async-start(f32[8,4,12,2048]{3,1,2,0:T(4,128)} %copy.76), calls=%async_computation.3 | async-start | bytes 6291456 | tf_op jit(solution)/shard_map/all_to_all | solution.py:173
  110.2 68.1 %all-to-all-done.3 = f32[8,4,12,2048]{3,1,2,0:T(4,128)} async-done(((f32[8,4,12,2048]{3,1,2,0:T(4,128)}), f32[8,4,12,2048]{3,1,2,0:T(4,128)}, u32[]{:S(2)}, u32[]{:S(2)}) %all-to-all-start.3) | async-done | bytes 3145760 | tf_op jit(solution)/shard_map/all_to_all | solution.py:173
  178.4 3.9 %reduce_sum.78 = f32[8,12,2048]{2,1,0:T(8,128)S(1)} reduce(f32[8,4,12,2048]{3,1,2,0:T(4,128)} %all-to-all-done.3, f32[]{:T(128)} %constant.19.clone.1), dimensions={1}, to_apply=%region_11.12 | reduce | flops 589824 | bytes 3932164 | tf_op jit(solution)/shard_map/reduce_sum | solution.py:174
  182.3 1.0 reshape.326
  183.3 2.3 %fusion.67 = f32[32,2048]{1,0:T(8,128)} fusion(f32[96,32]{0,1:T(8,128)S(1)} %select_reduce_fusion.2, f32[96,2048]{1,0:T(8,128)} %reshape.326), kind=kOutput, calls=%fused_computation.97 | convolution fusion | flops 75497472 | bytes 1060864 | tf_op jit(solution)/shard_map/dot_general | solution.py:175
  185.6 19.2 %reduce-scatter.2.cloned.1.call-done = f32[32,512]{1,0:T(8,128)} async-done(((f32[32,2048]{1,0:T(8,128)}), f32[32,512]{1,0:T(8,128)}) %reduce-scatter.2.cloned.1.call-update) | async-done | bytes 65552 | tf_op jit(solution)/shard_map/reduce_scatter | solution.py:178
  204.9 1.5 multiply_convert_fusion
  (62 shorter events, 4.4 us)
Async XLA Ops:
  6.5 94.2 %copy-start = (bf16[4,128,2048]{2,1,0:T(8,128)(2,1)S(1)}, bf16[4,128,2048]{2,1,0:T(8,128)(2,1)}, u32[]{:S(2)}) copy-start(bf16[4,128,2048]{2,1,0:T(8,128)(2,1)} %param.16) | copy-start | bytes 6291460
  6.5 13.4 %copy-start.1 = (s32[32]{0:T(128)S(1)}, s32[32]{0:T(128)}, u32[]{:S(2)}) copy-start(s32[32]{0:T(128)} %param.19) | copy-start | bytes 388
  7.6 12.6 %copy-start.2 = (s32[32,32]{1,0:T(8,128)S(1)}, s32[32,32]{1,0:T(8,128)}, u32[]{:S(2)}) copy-start(s32[32,32]{1,0:T(8,128)} %param.20) | copy-start | bytes 12292
  12.6 44.4 %all-to-all-start = ((bf16[8,4,12,2048]{3,1,2,0:T(4,128)(2,1)}), bf16[8,4,12,2048]{3,1,2,0:T(4,128)(2,1)}, u32[]{:S(2)}, u32[]{:S(2)}) async-start(bf16[8,4,12,2048]{3,1,2,0:T(4,128)(2,1)} %broadcast_in_dim.44), calls=%async_computation | async-start | bytes 3145728 | tf_op jit(solution)/shard_map/all_to_all | solution.py:79
  61.7 10.8 %all-to-all-start.1 = ((bf16[8,4,12,128]{3,1,2,0:T(4,128)(2,1)}), bf16[8,4,12,128]{3,1,2,0:T(4,128)(2,1)S(1)}, u32[]{:S(2)}, u32[]{:S(2)}) async-start(bf16[8,4,12,128]{3,1,2,0:T(4,128)(2,1)} %copy.64), calls=%async_computation.1 | async-start | bytes 196608 | tf_op jit(solution)/shard_map/all_to_all | solution.py:110
  105.2 4.9 %copy-start.3 = (f32[32,2]{0,1:T(2,128)S(1)}, f32[32,2]{0,1:T(2,128)}, u32[]{:S(2)}) copy-start(f32[32,2]{0,1:T(2,128)} %param.22) | copy-start | bytes 772
  105.2 73.2 %all-to-all-start.3 = ((f32[8,4,12,2048]{3,1,2,0:T(4,128)}), f32[8,4,12,2048]{3,1,2,0:T(4,128)}, u32[]{:S(2)}, u32[]{:S(2)}) async-start(f32[8,4,12,2048]{3,1,2,0:T(4,128)} %copy.76), calls=%async_computation.3 | async-start | bytes 6291456 | tf_op jit(solution)/shard_map/all_to_all | solution.py:173
  109.8 75.9 %copy-start.4 = (s32[32]{0:T(128)S(1)}, s32[32]{0:T(128)}, u32[]{:S(2)}) copy-start(s32[32]{0:T(128)} %param.23) | copy-start | bytes 388
  109.8 95.1 %reduce-scatter.2.cloned.1.call-start = ((), (), s32[]{:S(2)}) async-start(), calls=%async_computation.5 | async-start | bytes 327680 | tf_op jit(solution)/shard_map/reduce_scatter | solution.py:178
Sparse Core Ops, SparseCore 0:
  185.7 19.0 reduce-scatter.1
where the time goes:
time: 214 us; the launch traced here: 213 us
  waiting for transfers between devices  111 us (52%)
  local copies, waits for them, and re-layouts  27 us (13%)
  matrix products  25.3 us (12%)
  starting transfers between devices  15.7 us (7%)
  between operations  13.7 us (6%)
  other arithmetic  10.5 us (5%)
  blocking collectives  9.51 us (4%)
    all_to_all x1, waiting for transfers between devices, body(): lax.all_to_all(partial_far, 'req', split_axis=0, concat_axis=0, tiled=True)  68.1 us
    reduce_scatter x1, waiting for transfers between devices, body(): result = lax.psum_scatter(own_sum, 'head', scatter_dimension=1, tiled=True)  19.2 us
    all_to_all x1, waiting for transfers between devices, body(): lax.all_to_all(sendbuf, 'req', split_axis=0, concat_axis=0, tiled=True)  17.1 us
    all_to_all x1, blocking collectives, body(): lax.all_to_all(context_buf, 'req', split_axis=0, concat_axis=0, tiled=True)  9.51 us
    dot_general x1, matrix products, body(): jnp.einsum('pkhd,pthd->pkht', page_queries, cache_keys, preferred_element...  7.94 us
    reshape x1, local copies, waits for them, and re-layouts, body(): key_value_weight.reshape(model_width, heads_here * 2 * head_dim)  7.71 us
    all_to_all x1, starting transfers between devices, body(): lax.all_to_all(sendbuf, 'req', split_axis=0, concat_axis=0, tiled=True)  7.25 us
    all_to_all x1, waiting for transfers between devices, body(): lax.all_to_all(queries_far, 'req', split_axis=0, concat_axis=0, tiled=True)  7.03 us
  transfers between devices with their start and end apart: 4, of which 4 were waited for; matrix products, arithmetic and copies ran while one was open for 9% of the time, Pallas kernels for 0%

commit v1 on v0

--- a/solution.py
+++ b/solution.py
@@ -69,23 +69,21 @@
     sendbuf = jnp.dot(select_rows, repeated, preferred_element_type=jnp.float32).astype(
         jnp.bfloat16
     )
+    replicas = groups // experts
     sendbuf = jnp.broadcast_to(
         sendbuf.reshape(experts, 1, capacity, model_width),
-        (experts, heads_here, capacity, model_width),
-    )
-    sendbuf = sendbuf.reshape(groups, pairs_here, capacity, model_width)
+        (experts, replicas, capacity, model_width),
+    )
+    sendbuf = sendbuf.reshape(groups, capacity, model_width)
     queries_far = jnp.einsum(
-        "spnd,pdh->spnh",
+        "snd,pdh->spnh",
         lax.all_to_all(sendbuf, "req", split_axis=0, concat_axis=0, tiled=True),
         query_weight,
         preferred_element_type=jnp.float32,
     ).astype(jnp.bfloat16)
-    key_value = jnp.dot(
-        normed,
-        key_value_weight.reshape(model_width, heads_here * 2 * head_dim),
-        preferred_element_type=jnp.float32,
-    )
-    key_value = key_value.reshape(row_count, heads_here, 2, head_dim)
+    key_value = jnp.einsum(
+        "rf,fhkd->rhkd", normed, key_value_weight, preferred_element_type=jnp.float32
+    )
     key_new = rotate(key_value[:, :, 0], cache_length[:, None]).astype(jnp.bfloat16)
     value_new = key_value[:, :, 1].astype(jnp.bfloat16)
     local_ids = page_table - group_index * pages_here
@@ -157,7 +155,7 @@
     context_buf = context_buf.reshape(experts, capacity, heads_here, head_dim).transpose(0, 2, 1, 3)
     context_buf = context_buf.reshape(groups, pairs_here, capacity, head_dim)
     partial_far = jnp.einsum(
-        "spnh,phd->spnd",
+        "spnh,phd->snd",
         lax.all_to_all(context_buf, "req", split_axis=0, concat_axis=0, tiled=True),
         output_weight,
         preferred_element_type=jnp.float32,
@@ -171,7 +169,7 @@
     )
     alive_rows = live_mask.astype(jnp.float32)[:, None]
     returned = lax.all_to_all(partial_far, "req", split_axis=0, concat_axis=0, tiled=True)
-    summed = returned.reshape(experts, heads_here, capacity, model_width).sum(axis=1)
+    summed = returned.reshape(experts, replicas, capacity, model_width).sum(axis=1)
     own_sum = jnp.dot(
         spread, summed.reshape(experts * capacity, model_width), precision=lax.Precision.HIGHEST
     )

time: 214 us -> 135 us (0.63)
  waiting for transfers between devices: 111 us -> 58.8 us
  local copies, waits for them, and re-layouts: 27 us -> 7.82 us
  other arithmetic: 10.5 us -> 6.56 us
    all_to_all x1, waiting for transfers between devices: 68.1 us -> 23.6 us  [body(): lax.all_to_all(partial_far, 'req', split_axis=0, concat_axis=0, tiled=True)]
    all_to_all x1, waiting for transfers between devices: 17.1 us -> 9.18 us  [body(): lax.all_to_all(sendbuf, 'req', split_axis=0, concat_axis=0, tiled=True)]
    reshape x1 -> x0, local copies, waits for them, and re-layouts: 7.71 us -> none  [body(): key_value_weight.reshape(model_width, heads_here * 2 * head_dim)]
    dot_general x1 -> x0, local copies, waits for them, and re-layouts: 6.52 us -> none  [body(): jnp.dot(normed, key_value_weight.reshape(model_width, heads_here * 2 * he...]
    reduce_sum x1 -> x0, other arithmetic: 3.93 us -> none  [body(): returned.reshape(experts, heads_here, capacity, model_width).sum(axis=1)]
    transpose x1 -> x0, local copies, waits for them, and re-layouts: 3.75 us -> none  [body(): jnp.einsum('spnh,phd->spnd', lax.all_to_all(context_buf, 'req', split_axi...]
  transfers between devices with their start and end apart: 4 -> 4, of which waited for: 4 -> 4; matrix products, arithmetic and copies ran while one was open for 9% -> 4% of each run, Pallas kernels for 0% -> 0%
where the time goes in v1:
time: 135 us
  waiting for transfers between devices  58.8 us (44%)
  matrix products  23.6 us (17%)
  starting transfers between devices  14.6 us (11%)
  between operations  13.7 us (10%)
  blocking collectives  9.51 us (7%)
  local copies, waits for them, and re-layouts  7.82 us (6%)
  other arithmetic  6.56 us (5%)
    all_to_all x1, waiting for transfers between devices, body(): lax.all_to_all(partial_far, 'req', split_axis=0, concat_axis=0, tiled=True)  23.6 us
    reduce_scatter x1, waiting for transfers between devices, body(): result = lax.psum_scatter(own_sum, 'head', scatter_dimension=1, tiled=True)  19.1 us
    all_to_all x1, blocking collectives, body(): lax.all_to_all(context_buf, 'req', split_axis=0, concat_axis=0, tiled=True)  9.51 us
    all_to_all x1, waiting for transfers between devices, body(): lax.all_to_all(sendbuf, 'req', split_axis=0, concat_axis=0, tiled=True)  9.18 us
    dot_general x1, matrix products, body(): jnp.einsum('pkhd,pthd->pkht', page_queries, cache_keys, preferred_element...  7.94 us
    all_to_all x1, starting transfers between devices, body(): lax.all_to_all(sendbuf, 'req', split_axis=0, concat_axis=0, tiled=True)  7.25 us
    all_to_all x1, waiting for transfers between devices, body(): lax.all_to_all(queries_far, 'req', split_axis=0, concat_axis=0, tiled=True)  7.03 us
    dot_general x1, matrix products, body(): jnp.einsum('pkht,pthd->pkhd', weights_rounded, cache_values, preferred_el...  5.72 us
  transfers between devices with their start and end apart: 4, of which 4 were waited for; matrix products, arithmetic and copies ran while one was open for 4% of the time, Pallas kernels for 0%

profile of v1, /device:TPU:0, one launch (start us, length us, event | category | flops | bytes accessed | tf_op | source)
XLA Modules:
  0.0 134.6 jit_solution(1718991433824943033)
XLA Ops:
  6.5 0.9 copy.46
  7.9 1.0 fusion.33
  9.0 1.0 fusion.35
  10.3 0.2 convolution_convert_fusion
  10.5 0.9 reshape_reshape.3
  11.4 7.3 %all-to-all-start = ((bf16[8,12,2048]{2,1,0:T(8,128)(2,1)}), bf16[8,12,2048]{2,1,0:T(8,128)(2,1)S(1)}, u32[]{:S(2)}, u32[]{:S(2)}) async-start(bf16[8,12,2048]{2,1,0:T(8,128)(2,1)} %reshape_reshape.3), calls=%async_computation | async-start | bytes 1048576 | tf_op jit(solution)/shard_map/all_to_all | solution.py:80
  19.0 0.4 fusion.31
  19.4 0.8 gather_fusion
  20.2 3.0 %fusion.4 = f32[32,4,2,128]{3,0,2,1:T(8,128)S(1)} fusion(bf16[2048,4,2,128]{3,2,1,0:T(2,128)(2,1)} %param.14, bf16[32,2048]{1,0:T(8,128)(2,1)S(1)} %fusion.35), kind=kOutput, calls=%fused_computation.8 | convolution fusion | flops 134217728 | bytes 4456448 | tf_op jit(solution)/shard_map/rf,fhkd->rhkd/dot_general | solution.py:84
  23.6 0.4 select_reduce_fusion
  24.0 9.2 %all-to-all-done = bf16[8,12,2048]{2,1,0:T(8,128)(2,1)S(1)} async-done(((bf16[8,12,2048]{2,1,0:T(8,128)(2,1)}), bf16[8,12,2048]{2,1,0:T(8,128)(2,1)S(1)}, u32[]{:S(2)}, u32[]{:S(2)}) %all-to-all-start) | async-done | bytes 393248 | tf_op jit(solution)/shard_map/all_to_all | solution.py:80
  33.1 2.1 %fusion.18 = bf16[8,4,12,128]{3,2,1,0:T(8,128)(2,1)S(1)} fusion(bf16[4,2048,128]{2,1,0:T(8,128)(2,1)} %param.15, bf16[8,12,2048]{2,1,0:T(8,128)(2,1)S(1)} %all-to-all-done), kind=kOutput, calls=%fused_computation.19 | convolution fusion | flops 201375744 | bytes 2588672 | tf_op jit(solution)/shard_map/snd,pdh->spnh/dot_general | solution.py:78
  35.2 0.7 copy.49
  35.9 3.6 %all-to-all-start.1 = ((bf16[8,4,12,128]{3,1,2,0:T(4,128)(2,1)}), bf16[8,4,12,128]{3,1,2,0:T(4,128)(2,1)S(1)}, u32[]{:S(2)}, u32[]{:S(2)}) async-start(bf16[8,4,12,128]{3,1,2,0:T(4,128)(2,1)} %copy.49), calls=%async_computation.1 | async-start | bytes 196608 | tf_op jit(solution)/shard_map/all_to_all | solution.py:108
  39.6 7.0 %all-to-all-done.1 = bf16[8,4,12,128]{3,1,2,0:T(4,128)(2,1)S(1)} async-done(((bf16[8,4,12,128]{3,1,2,0:T(4,128)(2,1)}), bf16[8,4,12,128]{3,1,2,0:T(4,128)(2,1)S(1)}, u32[]{:S(2)}, u32[]{:S(2)}) %all-to-all-start.1) | async-done | bytes 98336 | tf_op jit(solution)/shard_map/all_to_all | solution.py:108
  46.6 0.7 gather_fusion.1
  47.6 0.7 gather_fusion.2
  48.3 7.9 %fusion.62 = (f32[64,2,4]{1,2,0:T(4,128)S(1)}, f32[64,2,4,128]{3,1,2,0:T(2,128)S(1)}) fusion(bf16[64,128,4,128]{3,2,1,0:T(4,128)(2,1)} %param.17, bf16[64,2,4,128]{3,2,1,0:T(4,128)(2,1)S(1)} %gather_fusion.2, pred[64,128]{1,0:T(8,128)(4,1)S(1)} %fusion.52), kind=kOutput, calls=%fused_computation.96 | convolution fusion | flops 16973312 | bytes 8792064 | tf_op jit(solution)/shard_map/pkhd,pthd->pkht/dot_general | solution.py:121
  56.5 0.3 fusion.46
  57.0 0.7 gather_fusion.3
  57.6 0.5 copy.55
  58.1 0.8 fusion.37
  58.9 5.7 %fusion.9 = f32[64,2,4,128]{3,1,2,0:T(2,128)S(1)} fusion(bf16[64,128,4,128]{3,2,1,0:T(4,128)(2,1)} %param.18, f32[64,2,4,128]{3,1,2,0:T(2,128)S(1)} %get-tuple-element.18, f32[64,2,4]{1,2,0:T(4,128)S(1)} %copy.55), kind=kOutput, calls=%fused_computation.15 | convolution fusion | flops 16908288 | bytes 8914944 | tf_op jit(solution)/shard_map/pkht,pthd->pkhd/dot_general | solution.py:143
  64.9 0.3 fusion.22
  65.4 9.5 %all_to_all.20 = bf16[8,4,12,128]{3,1,2,0:T(4,128)(2,1)S(1)} all-to-all(bf16[8,4,12,128]{3,1,2,0:T(4,128)(2,1)S(1)} %bitcast.98), channel_id=1, replica_groups=mesh['req'=8,'head'=4] {'req'}, dimensions={0} | all-to-all | bytes 196608 | tf_op jit(solution)/shard_map/all_to_all | solution.py:159
  74.9 1.4 %convolution_bitcast_fusion = f32[8,12,2048]{2,1,0:T(8,128)} fusion(bf16[4,128,2048]{2,1,0:T(8,128)(2,1)S(1)} %copy-done, bf16[8,4,12,128]{3,1,2,0:T(4,128)(2,1)S(1)} %all_to_all.20), kind=kOutput, calls=%fused_computation.10 | convolution fusion | flops 201326592 | bytes 2981888 | tf_op jit(solution)/shard_map/spnh,phd->snd/dot_general | solution.py:157
  76.4 3.7 %all-to-all-start.3 = ((f32[8,12,2048]{2,1,0:T(8,128)}), f32[8,12,2048]{2,1,0:T(8,128)S(1)}, u32[]{:S(2)}, u32[]{:S(2)}) async-start(f32[8,12,2048]{2,1,0:T(8,128)} %convolution_bitcast_fusion), calls=%async_computation.3 | async-start | bytes 2097152 | tf_op jit(solution)/shard_map/all_to_all | solution.py:171
  80.3 23.6 %all-to-all-done.3 = f32[8,12,2048]{2,1,0:T(8,128)S(1)} async-done(((f32[8,12,2048]{2,1,0:T(8,128)}), f32[8,12,2048]{2,1,0:T(8,128)S(1)}, u32[]{:S(2)}, u32[]{:S(2)}) %all-to-all-start.3) | async-done | bytes 786464 | tf_op jit(solution)/shard_map/all_to_all | solution.py:171
  103.9 1.0 reshape.322
  104.8 2.3 %fusion.64 = f32[32,2048]{1,0:T(8,128)} fusion(f32[96,32]{0,1:T(8,128)S(1)} %select_reduce_fusion.2, f32[96,2048]{1,0:T(8,128)} %reshape.322), kind=kOutput, calls=%fused_computation.98 | convolution fusion | flops 75497472 | bytes 1060864 | tf_op jit(solution)/shard_map/dot_general | solution.py:173
  107.2 19.1 %reduce-scatter.2.cloned.1.call-done = f32[32,512]{1,0:T(8,128)} async-done(((f32[32,2048]{1,0:T(8,128)}), f32[32,512]{1,0:T(8,128)}) %reduce-scatter.2.cloned.1.call-update) | async-done | bytes 65552 | tf_op jit(solution)/shard_map/reduce_scatter | solution.py:176
  126.3 1.5 %multiply_convert_fusion = bf16[32,512]{1,0:T(8,128)(2,1)} fusion(f32[32,512]{1,0:T(8,128)} %reduce-scatter.2.cloned.1.call-done, f32[32]{0:T(128)S(1)} %convert_element_type.89), kind=kLoop, calls=%fused_computation.52 | loop fusion | flops 32768 | bytes 98432 | tf_op jit(solution)/shard_map/convert_element_type | solution.py:177
  (57 shorter events, 3.0 us)
Async XLA Ops:
  6.5 68.4 %copy-start = (bf16[4,128,2048]{2,1,0:T(8,128)(2,1)S(1)}, bf16[4,128,2048]{2,1,0:T(8,128)(2,1)}, u32[]{:S(2)}) copy-start(bf16[4,128,2048]{2,1,0:T(8,128)(2,1)} %param.16) | copy-start | bytes 6291460
  6.5 12.4 %copy-start.1 = (s32[32]{0:T(128)S(1)}, s32[32]{0:T(128)}, u32[]{:S(2)}) copy-start(s32[32]{0:T(128)} %param.19) | copy-start | bytes 388
  6.5 12.5 %copy-start.2 = (s32[32,32]{1,0:T(8,128)S(1)}, s32[32,32]{1,0:T(8,128)}, u32[]{:S(2)}) copy-start(s32[32,32]{1,0:T(8,128)} %param.20) | copy-start | bytes 12292
  11.4 21.7 %all-to-all-start = ((bf16[8,12,2048]{2,1,0:T(8,128)(2,1)}), bf16[8,12,2048]{2,1,0:T(8,128)(2,1)S(1)}, u32[]{:S(2)}, u32[]{:S(2)}) async-start(bf16[8,12,2048]{2,1,0:T(8,128)(2,1)} %reshape_reshape.3), calls=%async_computation | async-start | bytes 1048576 | tf_op jit(solution)/shard_map/all_to_all | solution.py:80
  35.9 10.8 %all-to-all-start.1 = ((bf16[8,4,12,128]{3,1,2,0:T(4,128)(2,1)}), bf16[8,4,12,128]{3,1,2,0:T(4,128)(2,1)S(1)}, u32[]{:S(2)}, u32[]{:S(2)}) async-start(bf16[8,4,12,128]{3,1,2,0:T(4,128)(2,1)} %copy.49), calls=%async_computation.1 | async-start | bytes 196608 | tf_op jit(solution)/shard_map/all_to_all | solution.py:108
  74.9 5.3 %copy-start.3 = (f32[32,2]{0,1:T(2,128)S(1)}, f32[32,2]{0,1:T(2,128)}, u32[]{:S(2)}) copy-start(f32[32,2]{0,1:T(2,128)} %param.22) | copy-start | bytes 772
  76.4 30.8 %copy-start.4 = (s32[32]{0:T(128)S(1)}, s32[32]{0:T(128)}, u32[]{:S(2)}) copy-start(s32[32]{0:T(128)} %param.23) | copy-start | bytes 388
  76.4 27.5 %all-to-all-start.3 = ((f32[8,12,2048]{2,1,0:T(8,128)}), f32[8,12,2048]{2,1,0:T(8,128)S(1)}, u32[]{:S(2)}, u32[]{:S(2)}) async-start(f32[8,12,2048]{2,1,0:T(8,128)} %convolution_bitcast_fusion), calls=%async_computation.3 | async-start | bytes 2097152 | tf_op jit(solution)/shard_map/all_to_all | solution.py:171
  80.1 46.2 %reduce-scatter.2.cloned.1.call-start = ((), (), s32[]{:S(2)}) async-start(), calls=%async_computation.5 | async-start | bytes 327680 | tf_op jit(solution)/shard_map/reduce_scatter | solution.py:176
Sparse Core Ops, SparseCore 0:
  107.3 18.9 reduce-scatter.1

commit v2 on v1

--- a/solution.py
+++ b/solution.py
@@ -168,12 +168,20 @@
         .T
     )
     alive_rows = live_mask.astype(jnp.float32)[:, None]
-    returned = lax.all_to_all(partial_far, "req", split_axis=0, concat_axis=0, tiled=True)
-    summed = returned.reshape(experts, replicas, capacity, model_width).sum(axis=1)
-    own_sum = jnp.dot(
-        spread, summed.reshape(experts * capacity, model_width), precision=lax.Precision.HIGHEST
-    )
-    result = lax.psum_scatter(own_sum, "head", scatter_dimension=1, tiled=True)
+    head_count = lax.axis_size("head")
+    width_here = model_width // head_count
+    partial_far = partial_far.reshape(groups, capacity, head_count, width_here).transpose(0, 2, 1, 3)
+    returned = lax.all_to_all(
+        partial_far.reshape(groups * head_count, capacity, width_here),
+        ("req", "head"),
+        split_axis=0,
+        concat_axis=0,
+        tiled=True,
+    )
+    summed = returned.reshape(experts, replicas * head_count, capacity, width_here).sum(axis=1)
+    result = jnp.dot(
+        spread, summed.reshape(experts * capacity, width_here), precision=lax.Precision.HIGHEST
+    )
     return (result * alive_rows).astype(jnp.bfloat16)
 
 

time: 135 us -> 101 us (0.75)
  waiting for transfers between devices: 58.8 us -> 42.2 us
  between operations: 13.7 us -> 0.35 us
  matrix products: 23.6 us -> 21.1 us
    reduce_scatter x1 -> x0, waiting for transfers between devices: 19.1 us -> none  [body(): result = lax.psum_scatter(own_sum, 'head', scatter_dimension=1, tiled=True)]
    all_to_all x1, waiting for transfers between devices: 23.6 us -> 26 us  [body(): lax.all_to_all(partial_far.reshape(groups * head_count, capacity, width_h...]
    convert_element_type x1 -> x0, other arithmetic: 1.53 us -> none  [body(): return (result * alive_rows).astype(jnp.bfloat16)]
    dot_general x1, matrix products: 2.34 us -> 0.85 us  [body(): jnp.dot(spread, summed.reshape(experts * capacity, width_here), precision...]
  transfers between devices with their start and end apart: 4 -> 3, of which waited for: 4 -> 3; matrix products, arithmetic and copies ran while one was open for 4% -> 5% of each run, Pallas kernels for 0% -> 0%
where the time goes in v2:
time: 101 us; the launch traced here: 100 us
  waiting for transfers between devices  42.2 us (42%)
  matrix products  21.1 us (21%)
  starting transfers between devices  13.5 us (13%)
  blocking collectives  9.51 us (9%)
  local copies, waits for them, and re-layouts  8.05 us (8%)
  other arithmetic  5.24 us (5%)
    all_to_all x1, waiting for transfers between devices, body(): lax.all_to_all(partial_far.reshape(groups * head_count, capacity, width_h...  26 us
    all_to_all x1, blocking collectives, body(): lax.all_to_all(context_buf, 'req', split_axis=0, concat_axis=0, tiled=True)  9.51 us
    all_to_all x1, waiting for transfers between devices, body(): lax.all_to_all(sendbuf, 'req', split_axis=0, concat_axis=0, tiled=True)  9.18 us
    dot_general x1, matrix products, body(): jnp.einsum('pkhd,pthd->pkht', page_queries, cache_keys, preferred_element...  7.94 us
    all_to_all x1, starting transfers between devices, body(): lax.all_to_all(sendbuf, 'req', split_axis=0, concat_axis=0, tiled=True)  7.26 us
    all_to_all x1, waiting for transfers between devices, body(): lax.all_to_all(queries_far, 'req', split_axis=0, concat_axis=0, tiled=True)  7.03 us
    dot_general x1, matrix products, body(): jnp.einsum('pkht,pthd->pkhd', weights_rounded, cache_values, preferred_el...  5.72 us
    all_to_all x1, starting transfers between devices, body(): lax.all_to_all(queries_far, 'req', split_axis=0, concat_axis=0, tiled=True)  3.64 us
  transfers between devices with their start and end apart: 3, of which 3 were waited for; matrix products, arithmetic and copies ran while one was open for 5% of the time, Pallas kernels for 0%

profile of v2, /device:TPU:0, one launch (start us, length us, event | category | flops | bytes accessed | tf_op | source)
XLA Modules:
  0.0 100.0 jit_solution(14073468737367492475)
XLA Ops:
  0.0 0.9 copy.46
  1.2 0.2 select_reduce_fusion.3
  1.4 1.0 %fusion.34 = f32[32]{0:T(128)S(1)} fusion(bf16[32,2048]{1,0:T(8,128)(2,1)} %param.12), kind=kLoop, calls=%fused_computation.37 | loop fusion | flops 196576 | bytes 131200 | tf_op jit(solution)/shard_map/reduce_sum | solution.py:58
  2.4 1.0 %fusion.36 = bf16[32,2048]{1,0:T(8,128)(2,1)S(1)} fusion(bf16[32,2048]{1,0:T(8,128)(2,1)} %param.12, f32[2048]{0:T(1024)} %param.13, f32[32]{0:T(128)S(1)} %add_rsqrt_fusion), kind=kLoop, calls=%fused_computation.39 | loop fusion | flops 262144 | bytes 270464 | tf_op jit(solution)/shard_map/convert_element_type | solution.py:60
  3.7 0.2 convolution_convert_fusion
  4.0 0.9 reshape_reshape.3
  4.9 7.3 %all-to-all-start = ((bf16[8,12,2048]{2,1,0:T(8,128)(2,1)}), bf16[8,12,2048]{2,1,0:T(8,128)(2,1)S(1)}, u32[]{:S(2)}, u32[]{:S(2)}) async-start(bf16[8,12,2048]{2,1,0:T(8,128)(2,1)} %reshape_reshape.3), calls=%async_computation | async-start | bytes 1048576 | tf_op jit(solution)/shard_map/all_to_all | solution.py:80
  12.5 0.4 fusion.32
  12.9 0.8 gather_fusion
  13.7 3.0 %fusion.4 = f32[32,4,2,128]{3,0,2,1:T(8,128)S(1)} fusion(bf16[2048,4,2,128]{3,2,1,0:T(2,128)(2,1)} %param.14, bf16[32,2048]{1,0:T(8,128)(2,1)S(1)} %fusion.36), kind=kOutput, calls=%fused_computation.8 | convolution fusion | flops 134217728 | bytes 4456448 | tf_op jit(solution)/shard_map/rf,fhkd->rhkd/dot_general | solution.py:84
  17.1 0.4 select_reduce_fusion
  17.4 9.2 %all-to-all-done = bf16[8,12,2048]{2,1,0:T(8,128)(2,1)S(1)} async-done(((bf16[8,12,2048]{2,1,0:T(8,128)(2,1)}), bf16[8,12,2048]{2,1,0:T(8,128)(2,1)S(1)}, u32[]{:S(2)}, u32[]{:S(2)}) %all-to-all-start) | async-done | bytes 393248 | tf_op jit(solution)/shard_map/all_to_all | solution.py:80
  26.6 2.0 %fusion.18 = bf16[8,4,12,128]{3,2,1,0:T(8,128)(2,1)S(1)} fusion(bf16[4,2048,128]{2,1,0:T(8,128)(2,1)} %param.15, bf16[8,12,2048]{2,1,0:T(8,128)(2,1)S(1)} %all-to-all-done), kind=kOutput, calls=%fused_computation.19 | convolution fusion | flops 201375744 | bytes 2588672 | tf_op jit(solution)/shard_map/snd,pdh->spnh/dot_general | solution.py:78
  28.7 0.7 copy.49
  29.3 3.6 %all-to-all-start.1 = ((bf16[8,4,12,128]{3,1,2,0:T(4,128)(2,1)}), bf16[8,4,12,128]{3,1,2,0:T(4,128)(2,1)S(1)}, u32[]{:S(2)}, u32[]{:S(2)}) async-start(bf16[8,4,12,128]{3,1,2,0:T(4,128)(2,1)} %copy.49), calls=%async_computation.1 | async-start | bytes 196608 | tf_op jit(solution)/shard_map/all_to_all | solution.py:108
  33.1 7.0 %all-to-all-done.1 = bf16[8,4,12,128]{3,1,2,0:T(4,128)(2,1)S(1)} async-done(((bf16[8,4,12,128]{3,1,2,0:T(4,128)(2,1)}), bf16[8,4,12,128]{3,1,2,0:T(4,128)(2,1)S(1)}, u32[]{:S(2)}, u32[]{:S(2)}) %all-to-all-start.1) | async-done | bytes 98336 | tf_op jit(solution)/shard_map/all_to_all | solution.py:108
  40.1 0.7 gather_fusion.1
  40.8 0.2 subtract_convert_fusion
  41.1 0.7 gather_fusion.2
  41.8 7.9 %fusion.64 = (f32[64,2,4]{1,2,0:T(4,128)S(1)}, f32[64,2,4,128]{3,1,2,0:T(2,128)S(1)}) fusion(bf16[64,128,4,128]{3,2,1,0:T(4,128)(2,1)} %param.17, bf16[64,2,4,128]{3,2,1,0:T(4,128)(2,1)S(1)} %gather_fusion.2, pred[64,128]{1,0:T(8,128)(4,1)S(1)} %fusion.53), kind=kOutput, calls=%fused_computation.100 | convolution fusion | flops 16973312 | bytes 8792064 | tf_op jit(solution)/shard_map/pkhd,pthd->pkht/dot_general | solution.py:121
  50.0 0.3 fusion.47
  50.5 0.7 gather_fusion.3
  51.1 0.5 copy.55
  51.6 0.7 fusion.38
  52.4 5.7 %fusion.9 = f32[64,2,4,128]{3,1,2,0:T(2,128)S(1)} fusion(bf16[64,128,4,128]{3,2,1,0:T(4,128)(2,1)} %param.18, f32[64,2,4,128]{3,1,2,0:T(2,128)S(1)} %get-tuple-element.22, f32[64,2,4]{1,2,0:T(4,128)S(1)} %copy.55), kind=kOutput, calls=%fused_computation.15 | convolution fusion | flops 16908288 | bytes 8914944 | tf_op jit(solution)/shard_map/pkht,pthd->pkhd/dot_general | solution.py:143
  58.4 0.3 fusion.22
  58.9 9.5 %all_to_all.20 = bf16[8,4,12,128]{3,1,2,0:T(4,128)(2,1)S(1)} all-to-all(bf16[8,4,12,128]{3,1,2,0:T(4,128)(2,1)S(1)} %bitcast.100), channel_id=1, replica_groups=mesh['req'=8,'head'=4] {'req'}, dimensions={0} | all-to-all | bytes 196608 | tf_op jit(solution)/shard_map/all_to_all | solution.py:159
  68.4 0.4 convolution_bitcast_fusion
  69.1 1.1 %reshape.325 = f32[32,12,512]{2,1,0:T(8,128)} reshape(f32[8,48,512]{2,1,0:T(8,128)S(1)} %pad_maximum_fusion) | data formatting | bytes 1572864 | tf_op jit(solution)/shard_map/reshape | solution.py:175
  70.2 2.6 %all-to-all-start.3 = ((f32[32,12,512]{2,1,0:T(8,128)}), f32[32,12,512]{2,1,0:T(8,128)S(1)}, u32[]{:S(2)}, u32[]{:S(2)}) async-start(f32[32,12,512]{2,1,0:T(8,128)} %reshape.325), calls=%async_computation.3 | async-start | bytes 2097152 | tf_op jit(solution)/shard_map/all_to_all | solution.py:174
  73.0 26.0 %all-to-all-done.3 = f32[32,12,512]{2,1,0:T(8,128)S(1)} async-done(((f32[32,12,512]{2,1,0:T(8,128)}), f32[32,12,512]{2,1,0:T(8,128)S(1)}, u32[]{:S(2)}, u32[]{:S(2)}) %all-to-all-start.3) | async-done | bytes 786464 | tf_op jit(solution)/shard_map/all_to_all | solution.py:174
  99.2 0.8 fusion.23
  (57 shorter events, 2.9 us)
Async XLA Ops:
  0.0 68.4 %copy-start = (bf16[4,128,2048]{2,1,0:T(8,128)(2,1)S(1)}, bf16[4,128,2048]{2,1,0:T(8,128)(2,1)}, u32[]{:S(2)}) copy-start(bf16[4,128,2048]{2,1,0:T(8,128)(2,1)} %param.16) | copy-start | bytes 6291460
  0.0 12.4 %copy-start.1 = (s32[32]{0:T(128)S(1)}, s32[32]{0:T(128)}, u32[]{:S(2)}) copy-start(s32[32]{0:T(128)} %param.19) | copy-start | bytes 388
  0.0 12.5 %copy-start.2 = (s32[32,32]{1,0:T(8,128)S(1)}, s32[32,32]{1,0:T(8,128)}, u32[]{:S(2)}) copy-start(s32[32,32]{1,0:T(8,128)} %param.20) | copy-start | bytes 12292
  4.9 21.7 %all-to-all-start = ((bf16[8,12,2048]{2,1,0:T(8,128)(2,1)}), bf16[8,12,2048]{2,1,0:T(8,128)(2,1)S(1)}, u32[]{:S(2)}, u32[]{:S(2)}) async-start(bf16[8,12,2048]{2,1,0:T(8,128)(2,1)} %reshape_reshape.3), calls=%async_computation | async-start | bytes 1048576 | tf_op jit(solution)/shard_map/all_to_all | solution.py:80
  29.3 10.8 %all-to-all-start.1 = ((bf16[8,4,12,128]{3,1,2,0:T(4,128)(2,1)}), bf16[8,4,12,128]{3,1,2,0:T(4,128)(2,1)S(1)}, u32[]{:S(2)}, u32[]{:S(2)}) async-start(bf16[8,4,12,128]{3,1,2,0:T(4,128)(2,1)} %copy.49), calls=%async_computation.1 | async-start | bytes 196608 | tf_op jit(solution)/shard_map/all_to_all | solution.py:108
  68.9 4.1 %copy-start.4 = (s32[32]{0:T(128)S(1)}, s32[32]{0:T(128)}, u32[]{:S(2)}) copy-start(s32[32]{0:T(128)} %param.23) | copy-start | bytes 388
  68.9 4.0 %copy-start.3 = (f32[32,2]{0,1:T(2,128)S(1)}, f32[32,2]{0,1:T(2,128)}, u32[]{:S(2)}) copy-start(f32[32,2]{0,1:T(2,128)} %param.22) | copy-start | bytes 772
  70.2 28.9 %all-to-all-start.3 = ((f32[32,12,512]{2,1,0:T(8,128)}), f32[32,12,512]{2,1,0:T(8,128)S(1)}, u32[]{:S(2)}, u32[]{:S(2)}) async-start(f32[32,12,512]{2,1,0:T(8,128)} %reshape.325), calls=%async_computation.3 | async-start | bytes 2097152 | tf_op jit(solution)/shard_map/all_to_all | solution.py:174

commit v3 on v2

--- a/solution.py
+++ b/solution.py
@@ -172,13 +172,17 @@
     width_here = model_width // head_count
     partial_far = partial_far.reshape(groups, capacity, head_count, width_here).transpose(0, 2, 1, 3)
     returned = lax.all_to_all(
-        partial_far.reshape(groups * head_count, capacity, width_here),
+        partial_far.reshape(groups * head_count, capacity, width_here).astype(jnp.bfloat16),
         ("req", "head"),
         split_axis=0,
         concat_axis=0,
         tiled=True,
     )
-    summed = returned.reshape(experts, replicas * head_count, capacity, width_here).sum(axis=1)
+    summed = (
+        returned.astype(jnp.float32)
+        .reshape(experts, replicas * head_count, capacity, width_here)
+        .sum(axis=1)
+    )
     result = jnp.dot(
         spread, summed.reshape(experts * capacity, width_here), precision=lax.Precision.HIGHEST
     )

time: 101 us -> 89.7 us (0.89)
  waiting for transfers between devices: 42.2 us -> 31.6 us
    all_to_all x1, waiting for transfers between devices: 26 us -> 15.4 us  [body(): lax.all_to_all(partial_far.reshape(groups * head_count, capacity, width_h...]
    reshape x1 -> x0, local copies, waits for them, and re-layouts: 1.08 us -> none  [body(): partial_far.reshape(groups * head_count, capacity, width_here)]
  transfers between devices with their start and end apart: 3 -> 3, of which waited for: 3 -> 3; matrix products, arithmetic and copies ran while one was open for 5% -> 6% of each run, Pallas kernels for 0% -> 0%
where the time goes in v3:
time: 89.7 us; the launch traced here: 89.1 us
  waiting for transfers between devices  31.6 us (35%)
  matrix products  21.1 us (24%)
  starting transfers between devices  13.5 us (15%)
  blocking collectives  9.51 us (11%)
  local copies, waits for them, and re-layouts  7.8 us (9%)
  other arithmetic  5.24 us (6%)
    all_to_all x1, waiting for transfers between devices, body(): lax.all_to_all(partial_far.reshape(groups * head_count, capacity, width_h...  15.4 us
    all_to_all x1, blocking collectives, body(): lax.all_to_all(context_buf, 'req', split_axis=0, concat_axis=0, tiled=True)  9.51 us
    all_to_all x1, waiting for transfers between devices, body(): lax.all_to_all(sendbuf, 'req', split_axis=0, concat_axis=0, tiled=True)  9.19 us
    dot_general x1, matrix products, body(): jnp.einsum('pkhd,pthd->pkht', page_queries, cache_keys, preferred_element...  7.94 us
    all_to_all x1, starting transfers between devices, body(): lax.all_to_all(sendbuf, 'req', split_axis=0, concat_axis=0, tiled=True)  7.26 us
    all_to_all x1, waiting for transfers between devices, body(): lax.all_to_all(queries_far, 'req', split_axis=0, concat_axis=0, tiled=True)  7.03 us
    dot_general x1, matrix products, body(): jnp.einsum('pkht,pthd->pkhd', weights_rounded, cache_values, preferred_el...  5.71 us
    all_to_all x1, starting transfers between devices, body(): lax.all_to_all(queries_far, 'req', split_axis=0, concat_axis=0, tiled=True)  3.63 us
  transfers between devices with their start and end apart: 3, of which 3 were waited for; matrix products, arithmetic and copies ran while one was open for 6% of the time, Pallas kernels for 0%

profile of v3, /device:TPU:0, one launch (start us, length us, event | category | flops | bytes accessed | tf_op | source)
XLA Modules:
  0.0 89.1 jit_solution(18365262448472383297)
XLA Ops:
  0.0 0.9 %copy.46 = s32[32,2]{1,0:T(8,128)S(1)} copy(s32[32,2]{0,1:T(2,128)} %param.21) | data formatting | bytes 512 | tf_op args[9]
  1.2 0.2 select_reduce_fusion.3
  1.4 1.0 %fusion.35 = f32[32]{0:T(128)S(1)} fusion(bf16[32,2048]{1,0:T(8,128)(2,1)} %param.12), kind=kLoop, calls=%fused_computation.38 | loop fusion | flops 196576 | bytes 131200 | tf_op jit(solution)/shard_map/reduce_sum | solution.py:58
  2.4 1.0 %fusion.37 = bf16[32,2048]{1,0:T(8,128)(2,1)S(1)} fusion(bf16[32,2048]{1,0:T(8,128)(2,1)} %param.12, f32[2048]{0:T(1024)} %param.13, f32[32]{0:T(128)S(1)} %add_rsqrt_fusion), kind=kLoop, calls=%fused_computation.40 | loop fusion | flops 262144 | bytes 270464 | tf_op jit(solution)/shard_map/convert_element_type | solution.py:60
  3.7 0.2 convolution_convert_fusion
  4.0 0.9 reshape_reshape.3
  4.9 7.3 %all-to-all-start = ((bf16[8,12,2048]{2,1,0:T(8,128)(2,1)}), bf16[8,12,2048]{2,1,0:T(8,128)(2,1)S(1)}, u32[]{:S(2)}, u32[]{:S(2)}) async-start(bf16[8,12,2048]{2,1,0:T(8,128)(2,1)} %reshape_reshape.3), calls=%async_computation | async-start | bytes 1048576 | tf_op jit(solution)/shard_map/all_to_all | solution.py:80
  12.5 0.4 fusion.33
  12.9 0.8 gather_fusion
  13.7 3.0 %fusion.4 = f32[32,4,2,128]{3,0,2,1:T(8,128)S(1)} fusion(bf16[2048,4,2,128]{3,2,1,0:T(2,128)(2,1)} %param.14, bf16[32,2048]{1,0:T(8,128)(2,1)S(1)} %fusion.37), kind=kOutput, calls=%fused_computation.8 | convolution fusion | flops 134217728 | bytes 4456448 | tf_op jit(solution)/shard_map/rf,fhkd->rhkd/dot_general | solution.py:84
  17.0 0.4 select_reduce_fusion
  17.4 9.2 %all-to-all-done = bf16[8,12,2048]{2,1,0:T(8,128)(2,1)S(1)} async-done(((bf16[8,12,2048]{2,1,0:T(8,128)(2,1)}), bf16[8,12,2048]{2,1,0:T(8,128)(2,1)S(1)}, u32[]{:S(2)}, u32[]{:S(2)}) %all-to-all-start) | async-done | bytes 393248 | tf_op jit(solution)/shard_map/all_to_all | solution.py:80
  26.6 2.1 %fusion.19 = bf16[8,4,12,128]{3,2,1,0:T(8,128)(2,1)S(1)} fusion(bf16[4,2048,128]{2,1,0:T(8,128)(2,1)} %param.15, bf16[8,12,2048]{2,1,0:T(8,128)(2,1)S(1)} %all-to-all-done), kind=kOutput, calls=%fused_computation.20 | convolution fusion | flops 201375744 | bytes 2588672 | tf_op jit(solution)/shard_map/snd,pdh->spnh/dot_general | solution.py:78
  28.7 0.7 copy.49
  29.3 3.6 %all-to-all-start.1 = ((bf16[8,4,12,128]{3,1,2,0:T(4,128)(2,1)}), bf16[8,4,12,128]{3,1,2,0:T(4,128)(2,1)S(1)}, u32[]{:S(2)}, u32[]{:S(2)}) async-start(bf16[8,4,12,128]{3,1,2,0:T(4,128)(2,1)} %copy.49), calls=%async_computation.1 | async-start | bytes 196608 | tf_op jit(solution)/shard_map/all_to_all | solution.py:108
  33.1 7.0 %all-to-all-done.1 = bf16[8,4,12,128]{3,1,2,0:T(4,128)(2,1)S(1)} async-done(((bf16[8,4,12,128]{3,1,2,0:T(4,128)(2,1)}), bf16[8,4,12,128]{3,1,2,0:T(4,128)(2,1)S(1)}, u32[]{:S(2)}, u32[]{:S(2)}) %all-to-all-start.1) | async-done | bytes 98336 | tf_op jit(solution)/shard_map/all_to_all | solution.py:108
  40.1 0.7 gather_fusion.1
  40.8 0.2 subtract_convert_fusion
  41.1 0.7 gather_fusion.2
  41.8 7.9 %fusion.65 = (f32[64,2,4]{1,2,0:T(4,128)S(1)}, f32[64,2,4,128]{3,1,2,0:T(2,128)S(1)}) fusion(bf16[64,128,4,128]{3,2,1,0:T(4,128)(2,1)} %param.17, bf16[64,2,4,128]{3,2,1,0:T(4,128)(2,1)S(1)} %gather_fusion.2, pred[64,128]{1,0:T(8,128)(4,1)S(1)} %fusion.54), kind=kOutput, calls=%fused_computation.101 | convolution fusion | flops 16973312 | bytes 8792064 | tf_op jit(solution)/shard_map/pkhd,pthd->pkht/dot_general | solution.py:121
  49.9 0.3 fusion.48
  50.4 0.7 gather_fusion.3
  51.1 0.5 copy.55
  51.6 0.8 fusion.39
  52.7 5.7 %fusion.10 = f32[64,2,4,128]{3,1,2,0:T(2,128)S(1)} fusion(bf16[64,128,4,128]{3,2,1,0:T(4,128)(2,1)} %param.18, f32[64,2,4,128]{3,1,2,0:T(2,128)S(1)} %get-tuple-element.22, f32[64,2,4]{1,2,0:T(4,128)S(1)} %copy.55), kind=kOutput, calls=%fused_computation.16 | convolution fusion | flops 16908288 | bytes 8914944 | tf_op jit(solution)/shard_map/pkht,pthd->pkhd/dot_general | solution.py:143
  58.4 0.3 fusion.23
  58.9 9.5 %all_to_all.20 = bf16[8,4,12,128]{3,1,2,0:T(4,128)(2,1)S(1)} all-to-all(bf16[8,4,12,128]{3,1,2,0:T(4,128)(2,1)S(1)} %bitcast.103), channel_id=1, replica_groups=mesh['req'=8,'head'=4] {'req'}, dimensions={0} | all-to-all | bytes 196608 | tf_op jit(solution)/shard_map/all_to_all | solution.py:159
  68.4 0.5 fusion.6
  69.1 0.9 convert_element_type.97
  69.9 2.6 %all-to-all-start.3 = ((bf16[32,12,512]{2,1,0:T(8,128)(2,1)}), bf16[32,12,512]{2,1,0:T(8,128)(2,1)S(1)}, u32[]{:S(2)}, u32[]{:S(2)}) async-start(bf16[32,12,512]{2,1,0:T(8,128)(2,1)} %convert_element_type.97), calls=%async_computation.3 | async-start | bytes 1048576 | tf_op jit(solution)/shard_map/all_to_all | solution.py:174
  72.7 15.4 %all-to-all-done.3 = bf16[32,12,512]{2,1,0:T(8,128)(2,1)S(1)} async-done(((bf16[32,12,512]{2,1,0:T(8,128)(2,1)}), bf16[32,12,512]{2,1,0:T(8,128)(2,1)S(1)}, u32[]{:S(2)}, u32[]{:S(2)}) %all-to-all-start.3) | async-done | bytes 393248 | tf_op jit(solution)/shard_map/all_to_all | solution.py:174
  88.2 0.8 fusion.24
  (57 shorter events, 2.8 us)
Async XLA Ops:
  0.0 68.4 %copy-start = (bf16[4,128,2048]{2,1,0:T(8,128)(2,1)S(1)}, bf16[4,128,2048]{2,1,0:T(8,128)(2,1)}, u32[]{:S(2)}) copy-start(bf16[4,128,2048]{2,1,0:T(8,128)(2,1)} %param.16) | copy-start | bytes 6291460
  0.0 12.4 %copy-start.1 = (s32[32]{0:T(128)S(1)}, s32[32]{0:T(128)}, u32[]{:S(2)}) copy-start(s32[32]{0:T(128)} %param.19) | copy-start | bytes 388
  0.0 12.5 %copy-start.2 = (s32[32,32]{1,0:T(8,128)S(1)}, s32[32,32]{1,0:T(8,128)}, u32[]{:S(2)}) copy-start(s32[32,32]{1,0:T(8,128)} %param.20) | copy-start | bytes 12292
  4.9 21.7 %all-to-all-start = ((bf16[8,12,2048]{2,1,0:T(8,128)(2,1)}), bf16[8,12,2048]{2,1,0:T(8,128)(2,1)S(1)}, u32[]{:S(2)}, u32[]{:S(2)}) async-start(bf16[8,12,2048]{2,1,0:T(8,128)(2,1)} %reshape_reshape.3), calls=%async_computation | async-start | bytes 1048576 | tf_op jit(solution)/shard_map/all_to_all | solution.py:80
  29.3 10.8 %all-to-all-start.1 = ((bf16[8,4,12,128]{3,1,2,0:T(4,128)(2,1)}), bf16[8,4,12,128]{3,1,2,0:T(4,128)(2,1)S(1)}, u32[]{:S(2)}, u32[]{:S(2)}) async-start(bf16[8,4,12,128]{3,1,2,0:T(4,128)(2,1)} %copy.49), calls=%async_computation.1 | async-start | bytes 196608 | tf_op jit(solution)/shard_map/all_to_all | solution.py:108
  68.4 4.2 %copy-start.4 = (s32[32]{0:T(128)S(1)}, s32[32]{0:T(128)}, u32[]{:S(2)}) copy-start(s32[32]{0:T(128)} %param.23) | copy-start | bytes 388
  68.4 4.2 %copy-start.3 = (f32[32,2]{0,1:T(2,128)S(1)}, f32[32,2]{0,1:T(2,128)}, u32[]{:S(2)}) copy-start(f32[32,2]{0,1:T(2,128)} %param.22) | copy-start | bytes 772
  69.9 18.2 %all-to-all-start.3 = ((bf16[32,12,512]{2,1,0:T(8,128)(2,1)}), bf16[32,12,512]{2,1,0:T(8,128)(2,1)S(1)}, u32[]{:S(2)}, u32[]{:S(2)}) async-start(bf16[32,12,512]{2,1,0:T(8,128)(2,1)} %convert_element_type.97), calls=%async_computation.3 | async-start | bytes 1048576 | tf_op jit(solution)/shard_map/all_to_all | solution.py:174

commit v4 on v2

--- a/solution.py
+++ b/solution.py
@@ -5,6 +5,7 @@
 
 AEXP = 8
 CAP = 12
+CHUNKS = 2
 
 
 eps = 1e-06
@@ -75,12 +76,7 @@
         (experts, replicas, capacity, model_width),
     )
     sendbuf = sendbuf.reshape(groups, capacity, model_width)
-    queries_far = jnp.einsum(
-        "snd,pdh->spnh",
-        lax.all_to_all(sendbuf, "req", split_axis=0, concat_axis=0, tiled=True),
-        query_weight,
-        preferred_element_type=jnp.float32,
-    ).astype(jnp.bfloat16)
+    tokens_far = lax.all_to_all(sendbuf, "req", split_axis=0, concat_axis=0, tiled=True)
     key_value = jnp.einsum(
         "rf,fhkd->rhkd", normed, key_value_weight, preferred_element_type=jnp.float32
     )
@@ -105,61 +101,98 @@
     in_range = page_taken[:, None] & (
         page_start[:, None] + jnp.arange(page_len)[None, :] < page_limit[:, None]
     )
-    queries = lax.all_to_all(queries_far, "req", split_axis=0, concat_axis=0, tiled=True)
-    queries = (
-        queries.reshape(experts, heads_here, capacity, head_dim)
-        .transpose(0, 2, 1, 3)
-        .reshape(experts * capacity, heads_here, head_dim)
-    )
-    raw_query = queries[target].reshape(row_count, choices_each, heads_here, head_dim)
-    query_rot = rotate(raw_query.astype(jnp.float32), cache_length[:, None, None]).astype(
-        jnp.bfloat16
-    )
     score_scale = 1.0 / head_dim**0.5
-    page_queries = query_rot[page_owner]
-    scores = (
-        jnp.einsum("pkhd,pthd->pkht", page_queries, cache_keys, preferred_element_type=jnp.float32)
-        * score_scale
-    )
-    scores = jnp.where(in_range[:, None, None, :], scores, -jnp.inf)
-    fresh_score = (
-        jnp.einsum("rkhd,rhd->rkh", query_rot, key_new, preferred_element_type=jnp.float32)
-        * score_scale
-    )
-    page_top = jnp.max(scores, axis=3)
-    owned_top = jnp.max(jnp.where(owned_pages[:, :, None, None], page_top[None], -jnp.inf), axis=1)
-    row_top = jnp.maximum(owned_top, fresh_score)
-    weights = jnp.exp(scores - row_top[page_owner][..., None])
-    fresh_weight = jnp.exp(fresh_score - row_top)
     owned_float = owned_pages.astype(jnp.float32)
-    denominator = (
-        jnp.einsum(
-            "rp,pkh->rkh", owned_float, jnp.sum(weights, axis=3), precision=lax.Precision.HIGHEST
-        )
-        + fresh_weight
-    )
-    weights_rounded = weights.astype(jnp.bfloat16)
-    fresh_rounded = lax.optimization_barrier(fresh_weight.astype(jnp.bfloat16)).astype(jnp.float32)
-    page_context = jnp.einsum(
-        "pkht,pthd->pkhd", weights_rounded, cache_values, preferred_element_type=jnp.float32
-    )
-    accumulated = jnp.einsum(
-        "rp,pkhd->rkhd", owned_float, page_context, precision=lax.Precision.HIGHEST
-    )
-    accumulated = accumulated + fresh_rounded[..., None] * value_new.astype(jnp.float32)[:, None]
-    context = (accumulated / denominator[..., None]).astype(jnp.bfloat16)
-    context_flat = context.reshape(row_count * choices_each, heads_here * head_dim)
-    context_buf = jnp.dot(select_rows, context_flat, preferred_element_type=jnp.float32).astype(
-        jnp.bfloat16
-    )
-    context_buf = context_buf.reshape(experts, capacity, heads_here, head_dim).transpose(0, 2, 1, 3)
-    context_buf = context_buf.reshape(groups, pairs_here, capacity, head_dim)
-    partial_far = jnp.einsum(
-        "spnh,phd->snd",
-        lax.all_to_all(context_buf, "req", split_axis=0, concat_axis=0, tiled=True),
-        output_weight,
-        preferred_element_type=jnp.float32,
-    )
+    chunks = CHUNKS if pairs_here % CHUNKS == 0 else 1
+    pairs_chunk = pairs_here // chunks
+    partial_far = None
+    for chunk in range(chunks):
+        first = chunk * pairs_chunk
+        head_ids = [r * pairs_here + first + i for r in range(replicas) for i in range(pairs_chunk)]
+        chunk_heads = len(head_ids)
+
+        def pick(array, axis):
+            if head_ids == list(range(head_ids[0], head_ids[0] + chunk_heads)):
+                return lax.slice_in_dim(array, head_ids[0], head_ids[0] + chunk_heads, axis=axis)
+            return jnp.take(array, jnp.asarray(head_ids), axis=axis)
+
+        queries_far = jnp.einsum(
+            "snd,pdh->spnh",
+            tokens_far,
+            query_weight[first : first + pairs_chunk],
+            preferred_element_type=jnp.float32,
+        ).astype(jnp.bfloat16)
+        queries = lax.all_to_all(queries_far, "req", split_axis=0, concat_axis=0, tiled=True)
+        queries = (
+            queries.reshape(experts, chunk_heads, capacity, head_dim)
+            .transpose(0, 2, 1, 3)
+            .reshape(experts * capacity, chunk_heads, head_dim)
+        )
+        raw_query = queries[target].reshape(row_count, choices_each, chunk_heads, head_dim)
+        query_rot = rotate(raw_query.astype(jnp.float32), cache_length[:, None, None]).astype(
+            jnp.bfloat16
+        )
+        keys_here = pick(cache_keys, 2)
+        values_here = pick(cache_values, 2)
+        key_chunk = pick(key_new, 1)
+        value_chunk = pick(value_new, 1)
+        page_queries = query_rot[page_owner]
+        scores = (
+            jnp.einsum(
+                "pkhd,pthd->pkht", page_queries, keys_here, preferred_element_type=jnp.float32
+            )
+            * score_scale
+        )
+        scores = jnp.where(in_range[:, None, None, :], scores, -jnp.inf)
+        fresh_score = (
+            jnp.einsum("rkhd,rhd->rkh", query_rot, key_chunk, preferred_element_type=jnp.float32)
+            * score_scale
+        )
+        page_top = jnp.max(scores, axis=3)
+        owned_top = jnp.max(
+            jnp.where(owned_pages[:, :, None, None], page_top[None], -jnp.inf), axis=1
+        )
+        row_top = jnp.maximum(owned_top, fresh_score)
+        weights = jnp.exp(scores - row_top[page_owner][..., None])
+        fresh_weight = jnp.exp(fresh_score - row_top)
+        denominator = (
+            jnp.einsum(
+                "rp,pkh->rkh",
+                owned_float,
+                jnp.sum(weights, axis=3),
+                precision=lax.Precision.HIGHEST,
+            )
+            + fresh_weight
+        )
+        weights_rounded = weights.astype(jnp.bfloat16)
+        fresh_rounded = lax.optimization_barrier(fresh_weight.astype(jnp.bfloat16)).astype(
+            jnp.float32
+        )
+        page_context = jnp.einsum(
+            "pkht,pthd->pkhd", weights_rounded, values_here, preferred_element_type=jnp.float32
+        )
+        accumulated = jnp.einsum(
+            "rp,pkhd->rkhd", owned_float, page_context, precision=lax.Precision.HIGHEST
+        )
+        accumulated = (
+            accumulated + fresh_rounded[..., None] * value_chunk.astype(jnp.float32)[:, None]
+        )
+        context = (accumulated / denominator[..., None]).astype(jnp.bfloat16)
+        context_flat = context.reshape(row_count * choices_each, chunk_heads * head_dim)
+        context_buf = jnp.dot(
+            select_rows, context_flat, preferred_element_type=jnp.float32
+        ).astype(jnp.bfloat16)
+        context_buf = context_buf.reshape(
+            experts, capacity, replicas, pairs_chunk, head_dim
+        ).transpose(0, 2, 3, 1, 4)
+        context_buf = context_buf.reshape(groups, pairs_chunk, capacity, head_dim)
+        chunk_partial = jnp.einsum(
+            "spnh,phd->snd",
+            lax.all_to_all(context_buf, "req", split_axis=0, concat_axis=0, tiled=True),
+            output_weight[first : first + pairs_chunk],
+            preferred_element_type=jnp.float32,
+        )
+        partial_far = chunk_partial if partial_far is None else partial_far + chunk_partial
     gate_flat = expert_gate.reshape(-1)
     spread = (
         jnp.where(select, gate_flat[None, :], jnp.float32(0.0))

time: 101 us -> 140 us (1.39)
  local copies, waits for them, and re-layouts: 8.05 us -> 34.5 us
  starting transfers between devices: 13.5 us -> 26.1 us
  blocking collectives: 9.51 us -> 0 us
  waiting for transfers between devices: 42.2 us -> 50.1 us
  other arithmetic: 5.24 us -> 7.54 us
    slice x1 -> x3, local copies, waits for them, and re-layouts: 0.09 us -> 21.8 us  [the longest x2 21.7 us: pick(): lax.slice_in_dim(array, head_ids[0], head_ids[0] + chunk_heads, axis=axis)]
    all_to_all x0 -> x2, waiting for transfers between devices: none -> 12.4 us  [body(): lax.all_to_all(context_buf, 'req', split_axis=0, concat_axis=0, tiled=True)]
    all_to_all x1 -> x0, blocking collectives: 9.51 us -> none  [body(): lax.all_to_all(context_buf, 'req', split_axis=0, concat_axis=0, tiled=True)]
    all_to_all x1, waiting for transfers between devices: 9.18 us -> 0.01 us  [body(): lax.all_to_all(sendbuf, 'req', split_axis=0, concat_axis=0, tiled=True)]
    all_to_all x0 -> x2, starting transfers between devices: none -> 6.69 us  [body(): lax.all_to_all(context_buf, 'req', split_axis=0, concat_axis=0, tiled=True)]
    all_to_all x1 -> x2, starting transfers between devices: 3.64 us -> 9.51 us  [body(): lax.all_to_all(queries_far, 'req', split_axis=0, concat_axis=0, tiled=True)]
    all_to_all x1 -> x2, waiting for transfers between devices: 7.03 us -> 11.7 us  [body(): lax.all_to_all(queries_far, 'req', split_axis=0, concat_axis=0, tiled=True)]
    dot_general x4 -> x8, matrix products: 16 us -> 15 us  [the longest x2 9.18 us: body(): jnp.einsum('pkhd,pthd->pkht', page_queries, keys_here, preferred_element_...]
  transfers between devices with their start and end apart: 3 -> 6, of which waited for: 3 -> 5; matrix products, arithmetic and copies ran while one was open for 5% -> 23% of each run, Pallas kernels for 0% -> 0%
where the time goes in v4:
time: 140 us; the launch traced here: 139 us
  waiting for transfers between devices  50.1 us (36%)
  local copies, waits for them, and re-layouts  34.5 us (25%)
  starting transfers between devices  26.1 us (19%)
  matrix products  20.7 us (15%)
  other arithmetic  7.54 us (5%)
    all_to_all x1, waiting for transfers between devices, body(): lax.all_to_all(partial_far.reshape(groups * head_count, capacity, width_h...  26 us
    slice x2, local copies, waits for them, and re-layouts, pick(): lax.slice_in_dim(array, head_ids[0], head_ids[0] + chunk_heads, axis=axis)  21.7 us
    all_to_all x2, waiting for transfers between devices, body(): lax.all_to_all(context_buf, 'req', split_axis=0, concat_axis=0, tiled=True)  12.4 us
    all_to_all x2, waiting for transfers between devices, body(): lax.all_to_all(queries_far, 'req', split_axis=0, concat_axis=0, tiled=True)  11.7 us
    all_to_all x2, starting transfers between devices, body(): lax.all_to_all(queries_far, 'req', split_axis=0, concat_axis=0, tiled=True)  9.51 us
    dot_general x2, matrix products, body(): jnp.einsum('pkhd,pthd->pkht', page_queries, keys_here, preferred_element_...  9.18 us
    all_to_all x1, starting transfers between devices, body(): lax.all_to_all(sendbuf, 'req', split_axis=0, concat_axis=0, tiled=True)  7.25 us
    all_to_all x2, starting transfers between devices, body(): lax.all_to_all(context_buf, 'req', split_axis=0, concat_axis=0, tiled=True)  6.69 us
  transfers between devices with their start and end apart: 6, of which 5 were waited for; matrix products, arithmetic and copies ran while one was open for 23% of the time, Pallas kernels for 0%

profile of v4, /device:TPU:0, one launch (start us, length us, event | category | flops | bytes accessed | tf_op | source)
XLA Modules:
  0.0 139.4 jit_solution(995969881943516526)
XLA Ops:
  0.0 1.0 fusion.55
  1.0 0.8 copy.67
  2.3 1.0 fusion.57
  3.8 0.9 reshape_reshape.3
  4.7 7.3 %all-to-all-start = ((bf16[8,12,2048]{2,1,0:T(8,128)(2,1)}), bf16[8,12,2048]{2,1,0:T(8,128)(2,1)S(1)}, u32[]{:S(2)}, u32[]{:S(2)}) async-start(bf16[8,12,2048]{2,1,0:T(8,128)(2,1)} %reshape_reshape.3), calls=%async_computation | async-start | bytes 1048576 | tf_op jit(solution)/shard_map/all_to_all | solution.py:79
  12.0 0.7 convert_element_type.104
  12.6 0.7 broadcast_compare_fusion
  13.4 0.7 broadcast_subtract_fusion
  15.1 3.0 %fusion.8 = f32[32,4,2,128]{3,0,2,1:T(8,128)S(1)} fusion(bf16[2048,4,2,128]{3,2,1,0:T(2,128)(2,1)} %param.14, bf16[32,2048]{1,0:T(8,128)(2,1)S(1)} %fusion.57), kind=kOutput, calls=%fused_computation.15 | convolution fusion | flops 134217728 | bytes 4456448 | tf_op jit(solution)/shard_map/rf,fhkd->rhkd/dot_general | solution.py:80
  18.1 13.0 %fusion.104 = (bf16[64,128,2,128]{3,2,1,0:T(2,128)(2,1)}, bf16[64,128,2,128]{3,2,1,0:T(2,128)(2,1)}) fusion(bf16[64,128,4,128]{3,2,1,0:T(4,128)(2,1)} %param.17), kind=kLoop, calls=%fused_computation.155 | loop fusion | bytes 16777216 | tf_op jit(solution)/shard_map/slice | solution.py:116
  31.2 8.7 %fusion.103 = (bf16[64,128,2,128]{3,2,1,0:T(2,128)(2,1)}, bf16[64,128,2,128]{3,2,1,0:T(2,128)(2,1)}) fusion(bf16[64,128,4,128]{3,2,1,0:T(4,128)(2,1)S(1)} %bitcast.165), kind=kLoop, calls=%fused_computation.154 | loop fusion | bytes 16777216 | tf_op jit(solution)/shard_map/slice | solution.py:116
  40.2 0.8 gather_fusion
  42.1 6.0 %all-to-all-start.3 = ((bf16[8,2,12,128]{3,1,2,0:T(2,128)(2,1)}), bf16[8,2,12,128]{3,1,2,0:T(2,128)(2,1)S(1)}, u32[]{:S(2)}, u32[]{:S(2)}) async-start(bf16[8,2,12,128]{3,1,2,0:T(2,128)(2,1)} %copy.82), calls=%async_computation.3 | async-start | bytes 98304 | tf_op jit(solution)/shard_map/all_to_all | solution.py:125
  49.1 5.8 %all-to-all-done.3 = bf16[8,2,12,128]{3,1,2,0:T(2,128)(2,1)S(1)} async-done(((bf16[8,2,12,128]{3,1,2,0:T(2,128)(2,1)}), bf16[8,2,12,128]{3,1,2,0:T(2,128)(2,1)S(1)}, u32[]{:S(2)}, u32[]{:S(2)}) %all-to-all-start.3) | async-done | bytes 49184 | tf_op jit(solution)/shard_map/all_to_all | solution.py:125
  54.9 3.5 %all-to-all-start.1 = ((bf16[8,2,12,128]{3,1,2,0:T(2,128)(2,1)}), bf16[8,2,12,128]{3,1,2,0:T(2,128)(2,1)S(1)}, u32[]{:S(2)}, u32[]{:S(2)}) async-start(bf16[8,2,12,128]{3,1,2,0:T(2,128)(2,1)} %copy.70), calls=%async_computation.1 | async-start | bytes 98304 | tf_op jit(solution)/shard_map/all_to_all | solution.py:125
  59.1 5.9 %all-to-all-done.1 = bf16[8,2,12,128]{3,1,2,0:T(2,128)(2,1)S(1)} async-done(((bf16[8,2,12,128]{3,1,2,0:T(2,128)(2,1)}), bf16[8,2,12,128]{3,1,2,0:T(2,128)(2,1)S(1)}, u32[]{:S(2)}, u32[]{:S(2)}) %all-to-all-start.1) | async-done | bytes 49184 | tf_op jit(solution)/shard_map/all_to_all | solution.py:125
  66.2 0.7 gather_fusion.2
  67.2 0.7 gather_fusion.5
  68.2 4.6 %fusion.107 = (f32[64,2,2]{1,2,0:T(2,128)S(1)}, f32[64,2,2,128]{3,1,2,0:T(2,128)S(1)}) fusion(bf16[64,128,2,128]{3,2,1,0:T(2,128)(2,1)} %get-tuple-element.12, bf16[64,2,2,128]{3,2,1,0:T(2,128)(2,1)S(1)} %gather_fusion.5, pred[64,128]{1,0:T(8,128)(4,1)S(1)} %fusion.79), kind=kOutput, calls=%fused_computation.158 | convolution fusion | flops 8486656 | bytes 4400128 | tf_op jit(solution)/shard_map/pkhd,pthd->pkht/dot_general | solution.py:141
  72.9 4.6 %fusion.106 = (f32[64,2,2]{1,2,0:T(2,128)S(1)}, f32[64,2,2,128]{3,1,2,0:T(2,128)S(1)}) fusion(bf16[64,128,2,128]{3,2,1,0:T(2,128)(2,1)} %get-tuple-element.11, bf16[64,2,2,128]{3,2,1,0:T(2,128)(2,1)S(1)} %gather_fusion.2, pred[64,128]{1,0:T(8,128)(4,1)S(1)} %fusion.79), kind=kOutput, calls=%fused_computation.157 | convolution fusion | flops 8486656 | bytes 4400128 | tf_op jit(solution)/shard_map/pkhd,pthd->pkht/dot_general | solution.py:141
  77.9 0.7 gather_fusion.3
  79.1 0.7 gather_fusion.6
  81.6 3.6 %fusion.14 = f32[64,2,2,128]{3,1,2,0:T(2,128)S(1)} fusion(bf16[64,128,2,128]{3,2,1,0:T(2,128)(2,1)} %get-tuple-element.10, f32[64,2,2,128]{3,1,2,0:T(2,128)S(1)} %get-tuple-element.40, f32[64,2,2]{1,2,0:T(2,128)S(1)} %copy.87), kind=kOutput, calls=%fused_computation.22 | convolution fusion | flops 8454144 | bytes 4457472 | tf_op jit(solution)/shard_map/pkht,pthd->pkhd/dot_general | solution.py:171
  85.2 1.3 fusion.11
  87.7 3.3 %all-to-all-start.4 = ((bf16[8,2,12,128]{3,1,2,0:T(2,128)(2,1)}), bf16[8,2,12,128]{3,1,2,0:T(2,128)(2,1)S(1)}, u32[]{:S(2)}, u32[]{:S(2)}) async-start(bf16[8,2,12,128]{3,1,2,0:T(2,128)(2,1)} %bitcast.44), calls=%async_computation.4 | async-start | bytes 98304 | tf_op jit(solution)/shard_map/all_to_all | solution.py:191
  91.9 6.0 %all-to-all-done.4 = bf16[8,2,12,128]{3,1,2,0:T(2,128)(2,1)S(1)} async-done(((bf16[8,2,12,128]{3,1,2,0:T(2,128)(2,1)}), bf16[8,2,12,128]{3,1,2,0:T(2,128)(2,1)S(1)}, u32[]{:S(2)}, u32[]{:S(2)}) %all-to-all-start.4) | async-done | bytes 49184 | tf_op jit(solution)/shard_map/all_to_all | solution.py:191
  97.8 3.3 %all-to-all-start.2 = ((bf16[8,2,12,128]{3,1,2,0:T(2,128)(2,1)}), bf16[8,2,12,128]{3,1,2,0:T(2,128)(2,1)S(1)}, u32[]{:S(2)}, u32[]{:S(2)}) async-start(bf16[8,2,12,128]{3,1,2,0:T(2,128)(2,1)} %bitcast.25), calls=%async_computation.2 | async-start | bytes 98304 | tf_op jit(solution)/shard_map/all_to_all | solution.py:191
  101.5 6.4 %all-to-all-done.2 = bf16[8,2,12,128]{3,1,2,0:T(2,128)(2,1)S(1)} async-done(((bf16[8,2,12,128]{3,1,2,0:T(2,128)(2,1)}), bf16[8,2,12,128]{3,1,2,0:T(2,128)(2,1)S(1)}, u32[]{:S(2)}, u32[]{:S(2)}) %all-to-all-start.2) | async-done | bytes 49184 | tf_op jit(solution)/shard_map/all_to_all | solution.py:191
  108.5 1.1 reshape.346
  109.5 2.6 %all-to-all-start.5 = ((f32[32,12,512]{2,1,0:T(8,128)}), f32[32,12,512]{2,1,0:T(8,128)S(1)}, u32[]{:S(2)}, u32[]{:S(2)}) async-start(f32[32,12,512]{2,1,0:T(8,128)} %reshape.346), calls=%async_computation.5 | async-start | bytes 2097152 | tf_op jit(solution)/shard_map/all_to_all | solution.py:207
  112.4 26.0 %all-to-all-done.5 = f32[32,12,512]{2,1,0:T(8,128)S(1)} async-done(((f32[32,12,512]{2,1,0:T(8,128)}), f32[32,12,512]{2,1,0:T(8,128)S(1)}, u32[]{:S(2)}, u32[]{:S(2)}) %all-to-all-start.5) | async-done | bytes 786464 | tf_op jit(solution)/shard_map/all_to_all | solution.py:207
  138.5 0.8 fusion.41
  (98 shorter events, 12.6 us)
Async XLA Ops:
  4.7 36.4 %all-to-all-start = ((bf16[8,12,2048]{2,1,0:T(8,128)(2,1)}), bf16[8,12,2048]{2,1,0:T(8,128)(2,1)S(1)}, u32[]{:S(2)}, u32[]{:S(2)}) async-start(bf16[8,12,2048]{2,1,0:T(8,128)(2,1)} %reshape_reshape.3), calls=%async_computation | async-start | bytes 1048576 | tf_op jit(solution)/shard_map/all_to_all | solution.py:79
  18.1 13.1 %slice-start = ((s8[8388608]{0:T(1024)(128)(4,1)}), s8[4194304]{0:T(1024)(128)(4,1)S(1)}, s32[]{:S(2)}) async-start(s8[8388608]{0:T(1024)(128)(4,1)} %bitcast.164), calls=%async_computation.6 | async-start | bytes 8388608
  18.1 13.0 %slice-start.1 = ((s8[8388608]{0:T(1024)(128)(4,1)}), s8[4194304]{0:T(1024)(128)(4,1)S(1)}, s32[]{:S(2)}) async-start(s8[8388608]{0:T(1024)(128)(4,1)} %bitcast.164), calls=%async_computation.7 | async-start | bytes 8388608
  31.2 9.1 %copy-start = (s32[32]{0:T(128)S(1)}, s32[32]{0:T(128)}, u32[]{:S(2)}) copy-start(s32[32]{0:T(128)} %param.19) | copy-start | bytes 388
  31.2 10.0 %copy-start.4 = (bf16[4,2048,128]{2,1,0:T(8,128)(2,1)S(1)}, bf16[4,2048,128]{2,1,0:T(8,128)(2,1)}, u32[]{:S(2)}) copy-start(bf16[4,2048,128]{2,1,0:T(8,128)(2,1)} %param.15) | copy-start | bytes 6291460
  42.1 12.8 %all-to-all-start.3 = ((bf16[8,2,12,128]{3,1,2,0:T(2,128)(2,1)}), bf16[8,2,12,128]{3,1,2,0:T(2,128)(2,1)S(1)}, u32[]{:S(2)}, u32[]{:S(2)}) async-start(bf16[8,2,12,128]{3,1,2,0:T(2,128)(2,1)} %copy.82), calls=%async_computation.3 | async-start | bytes 98304 | tf_op jit(solution)/shard_map/all_to_all | solution.py:125
  54.9 10.1 %all-to-all-start.1 = ((bf16[8,2,12,128]{3,1,2,0:T(2,128)(2,1)}), bf16[8,2,12,128]{3,1,2,0:T(2,128)(2,1)S(1)}, u32[]{:S(2)}, u32[]{:S(2)}) async-start(bf16[8,2,12,128]{3,1,2,0:T(2,128)(2,1)} %copy.70), calls=%async_computation.1 | async-start | bytes 98304 | tf_op jit(solution)/shard_map/all_to_all | solution.py:125
  81.6 3.6 %copy-start.1 = (bf16[64,128,2,128]{3,2,1,0:T(2,128)(2,1)S(1)}, bf16[64,128,2,128]{3,2,1,0:T(2,128)(2,1)}, u32[]{:S(2)}) copy-start(bf16[64,128,2,128]{3,2,1,0:T(2,128)(2,1)} %get-tuple-element.9) | copy-start | bytes 12582916
  85.2 15.9 %copy-start.2 = (bf16[4,128,2048]{2,1,0:T(8,128)(2,1)S(1)}, bf16[4,128,2048]{2,1,0:T(8,128)(2,1)}, u32[]{:S(2)}) copy-start(bf16[4,128,2048]{2,1,0:T(8,128)(2,1)} %param.16) | copy-start | bytes 6291460
  87.7 10.1 %all-to-all-start.4 = ((bf16[8,2,12,128]{3,1,2,0:T(2,128)(2,1)}), bf16[8,2,12,128]{3,1,2,0:T(2,128)(2,1)S(1)}, u32[]{:S(2)}, u32[]{:S(2)}) async-start(bf16[8,2,12,128]{3,1,2,0:T(2,128)(2,1)} %bitcast.44), calls=%async_computation.4 | async-start | bytes 98304 | tf_op jit(solution)/shard_map/all_to_all | solution.py:191
  97.8 10.1 %all-to-all-start.2 = ((bf16[8,2,12,128]{3,1,2,0:T(2,128)(2,1)}), bf16[8,2,12,128]{3,1,2,0:T(2,128)(2,1)S(1)}, u32[]{:S(2)}, u32[]{:S(2)}) async-start(bf16[8,2,12,128]{3,1,2,0:T(2,128)(2,1)} %bitcast.25), calls=%async_computation.2 | async-start | bytes 98304 | tf_op jit(solution)/shard_map/all_to_all | solution.py:191
  108.2 4.0 %copy-start.5 = (s32[32]{0:T(128)S(1)}, s32[32]{0:T(128)}, u32[]{:S(2)}) copy-start(s32[32]{0:T(128)} %param.23) | copy-start | bytes 388
  108.2 4.1 %copy-start.3 = (f32[32,2]{0,1:T(2,128)S(1)}, f32[32,2]{0,1:T(2,128)}, u32[]{:S(2)}) copy-start(f32[32,2]{0,1:T(2,128)} %param.22) | copy-start | bytes 772
  109.5 28.9 %all-to-all-start.5 = ((f32[32,12,512]{2,1,0:T(8,128)}), f32[32,12,512]{2,1,0:T(8,128)S(1)}, u32[]{:S(2)}, u32[]{:S(2)}) async-start(f32[32,12,512]{2,1,0:T(8,128)} %reshape.346), calls=%async_computation.5 | async-start | bytes 2097152 | tf_op jit(solution)/shard_map/all_to_all | solution.py:207

commit v5 on v2

--- a/solution.py
+++ b/solution.py
@@ -117,8 +117,12 @@
     )
     score_scale = 1.0 / head_dim**0.5
     page_queries = query_rot[page_owner]
+    head_eye = jnp.eye(heads_here, dtype=jnp.bfloat16)
+    spread_queries = page_queries[:, :, :, None, :] * head_eye[None, None, :, :, None]
     scores = (
-        jnp.einsum("pkhd,pthd->pkht", page_queries, cache_keys, preferred_element_type=jnp.float32)
+        jnp.einsum(
+            "pkjhd,pthd->pkjt", spread_queries, cache_keys, preferred_element_type=jnp.float32
+        )
         * score_scale
     )
     scores = jnp.where(in_range[:, None, None, :], scores, -jnp.inf)
@@ -141,8 +145,9 @@
     weights_rounded = weights.astype(jnp.bfloat16)
     fresh_rounded = lax.optimization_barrier(fresh_weight.astype(jnp.bfloat16)).astype(jnp.float32)
     page_context = jnp.einsum(
-        "pkht,pthd->pkhd", weights_rounded, cache_values, preferred_element_type=jnp.float32
-    )
+        "pkjt,pthd->pkjhd", weights_rounded, cache_values, preferred_element_type=jnp.float32
+    )
+    page_context = jnp.sum(page_context * head_eye.astype(jnp.float32)[None, None, :, :, None], axis=3)
     accumulated = jnp.einsum(
         "rp,pkhd->rkhd", owned_float, page_context, precision=lax.Precision.HIGHEST
     )

time: 101 us -> 96.7 us (0.957)
  matrix products: 21.1 us -> 18.1 us
    dot_general x2, matrix products: 13.7 us -> 10.7 us  [the longest x1 5.92 us: body(): jnp.einsum('pkjhd,pthd->pkjt', spread_queries, cache_keys, preferred_elem...]
  transfers between devices with their start and end apart: 3 -> 3, of which waited for: 3 -> 3; matrix products, arithmetic and copies ran while one was open for 5% -> 6% of each run, Pallas kernels for 0% -> 0%
where the time goes in v5:
time: 96.7 us; the launch traced here: 96.1 us
  waiting for transfers between devices  42.2 us (44%)
  matrix products  18.1 us (19%)
  starting transfers between devices  13.5 us (14%)
  blocking collectives  9.51 us (10%)
  local copies, waits for them, and re-layouts  7.52 us (8%)
  other arithmetic  4.93 us (5%)
    all_to_all x1, waiting for transfers between devices, body(): lax.all_to_all(partial_far.reshape(groups * head_count, capacity, width_h...  26 us
    all_to_all x1, blocking collectives, body(): lax.all_to_all(context_buf, 'req', split_axis=0, concat_axis=0, tiled=True)  9.51 us
    all_to_all x1, waiting for transfers between devices, body(): lax.all_to_all(sendbuf, 'req', split_axis=0, concat_axis=0, tiled=True)  9.16 us
    all_to_all x1, starting transfers between devices, body(): lax.all_to_all(sendbuf, 'req', split_axis=0, concat_axis=0, tiled=True)  7.26 us
    all_to_all x1, waiting for transfers between devices, body(): lax.all_to_all(queries_far, 'req', split_axis=0, concat_axis=0, tiled=True)  7.03 us
    dot_general x1, matrix products, body(): jnp.einsum('pkjhd,pthd->pkjt', spread_queries, cache_keys, preferred_elem...  5.92 us
    dot_general x1, matrix products, body(): jnp.einsum('pkjt,pthd->pkjhd', weights_rounded, cache_values, preferred_e...  4.74 us
    all_to_all x1, starting transfers between devices, body(): lax.all_to_all(queries_far, 'req', split_axis=0, concat_axis=0, tiled=True)  3.63 us
  transfers between devices with their start and end apart: 3, of which 3 were waited for; matrix products, arithmetic and copies ran while one was open for 6% of the time, Pallas kernels for 0%

profile of v5, /device:TPU:0, one launch (start us, length us, event | category | flops | bytes accessed | tf_op | source)
XLA Modules:
  0.0 96.1 jit_solution(11689467005268501671)
XLA Ops:
  0.0 0.9 copy.66
  1.2 0.2 select_reduce_fusion.3
  1.4 1.0 %fusion.38 = f32[32]{0:T(128)S(1)} fusion(bf16[32,2048]{1,0:T(8,128)(2,1)} %param.12), kind=kLoop, calls=%fused_computation.39 | loop fusion | flops 196576 | bytes 131200 | tf_op jit(solution)/shard_map/reduce_sum | solution.py:58
  2.4 1.0 %fusion.40 = bf16[32,2048]{1,0:T(8,128)(2,1)S(1)} fusion(bf16[32,2048]{1,0:T(8,128)(2,1)} %param.12, f32[2048]{0:T(1024)} %param.13, f32[32]{0:T(128)S(1)} %add_rsqrt_fusion), kind=kLoop, calls=%fused_computation.41 | loop fusion | flops 262144 | bytes 270464 | tf_op jit(solution)/shard_map/convert_element_type | solution.py:60
  3.7 0.2 convolution_convert_fusion
  4.0 0.9 reshape_reshape.3
  4.9 7.3 %all-to-all-start = ((bf16[8,12,2048]{2,1,0:T(8,128)(2,1)}), bf16[8,12,2048]{2,1,0:T(8,128)(2,1)S(1)}, u32[]{:S(2)}, u32[]{:S(2)}) async-start(bf16[8,12,2048]{2,1,0:T(8,128)(2,1)} %reshape_reshape.3), calls=%async_computation | async-start | bytes 1048576 | tf_op jit(solution)/shard_map/all_to_all | solution.py:80
  12.5 0.4 fusion.36
  12.9 0.8 gather_fusion
  13.7 3.0 %fusion.4 = f32[32,4,2,128]{3,0,2,1:T(8,128)S(1)} fusion(bf16[2048,4,2,128]{3,2,1,0:T(2,128)(2,1)} %param.14, bf16[32,2048]{1,0:T(8,128)(2,1)S(1)} %fusion.40), kind=kOutput, calls=%fused_computation.8 | convolution fusion | flops 134217728 | bytes 4456448 | tf_op jit(solution)/shard_map/rf,fhkd->rhkd/dot_general | solution.py:84
  17.1 0.4 select_reduce_fusion
  17.5 9.2 %all-to-all-done = bf16[8,12,2048]{2,1,0:T(8,128)(2,1)S(1)} async-done(((bf16[8,12,2048]{2,1,0:T(8,128)(2,1)}), bf16[8,12,2048]{2,1,0:T(8,128)(2,1)S(1)}, u32[]{:S(2)}, u32[]{:S(2)}) %all-to-all-start) | async-done | bytes 393248 | tf_op jit(solution)/shard_map/all_to_all | solution.py:80
  26.6 2.0 %fusion.24 = bf16[8,4,12,128]{3,2,1,0:T(8,128)(2,1)S(1)} fusion(bf16[4,2048,128]{2,1,0:T(8,128)(2,1)} %param.15, bf16[8,12,2048]{2,1,0:T(8,128)(2,1)S(1)} %all-to-all-done), kind=kOutput, calls=%fused_computation.21 | convolution fusion | flops 201375744 | bytes 2588672 | tf_op jit(solution)/shard_map/snd,pdh->spnh/dot_general | solution.py:78
  28.6 0.7 copy.69
  29.3 3.6 %all-to-all-start.1 = ((bf16[8,4,12,128]{3,1,2,0:T(4,128)(2,1)}), bf16[8,4,12,128]{3,1,2,0:T(4,128)(2,1)S(1)}, u32[]{:S(2)}, u32[]{:S(2)}) async-start(bf16[8,4,12,128]{3,1,2,0:T(4,128)(2,1)} %copy.69), calls=%async_computation.1 | async-start | bytes 196608 | tf_op jit(solution)/shard_map/all_to_all | solution.py:108
  33.0 7.0 %all-to-all-done.1 = bf16[8,4,12,128]{3,1,2,0:T(4,128)(2,1)S(1)} async-done(((bf16[8,4,12,128]{3,1,2,0:T(4,128)(2,1)}), bf16[8,4,12,128]{3,1,2,0:T(4,128)(2,1)S(1)}, u32[]{:S(2)}, u32[]{:S(2)}) %all-to-all-start.1) | async-done | bytes 98336 | tf_op jit(solution)/shard_map/all_to_all | solution.py:108
  40.1 0.7 gather_fusion.1
  40.7 0.2 subtract_convert_fusion
  41.1 0.7 gather_fusion.2
  41.8 5.9 %fusion.72 = (f32[64,2,4]{2,1,0:T(2,128)S(1)}, f32[64,2,4,128]{3,2,1,0:T(4,128)S(1)}) fusion(bf16[64,128,4,128,1]{3,2,1,0,4:T(4,128)(2,1)} %bitcast.116, bf16[4,4]{0,1:T(4,128)(2,1)S(1)} %fusion.64, bf16[64,2,4,128]{3,2,1,0:T(4,128)(2,1)S(1)} %gather_fusion.2, pred[64,128]{1,0:T(8,128)(4,1)S(1)} %fusion.59), kind=kOutput, calls=%fused_computation.107 | convolution fusion | flops 68353536 | bytes 8792096 | tf_op jit(solution)/shard_map/pkjhd,pthd->pkjt/dot_general | solution.py:123
  47.9 0.3 fusion.53
  48.4 0.7 gather_fusion.3
  49.1 0.4 fusion.44
  49.8 4.7 %fusion.12 = f32[64,2,4,128]{3,2,1,0:T(4,128)S(1)} fusion(bf16[64,128,4,128,1]{3,2,1,0,4:T(4,128)(2,1)} %bitcast.117, f32[4,4]{0,1:T(4,128)S(1)} %fusion.69, f32[64,2,4,128]{3,2,1,0:T(4,128)S(1)} %get-tuple-element.22, f32[64,2,4]{2,1,0:T(2,128)S(1)} %gather_fusion.3), kind=kOutput, calls=%fused_computation.16 | convolution fusion | flops 67698688 | bytes 8915008 | tf_op jit(solution)/shard_map/pkjt,pthd->pkjhd/dot_general | solution.py:147
  54.5 0.3 fusion.28
  54.8 0.2 convolution_convert_fusion.1
  55.0 9.5 %all_to_all.20 = bf16[8,4,12,128]{3,1,2,0:T(4,128)(2,1)S(1)} all-to-all(bf16[8,4,12,128]{3,1,2,0:T(4,128)(2,1)S(1)} %bitcast.110), channel_id=1, replica_groups=mesh['req'=8,'head'=4] {'req'}, dimensions={0} | all-to-all | bytes 196608 | tf_op jit(solution)/shard_map/all_to_all | solution.py:164
  64.5 0.5 convolution_bitcast_fusion
  65.2 1.1 %reshape.339 = f32[32,12,512]{2,1,0:T(8,128)} reshape(f32[8,48,512]{2,1,0:T(8,128)S(1)} %pad_maximum_fusion) | data formatting | bytes 1572864 | tf_op jit(solution)/shard_map/reshape | solution.py:180
  66.3 2.6 %all-to-all-start.3 = ((f32[32,12,512]{2,1,0:T(8,128)}), f32[32,12,512]{2,1,0:T(8,128)S(1)}, u32[]{:S(2)}, u32[]{:S(2)}) async-start(f32[32,12,512]{2,1,0:T(8,128)} %reshape.339), calls=%async_computation.3 | async-start | bytes 2097152 | tf_op jit(solution)/shard_map/all_to_all | solution.py:179
  69.1 26.0 %all-to-all-done.3 = f32[32,12,512]{2,1,0:T(8,128)S(1)} async-done(((f32[32,12,512]{2,1,0:T(8,128)}), f32[32,12,512]{2,1,0:T(8,128)S(1)}, u32[]{:S(2)}, u32[]{:S(2)}) %all-to-all-start.3) | async-done | bytes 786464 | tf_op jit(solution)/shard_map/all_to_all | solution.py:179
  95.3 0.8 fusion.29
  (58 shorter events, 2.7 us)
Async XLA Ops:
  0.0 64.5 %copy-start = (bf16[4,128,2048]{2,1,0:T(8,128)(2,1)S(1)}, bf16[4,128,2048]{2,1,0:T(8,128)(2,1)}, u32[]{:S(2)}) copy-start(bf16[4,128,2048]{2,1,0:T(8,128)(2,1)} %param.16) | copy-start | bytes 6291460
  0.0 12.4 %copy-start.1 = (s32[32]{0:T(128)S(1)}, s32[32]{0:T(128)}, u32[]{:S(2)}) copy-start(s32[32]{0:T(128)} %param.19) | copy-start | bytes 388
  0.0 12.5 %copy-start.2 = (s32[32,32]{1,0:T(8,128)S(1)}, s32[32,32]{1,0:T(8,128)}, u32[]{:S(2)}) copy-start(s32[32,32]{1,0:T(8,128)} %param.20) | copy-start | bytes 12292
  4.9 21.7 %all-to-all-start = ((bf16[8,12,2048]{2,1,0:T(8,128)(2,1)}), bf16[8,12,2048]{2,1,0:T(8,128)(2,1)S(1)}, u32[]{:S(2)}, u32[]{:S(2)}) async-start(bf16[8,12,2048]{2,1,0:T(8,128)(2,1)} %reshape_reshape.3), calls=%async_computation | async-start | bytes 1048576 | tf_op jit(solution)/shard_map/all_to_all | solution.py:80
  29.3 10.8 %all-to-all-start.1 = ((bf16[8,4,12,128]{3,1,2,0:T(4,128)(2,1)}), bf16[8,4,12,128]{3,1,2,0:T(4,128)(2,1)S(1)}, u32[]{:S(2)}, u32[]{:S(2)}) async-start(bf16[8,4,12,128]{3,1,2,0:T(4,128)(2,1)} %copy.69), calls=%async_computation.1 | async-start | bytes 196608 | tf_op jit(solution)/shard_map/all_to_all | solution.py:108
  65.0 4.1 %copy-start.4 = (s32[32]{0:T(128)S(1)}, s32[32]{0:T(128)}, u32[]{:S(2)}) copy-start(s32[32]{0:T(128)} %param.23) | copy-start | bytes 388
  65.0 4.0 %copy-start.3 = (f32[32,2]{0,1:T(2,128)S(1)}, f32[32,2]{0,1:T(2,128)}, u32[]{:S(2)}) copy-start(f32[32,2]{0,1:T(2,128)} %param.22) | copy-start | bytes 772
  66.3 28.9 %all-to-all-start.3 = ((f32[32,12,512]{2,1,0:T(8,128)}), f32[32,12,512]{2,1,0:T(8,128)S(1)}, u32[]{:S(2)}, u32[]{:S(2)}) async-start(f32[32,12,512]{2,1,0:T(8,128)} %reshape.339), calls=%async_computation.3 | async-start | bytes 2097152 | tf_op jit(solution)/shard_map/all_to_all | solution.py:179

commit v6 on v5

--- a/solution.py
+++ b/solution.py
@@ -65,20 +65,23 @@
     target = flat_expert * capacity + slot_index
     select = target[None, :] == jnp.arange(experts * capacity)[:, None]
     select_rows = select.astype(jnp.bfloat16)
-    repeated = jnp.repeat(normed, choices_each, axis=0)
-    sendbuf = jnp.dot(select_rows, repeated, preferred_element_type=jnp.float32).astype(
-        jnp.bfloat16
-    )
+    lanes = 128
+    blocks = model_width // lanes
+    repeated = jnp.repeat(normed, choices_each, axis=0).reshape(-1, blocks, lanes)
+    sendbuf = jnp.einsum(
+        "mr,rab->mab", select_rows, repeated, preferred_element_type=jnp.float32
+    ).astype(jnp.bfloat16)
     replicas = groups // experts
     sendbuf = jnp.broadcast_to(
-        sendbuf.reshape(experts, 1, capacity, model_width),
-        (experts, replicas, capacity, model_width),
-    )
-    sendbuf = sendbuf.reshape(groups, capacity, model_width)
+        sendbuf.reshape(experts, 1, capacity, blocks, lanes),
+        (experts, replicas, capacity, blocks, lanes),
+    )
+    sendbuf = sendbuf.reshape(groups, capacity * blocks, lanes)
+    tokens_far = lax.all_to_all(sendbuf, "req", split_axis=0, concat_axis=0, tiled=True)
     queries_far = jnp.einsum(
-        "snd,pdh->spnh",
-        lax.all_to_all(sendbuf, "req", split_axis=0, concat_axis=0, tiled=True),
-        query_weight,
+        "snab,pabh->spnh",
+        tokens_far.reshape(groups, capacity, blocks, lanes),
+        query_weight.reshape(pairs_here, blocks, lanes, head_dim),
         preferred_element_type=jnp.float32,
     ).astype(jnp.bfloat16)
     key_value = jnp.einsum(
@@ -159,10 +162,13 @@
     )
     context_buf = context_buf.reshape(experts, capacity, heads_here, head_dim).transpose(0, 2, 1, 3)
     context_buf = context_buf.reshape(groups, pairs_here, capacity, head_dim)
+    head_count = lax.axis_size("head")
+    width_here = model_width // head_count
+    wblocks = width_here // lanes
     partial_far = jnp.einsum(
-        "spnh,phd->snd",
+        "spnh,phcab->scnab",
         lax.all_to_all(context_buf, "req", split_axis=0, concat_axis=0, tiled=True),
-        output_weight,
+        output_weight.reshape(pairs_here, head_dim, head_count, wblocks, lanes),
         preferred_element_type=jnp.float32,
     )
     gate_flat = expert_gate.reshape(-1)
@@ -173,20 +179,20 @@
         .T
     )
     alive_rows = live_mask.astype(jnp.float32)[:, None]
-    head_count = lax.axis_size("head")
-    width_here = model_width // head_count
-    partial_far = partial_far.reshape(groups, capacity, head_count, width_here).transpose(0, 2, 1, 3)
     returned = lax.all_to_all(
-        partial_far.reshape(groups * head_count, capacity, width_here),
+        partial_far.reshape(groups * head_count, capacity * wblocks, lanes),
         ("req", "head"),
         split_axis=0,
         concat_axis=0,
         tiled=True,
     )
-    summed = returned.reshape(experts, replicas * head_count, capacity, width_here).sum(axis=1)
-    result = jnp.dot(
-        spread, summed.reshape(experts * capacity, width_here), precision=lax.Precision.HIGHEST
-    )
+    summed = returned.reshape(experts, replicas * head_count, capacity * wblocks, lanes).sum(axis=1)
+    result = jnp.einsum(
+        "rm,mab->rab",
+        spread,
+        summed.reshape(experts * capacity, wblocks, lanes),
+        precision=lax.Precision.HIGHEST,
+    ).reshape(row_count, width_here)
     return (result * alive_rows).astype(jnp.bfloat16)
 
 

time: 96.7 us -> 91 us (0.941)
  blocking collectives: 9.51 us -> 0 us
  waiting for transfers between devices: 42.2 us -> 34.4 us
  local copies, waits for them, and re-layouts: 7.52 us -> 12.7 us
  starting transfers between devices: 13.5 us -> 17.6 us
  other arithmetic: 4.93 us -> 6.79 us
    all_to_all x1 -> x0, blocking collectives: 9.51 us -> none  [body(): lax.all_to_all(context_buf, 'req', split_axis=0, concat_axis=0, tiled=True)]
    all_to_all x1, waiting for transfers between devices: 9.16 us -> 4.35 us  [body(): lax.all_to_all(sendbuf, 'req', split_axis=0, concat_axis=0, tiled=True)]
    all_to_all x1 -> x2, starting transfers between devices: 2.64 us -> 6.75 us  [the longest x1 3.39 us: body(): lax.all_to_all(partial_far.reshape(groups * head_count, capacity * wblock...]
    reshape x3 -> x1, local copies, waits for them, and re-layouts: 1.2 us -> 4.44 us  [body(): output_weight.reshape(pairs_here, head_dim, head_count, wblocks, lanes)]
    all_to_all x1 -> x2, waiting for transfers between devices: 26 us -> 23.1 us  [the longest x1 20.4 us: body(): lax.all_to_all(partial_far.reshape(groups * head_count, capacity * wblock...]
    transpose x0 -> x1, local copies, waits for them, and re-layouts: none -> 1.19 us  [body(): jnp.einsum('spnh,phcab->scnab', lax.all_to_all(context_buf, 'req', split_...]
  transfers between devices with their start and end apart: 3 -> 4, of which waited for: 3 -> 4; matrix products, arithmetic and copies ran while one was open for 6% -> 13% of each run, Pallas kernels for 0% -> 0%
where the time goes in v6:
time: 91 us; the launch traced here: 90.2 us
  waiting for transfers between devices  34.4 us (38%)
  matrix products  18.3 us (20%)
  starting transfers between devices  17.6 us (19%)
  local copies, waits for them, and re-layouts  12.7 us (14%)
  other arithmetic  6.79 us (7%)
    all_to_all x1, waiting for transfers between devices, body(): lax.all_to_all(partial_far.reshape(groups * head_count, capacity * wblock...  20.4 us
    all_to_all x1, starting transfers between devices, body(): lax.all_to_all(sendbuf, 'req', split_axis=0, concat_axis=0, tiled=True)  7.25 us
    all_to_all x1, waiting for transfers between devices, body(): lax.all_to_all(queries_far, 'req', split_axis=0, concat_axis=0, tiled=True)  7.03 us
    dot_general x1, matrix products, body(): jnp.einsum('pkjhd,pthd->pkjt', spread_queries, cache_keys, preferred_elem...  5.92 us
    dot_general x1, matrix products, body(): jnp.einsum('pkjt,pthd->pkjhd', weights_rounded, cache_values, preferred_e...  4.74 us
    reshape x1, local copies, waits for them, and re-layouts, body(): output_weight.reshape(pairs_here, head_dim, head_count, wblocks, lanes)  4.44 us
    all_to_all x1, waiting for transfers between devices, body(): lax.all_to_all(sendbuf, 'req', split_axis=0, concat_axis=0, tiled=True)  4.35 us
    all_to_all x1, starting transfers between devices, body(): lax.all_to_all(queries_far, 'req', split_axis=0, concat_axis=0, tiled=True)  3.62 us
  transfers between devices with their start and end apart: 4, of which 4 were waited for; matrix products, arithmetic and copies ran while one was open for 13% of the time, Pallas kernels for 0%

profile of v6, /device:TPU:0, one launch (start us, length us, event | category | flops | bytes accessed | tf_op | source)
XLA Modules:
  0.0 90.2 jit_solution(8841008491357238572)
XLA Ops:
  0.0 0.9 %copy.87 = s32[32,2]{1,0:T(8,128)S(1)} copy(s32[32,2]{0,1:T(2,128)} %param.21) | data formatting | bytes 512 | tf_op args[9]
  1.4 1.0 %fusion.37 = f32[32]{0:T(128)S(1)} fusion(bf16[32,2048]{1,0:T(8,128)(2,1)} %param.12), kind=kLoop, calls=%fused_computation.39 | loop fusion | flops 196576 | bytes 131200 | tf_op jit(solution)/shard_map/reduce_sum | solution.py:58
  2.4 1.0 %fusion.39 = bf16[32,2048]{1,0:T(8,128)(2,1)S(1)} fusion(bf16[32,2048]{1,0:T(8,128)(2,1)} %param.12, f32[2048]{0:T(1024)} %param.13, f32[32]{0:T(128)S(1)} %add_rsqrt_fusion), kind=kLoop, calls=%fused_computation.41 | loop fusion | flops 262144 | bytes 270464 | tf_op jit(solution)/shard_map/convert_element_type | solution.py:60
  3.8 0.4 convolution_convert_fusion
  4.2 0.9 copy.91
  5.1 7.3 %all-to-all-start = ((bf16[8,192,128]{2,1,0:T(8,128)(2,1)}), bf16[8,192,128]{2,1,0:T(8,128)(2,1)S(1)}, u32[]{:S(2)}, u32[]{:S(2)}) async-start(bf16[8,192,128]{2,1,0:T(8,128)(2,1)} %bitcast.5), calls=%async_computation | async-start | bytes 786432 | tf_op jit(solution)/shard_map/all_to_all | solution.py:80
  12.6 0.7 convert_element_type.100
  13.3 0.7 broadcast_compare_fusion
  14.0 0.7 broadcast_subtract_fusion
  14.7 0.4 fusion.35
  15.2 0.8 gather_fusion
  15.9 3.0 %fusion.4 = f32[32,4,2,128]{3,0,2,1:T(8,128)S(1)} fusion(bf16[2048,4,2,128]{3,2,1,0:T(2,128)(2,1)} %param.14, bf16[32,2048]{1,0:T(8,128)(2,1)S(1)} %fusion.39), kind=kOutput, calls=%fused_computation.8 | convolution fusion | flops 134217728 | bytes 4456448 | tf_op jit(solution)/shard_map/rf,fhkd->rhkd/dot_general | solution.py:87
  19.7 4.4 %all-to-all-done = bf16[8,192,128]{2,1,0:T(8,128)(2,1)S(1)} async-done(((bf16[8,192,128]{2,1,0:T(8,128)(2,1)}), bf16[8,192,128]{2,1,0:T(8,128)(2,1)S(1)}, u32[]{:S(2)}, u32[]{:S(2)}) %all-to-all-start) | async-done | bytes 393248 | tf_op jit(solution)/shard_map/all_to_all | solution.py:80
  24.0 0.4 fusion.25
  24.5 0.7 copy.93
  25.1 3.6 %all-to-all-start.1 = ((bf16[8,4,12,128]{3,1,2,0:T(4,128)(2,1)}), bf16[8,4,12,128]{3,1,2,0:T(4,128)(2,1)S(1)}, u32[]{:S(2)}, u32[]{:S(2)}) async-start(bf16[8,4,12,128]{3,1,2,0:T(4,128)(2,1)} %copy.93), calls=%async_computation.1 | async-start | bytes 196608 | tf_op jit(solution)/shard_map/all_to_all | solution.py:111
  28.9 7.0 %all-to-all-done.1 = bf16[8,4,12,128]{3,1,2,0:T(4,128)(2,1)S(1)} async-done(((bf16[8,4,12,128]{3,1,2,0:T(4,128)(2,1)}), bf16[8,4,12,128]{3,1,2,0:T(4,128)(2,1)S(1)}, u32[]{:S(2)}, u32[]{:S(2)}) %all-to-all-start.1) | async-done | bytes 98336 | tf_op jit(solution)/shard_map/all_to_all | solution.py:111
  35.9 0.7 gather_fusion.1
  36.9 0.7 gather_fusion.2
  37.6 5.9 %fusion.75 = (f32[64,2,4]{2,1,0:T(2,128)S(1)}, f32[64,2,4,128]{3,2,1,0:T(4,128)S(1)}) fusion(bf16[64,128,4,128,1]{3,2,1,0,4:T(4,128)(2,1)} %bitcast.138, bf16[4,4]{0,1:T(4,128)(2,1)S(1)} %fusion.68, bf16[64,2,4,128]{3,2,1,0:T(4,128)(2,1)S(1)} %gather_fusion.2, pred[64,128]{1,0:T(8,128)(4,1)S(1)} %fusion.63), kind=kOutput, calls=%fused_computation.110 | convolution fusion | flops 68353536 | bytes 8792096 | tf_op jit(solution)/shard_map/pkjhd,pthd->pkjt/dot_general | solution.py:126
  44.2 0.7 gather_fusion.3
  44.9 0.4 fusion.44
  45.6 4.7 %fusion.15 = f32[64,2,4,128]{3,2,1,0:T(4,128)S(1)} fusion(bf16[64,128,4,128,1]{3,2,1,0,4:T(4,128)(2,1)} %bitcast.139, f32[4,4]{0,1:T(4,128)S(1)} %fusion.73, f32[64,2,4,128]{3,2,1,0:T(4,128)S(1)} %get-tuple-element.18, f32[64,2,4]{2,1,0:T(2,128)S(1)} %gather_fusion.3), kind=kOutput, calls=%fused_computation.16 | convolution fusion | flops 67698688 | bytes 8915008 | tf_op jit(solution)/shard_map/pkjt,pthd->pkjhd/dot_general | solution.py:150
  50.9 0.7 reshape.346
  51.6 3.4 %all-to-all-start.2 = ((bf16[8,4,12,128]{3,1,2,0:T(4,128)(2,1)}), bf16[8,4,12,128]{3,1,2,0:T(4,128)(2,1)S(1)}, u32[]{:S(2)}, u32[]{:S(2)}) async-start(bf16[8,4,12,128]{3,1,2,0:T(4,128)(2,1)} %bitcast.34), calls=%async_computation.2 | async-start | bytes 196608 | tf_op jit(solution)/shard_map/all_to_all | solution.py:170
  55.0 4.4 %reshape.347 = bf16[4,128,4,4,128]{4,3,2,1,0:T(4,128)(2,1)} reshape(bf16[4,128,2048]{2,1,0:T(8,128)(2,1)} %param.16) | data formatting | bytes 4194304 | tf_op jit(solution)/shard_map/reshape | solution.py:171
  59.4 2.6 %all-to-all-done.2 = bf16[8,4,12,128]{3,1,2,0:T(4,128)(2,1)S(1)} async-done(((bf16[8,4,12,128]{3,1,2,0:T(4,128)(2,1)}), bf16[8,4,12,128]{3,1,2,0:T(4,128)(2,1)S(1)}, u32[]{:S(2)}, u32[]{:S(2)}) %all-to-all-start.2) | async-done | bytes 98336 | tf_op jit(solution)/shard_map/all_to_all | solution.py:170
  62.0 2.1 %fusion.9 = f32[8,4,12,4,128]{4,2,3,1,0:T(8,128)S(1)} fusion(bf16[4,128,4,4,128]{4,3,2,1,0:T(4,128)(2,1)} %reshape.347, bf16[8,4,12,128,1,1]{3,1,2,0,5,4:T(4,128)(2,1)S(1)} %bitcast.130), kind=kOutput, calls=%fused_computation.13 | convolution fusion | flops 201326592 | bytes 2981888 | tf_op jit(solution)/shard_map/spnh,phcab->scnab/dot_general | solution.py:168
  64.1 1.2 %copy.104 = f32[8,4,12,4,128]{4,3,2,1,0:T(4,128)} copy(f32[8,4,12,4,128]{4,2,3,1,0:T(8,128)S(1)} %fusion.9) | data formatting | bytes 1572864 | tf_op jit(solution)/shard_map/spnh,phcab->scnab/transpose | solution.py:168
  65.3 3.4 %all-to-all-start.3 = ((f32[32,48,128]{2,1,0:T(8,128)}), f32[32,48,128]{2,1,0:T(8,128)S(1)}, u32[]{:S(2)}, u32[]{:S(2)}) async-start(f32[32,48,128]{2,1,0:T(8,128)} %bitcast.40), calls=%async_computation.3 | async-start | bytes 1572864 | tf_op jit(solution)/shard_map/all_to_all | solution.py:182
  68.9 20.4 %all-to-all-done.3 = f32[32,48,128]{2,1,0:T(8,128)S(1)} async-done(((f32[32,48,128]{2,1,0:T(8,128)}), f32[32,48,128]{2,1,0:T(8,128)S(1)}, u32[]{:S(2)}, u32[]{:S(2)}) %all-to-all-start.3) | async-done | bytes 786464 | tf_op jit(solution)/shard_map/all_to_all | solution.py:182
  89.3 0.8 fusion.28
  (55 shorter events, 3.9 us)
Async XLA Ops:
  0.0 24.0 %copy-start = (bf16[4,2048,128]{2,1,0:T(8,128)(2,1)S(1)}, bf16[4,2048,128]{2,1,0:T(8,128)(2,1)}, u32[]{:S(2)}) copy-start(bf16[4,2048,128]{2,1,0:T(8,128)(2,1)} %param.15) | copy-start | bytes 6291460
  0.0 15.2 %copy-start.1 = (s32[32]{0:T(128)S(1)}, s32[32]{0:T(128)}, u32[]{:S(2)}) copy-start(s32[32]{0:T(128)} %param.19) | copy-start | bytes 388
  5.1 18.9 %all-to-all-start = ((bf16[8,192,128]{2,1,0:T(8,128)(2,1)}), bf16[8,192,128]{2,1,0:T(8,128)(2,1)S(1)}, u32[]{:S(2)}, u32[]{:S(2)}) async-start(bf16[8,192,128]{2,1,0:T(8,128)(2,1)} %bitcast.5), calls=%async_computation | async-start | bytes 786432 | tf_op jit(solution)/shard_map/all_to_all | solution.py:80
  25.1 10.7 %all-to-all-start.1 = ((bf16[8,4,12,128]{3,1,2,0:T(4,128)(2,1)}), bf16[8,4,12,128]{3,1,2,0:T(4,128)(2,1)S(1)}, u32[]{:S(2)}, u32[]{:S(2)}) async-start(bf16[8,4,12,128]{3,1,2,0:T(4,128)(2,1)} %copy.93), calls=%async_computation.1 | async-start | bytes 196608 | tf_op jit(solution)/shard_map/all_to_all | solution.py:111
  51.6 10.4 %all-to-all-start.2 = ((bf16[8,4,12,128]{3,1,2,0:T(4,128)(2,1)}), bf16[8,4,12,128]{3,1,2,0:T(4,128)(2,1)S(1)}, u32[]{:S(2)}, u32[]{:S(2)}) async-start(bf16[8,4,12,128]{3,1,2,0:T(4,128)(2,1)} %bitcast.34), calls=%async_computation.2 | async-start | bytes 196608 | tf_op jit(solution)/shard_map/all_to_all | solution.py:170
  59.4 9.4 %copy-start.3 = (s32[32]{0:T(128)S(1)}, s32[32]{0:T(128)}, u32[]{:S(2)}) copy-start(s32[32]{0:T(128)} %param.23) | copy-start | bytes 388
  59.4 9.4 %copy-start.2 = (f32[32,2]{0,1:T(2,128)S(1)}, f32[32,2]{0,1:T(2,128)}, u32[]{:S(2)}) copy-start(f32[32,2]{0,1:T(2,128)} %param.22) | copy-start | bytes 772
  65.3 24.0 %all-to-all-start.3 = ((f32[32,48,128]{2,1,0:T(8,128)}), f32[32,48,128]{2,1,0:T(8,128)S(1)}, u32[]{:S(2)}, u32[]{:S(2)}) async-start(f32[32,48,128]{2,1,0:T(8,128)} %bitcast.40), calls=%async_computation.3 | async-start | bytes 1572864 | tf_op jit(solution)/shard_map/all_to_all | solution.py:182

commit v7 on v6

--- a/solution.py
+++ b/solution.py
@@ -166,10 +166,13 @@
     width_here = model_width // head_count
     wblocks = width_here // lanes
     partial_far = jnp.einsum(
-        "spnh,phcab->scnab",
+        "spnh,phd->snd",
         lax.all_to_all(context_buf, "req", split_axis=0, concat_axis=0, tiled=True),
-        output_weight.reshape(pairs_here, head_dim, head_count, wblocks, lanes),
+        output_weight,
         preferred_element_type=jnp.float32,
+    )
+    partial_far = partial_far.reshape(groups, capacity, head_count, wblocks, lanes).transpose(
+        0, 2, 1, 3, 4
     )
     gate_flat = expert_gate.reshape(-1)
     spread = (

time: 91 us -> 88.4 us (0.971)
  blocking collectives: 0 us -> 9.51 us
  local copies, waits for them, and re-layouts: 12.7 us -> 7.51 us
  starting transfers between devices: 17.6 us -> 13.5 us
  waiting for transfers between devices: 34.4 us -> 31.8 us
    all_to_all x0 -> x1, blocking collectives: none -> 9.51 us  [body(): lax.all_to_all(context_buf, 'req', split_axis=0, concat_axis=0, tiled=True)]
    reshape x1 -> x0, local copies, waits for them, and re-layouts: 4.44 us -> none  [body(): output_weight.reshape(pairs_here, head_dim, head_count, wblocks, lanes)]
    all_to_all x1 -> x0, starting transfers between devices: 3.36 us -> none  [body(): lax.all_to_all(context_buf, 'req', split_axis=0, concat_axis=0, tiled=True)]
    all_to_all x1 -> x0, waiting for transfers between devices: 2.62 us -> none  [body(): lax.all_to_all(context_buf, 'req', split_axis=0, concat_axis=0, tiled=True)]
  transfers between devices with their start and end apart: 4 -> 3, of which waited for: 4 -> 3; matrix products, arithmetic and copies ran while one was open for 13% -> 9% of each run, Pallas kernels for 0% -> 0%
where the time goes in v7:
time: 88.4 us; the launch traced here: 87.8 us
  waiting for transfers between devices  31.8 us (36%)
  matrix products  18.4 us (21%)
  starting transfers between devices  13.5 us (15%)
  blocking collectives  9.51 us (11%)
  local copies, waits for them, and re-layouts  7.51 us (8%)
  other arithmetic  6.79 us (8%)
    all_to_all x1, waiting for transfers between devices, body(): lax.all_to_all(partial_far.reshape(groups * head_count, capacity * wblock...  20.4 us
    all_to_all x1, blocking collectives, body(): lax.all_to_all(context_buf, 'req', split_axis=0, concat_axis=0, tiled=True)  9.51 us
    all_to_all x1, starting transfers between devices, body(): lax.all_to_all(sendbuf, 'req', split_axis=0, concat_axis=0, tiled=True)  7.25 us
    all_to_all x1, waiting for transfers between devices, body(): lax.all_to_all(queries_far, 'req', split_axis=0, concat_axis=0, tiled=True)  7.03 us
    dot_general x1, matrix products, body(): jnp.einsum('pkjhd,pthd->pkjt', spread_queries, cache_keys, preferred_elem...  5.92 us
    dot_general x1, matrix products, body(): jnp.einsum('pkjt,pthd->pkjhd', weights_rounded, cache_values, preferred_e...  4.74 us
    all_to_all x1, waiting for transfers between devices, body(): lax.all_to_all(sendbuf, 'req', split_axis=0, concat_axis=0, tiled=True)  4.35 us
    all_to_all x1, starting transfers between devices, body(): lax.all_to_all(queries_far, 'req', split_axis=0, concat_axis=0, tiled=True)  3.62 us
  transfers between devices with their start and end apart: 3, of which 3 were waited for; matrix products, arithmetic and copies ran while one was open for 9% of the time, Pallas kernels for 0%

profile of v7, /device:TPU:0, one launch (start us, length us, event | category | flops | bytes accessed | tf_op | source)
XLA Modules:
  0.0 87.8 jit_solution(12317814012520865123)
XLA Ops:
  0.0 0.9 %copy.86 = s32[32,2]{1,0:T(8,128)S(1)} copy(s32[32,2]{0,1:T(2,128)} %param.21) | data formatting | bytes 512 | tf_op args[9]
  1.4 1.0 %fusion.33 = f32[32]{0:T(128)S(1)} fusion(bf16[32,2048]{1,0:T(8,128)(2,1)} %param.12), kind=kLoop, calls=%fused_computation.37 | loop fusion | flops 196576 | bytes 131200 | tf_op jit(solution)/shard_map/reduce_sum | solution.py:58
  2.4 1.0 %fusion.35 = bf16[32,2048]{1,0:T(8,128)(2,1)S(1)} fusion(bf16[32,2048]{1,0:T(8,128)(2,1)} %param.12, f32[2048]{0:T(1024)} %param.13, f32[32]{0:T(128)S(1)} %add_rsqrt_fusion), kind=kLoop, calls=%fused_computation.39 | loop fusion | flops 262144 | bytes 270464 | tf_op jit(solution)/shard_map/convert_element_type | solution.py:60
  3.8 0.4 convolution_convert_fusion
  4.2 0.9 %copy.90 = bf16[96,16,128]{2,1,0:T(8,128)(2,1)} copy(bf16[96,16,128]{2,0,1:T(8,128)(2,1)S(1)} %convolution_convert_fusion) | data formatting | bytes 786432 | tf_op jit(solution)/shard_map/convert_element_type | solution.py:73
  5.1 7.3 %all-to-all-start = ((bf16[8,192,128]{2,1,0:T(8,128)(2,1)}), bf16[8,192,128]{2,1,0:T(8,128)(2,1)S(1)}, u32[]{:S(2)}, u32[]{:S(2)}) async-start(bf16[8,192,128]{2,1,0:T(8,128)(2,1)} %bitcast.5), calls=%async_computation | async-start | bytes 786432 | tf_op jit(solution)/shard_map/all_to_all | solution.py:80
  12.6 0.7 convert_element_type.100
  13.3 0.7 broadcast_compare_fusion
  14.0 0.7 broadcast_subtract_fusion
  14.7 0.4 fusion.31
  15.2 0.8 gather_fusion
  15.9 3.0 %fusion.4 = f32[32,4,2,128]{3,0,2,1:T(8,128)S(1)} fusion(bf16[2048,4,2,128]{3,2,1,0:T(2,128)(2,1)} %param.14, bf16[32,2048]{1,0:T(8,128)(2,1)S(1)} %fusion.35), kind=kOutput, calls=%fused_computation.8 | convolution fusion | flops 134217728 | bytes 4456448 | tf_op jit(solution)/shard_map/rf,fhkd->rhkd/dot_general | solution.py:87
  19.3 0.4 select_reduce_fusion
  19.7 4.4 %all-to-all-done = bf16[8,192,128]{2,1,0:T(8,128)(2,1)S(1)} async-done(((bf16[8,192,128]{2,1,0:T(8,128)(2,1)}), bf16[8,192,128]{2,1,0:T(8,128)(2,1)S(1)}, u32[]{:S(2)}, u32[]{:S(2)}) %all-to-all-start) | async-done | bytes 393248 | tf_op jit(solution)/shard_map/all_to_all | solution.py:80
  24.0 0.4 fusion.21
  24.5 0.7 copy.92
  25.1 3.6 %all-to-all-start.1 = ((bf16[8,4,12,128]{3,1,2,0:T(4,128)(2,1)}), bf16[8,4,12,128]{3,1,2,0:T(4,128)(2,1)S(1)}, u32[]{:S(2)}, u32[]{:S(2)}) async-start(bf16[8,4,12,128]{3,1,2,0:T(4,128)(2,1)} %copy.92), calls=%async_computation.1 | async-start | bytes 196608 | tf_op jit(solution)/shard_map/all_to_all | solution.py:111
  28.9 7.0 %all-to-all-done.1 = bf16[8,4,12,128]{3,1,2,0:T(4,128)(2,1)S(1)} async-done(((bf16[8,4,12,128]{3,1,2,0:T(4,128)(2,1)}), bf16[8,4,12,128]{3,1,2,0:T(4,128)(2,1)S(1)}, u32[]{:S(2)}, u32[]{:S(2)}) %all-to-all-start.1) | async-done | bytes 98336 | tf_op jit(solution)/shard_map/all_to_all | solution.py:111
  35.9 0.7 gather_fusion.1
  36.9 0.7 gather_fusion.2
  37.6 5.9 %fusion.71 = (f32[64,2,4]{2,1,0:T(2,128)S(1)}, f32[64,2,4,128]{3,2,1,0:T(4,128)S(1)}) fusion(bf16[64,128,4,128,1]{3,2,1,0,4:T(4,128)(2,1)} %bitcast.136, bf16[4,4]{0,1:T(4,128)(2,1)S(1)} %fusion.64, bf16[64,2,4,128]{3,2,1,0:T(4,128)(2,1)S(1)} %gather_fusion.2, pred[64,128]{1,0:T(8,128)(4,1)S(1)} %fusion.59), kind=kOutput, calls=%fused_computation.108 | convolution fusion | flops 68353536 | bytes 8792096 | tf_op jit(solution)/shard_map/pkjhd,pthd->pkjt/dot_general | solution.py:126
  43.7 0.3 fusion.51
  44.2 0.7 gather_fusion.3
  44.9 0.4 fusion.40
  45.6 4.7 %fusion.11 = f32[64,2,4,128]{3,2,1,0:T(4,128)S(1)} fusion(bf16[64,128,4,128,1]{3,2,1,0,4:T(4,128)(2,1)} %bitcast.137, f32[4,4]{0,1:T(4,128)S(1)} %fusion.69, f32[64,2,4,128]{3,2,1,0:T(4,128)S(1)} %get-tuple-element.18, f32[64,2,4]{2,1,0:T(2,128)S(1)} %gather_fusion.3), kind=kOutput, calls=%fused_computation.14 | convolution fusion | flops 67698688 | bytes 8915008 | tf_op jit(solution)/shard_map/pkjt,pthd->pkjhd/dot_general | solution.py:150
  50.6 0.3 convolution_convert_fusion.1
  51.0 9.5 %all_to_all.20 = bf16[8,4,12,128]{3,1,2,0:T(4,128)(2,1)S(1)} all-to-all(bf16[8,4,12,128]{3,1,2,0:T(4,128)(2,1)S(1)} %bitcast.130), channel_id=1, replica_groups=mesh['req'=8,'head'=4] {'req'}, dimensions={0} | all-to-all | bytes 196608 | tf_op jit(solution)/shard_map/all_to_all | solution.py:170
  60.5 2.1 %fusion.6 = f32[8,12,2048,1]{2,0,3,1:T(8,128)S(1)} fusion(bf16[4,128,2048]{2,1,0:T(8,128)(2,1)} %param.16, bf16[8,4,12,128]{3,1,2,0:T(4,128)(2,1)S(1)} %all_to_all.20), kind=kOutput, calls=%fused_computation.10 | convolution fusion | flops 201326592 | bytes 2981888 | tf_op jit(solution)/shard_map/spnh,phd->snd/dot_general | solution.py:168
  62.6 1.1 %copy.103 = f32[8,4,12,4,128]{4,3,2,1,0:T(4,128)} copy(f32[8,4,12,4,128]{4,0,3,1,2:T(8,128)S(1)} %bitcast.127) | data formatting | bytes 1572864 | tf_op jit(solution)/shard_map/transpose | solution.py:174
  63.6 2.6 %all-to-all-start.3 = ((f32[32,48,128]{2,1,0:T(8,128)}), f32[32,48,128]{2,1,0:T(8,128)S(1)}, u32[]{:S(2)}, u32[]{:S(2)}) async-start(f32[32,48,128]{2,1,0:T(8,128)} %bitcast.39), calls=%async_computation.3 | async-start | bytes 1572864 | tf_op jit(solution)/shard_map/all_to_all | solution.py:185
  66.5 20.4 %all-to-all-done.3 = f32[32,48,128]{2,1,0:T(8,128)S(1)} async-done(((f32[32,48,128]{2,1,0:T(8,128)}), f32[32,48,128]{2,1,0:T(8,128)S(1)}, u32[]{:S(2)}, u32[]{:S(2)}) %all-to-all-start.3) | async-done | bytes 786464 | tf_op jit(solution)/shard_map/all_to_all | solution.py:185
  86.9 0.8 fusion.24
  (53 shorter events, 3.0 us)
Async XLA Ops:
  0.0 24.0 %copy-start = (bf16[4,2048,128]{2,1,0:T(8,128)(2,1)S(1)}, bf16[4,2048,128]{2,1,0:T(8,128)(2,1)}, u32[]{:S(2)}) copy-start(bf16[4,2048,128]{2,1,0:T(8,128)(2,1)} %param.15) | copy-start | bytes 6291460
  0.0 15.2 %copy-start.1 = (s32[32]{0:T(128)S(1)}, s32[32]{0:T(128)}, u32[]{:S(2)}) copy-start(s32[32]{0:T(128)} %param.19) | copy-start | bytes 388
  5.1 18.9 %all-to-all-start = ((bf16[8,192,128]{2,1,0:T(8,128)(2,1)}), bf16[8,192,128]{2,1,0:T(8,128)(2,1)S(1)}, u32[]{:S(2)}, u32[]{:S(2)}) async-start(bf16[8,192,128]{2,1,0:T(8,128)(2,1)} %bitcast.5), calls=%async_computation | async-start | bytes 786432 | tf_op jit(solution)/shard_map/all_to_all | solution.py:80
  25.1 10.7 %all-to-all-start.1 = ((bf16[8,4,12,128]{3,1,2,0:T(4,128)(2,1)}), bf16[8,4,12,128]{3,1,2,0:T(4,128)(2,1)S(1)}, u32[]{:S(2)}, u32[]{:S(2)}) async-start(bf16[8,4,12,128]{3,1,2,0:T(4,128)(2,1)} %copy.92), calls=%async_computation.1 | async-start | bytes 196608 | tf_op jit(solution)/shard_map/all_to_all | solution.py:111
  60.5 5.9 %copy-start.3 = (s32[32]{0:T(128)S(1)}, s32[32]{0:T(128)}, u32[]{:S(2)}) copy-start(s32[32]{0:T(128)} %param.23) | copy-start | bytes 388
  60.5 5.9 %copy-start.2 = (f32[32,2]{0,1:T(2,128)S(1)}, f32[32,2]{0,1:T(2,128)}, u32[]{:S(2)}) copy-start(f32[32,2]{0,1:T(2,128)} %param.22) | copy-start | bytes 772
  63.6 23.2 %all-to-all-start.3 = ((f32[32,48,128]{2,1,0:T(8,128)}), f32[32,48,128]{2,1,0:T(8,128)S(1)}, u32[]{:S(2)}, u32[]{:S(2)}) async-start(f32[32,48,128]{2,1,0:T(8,128)} %bitcast.39), calls=%async_computation.3 | async-start | bytes 1572864 | tf_op jit(solution)/shard_map/all_to_all | solution.py:185

commit v8 on v7

--- a/solution.py
+++ b/solution.py
@@ -58,19 +58,25 @@
         * lax.rsqrt(jnp.mean(as_float * as_float, axis=-1, keepdims=True) + eps)
         * norm_gain
     ).astype(jnp.bfloat16)
-    flat_expert = expert_choice.reshape(-1)
-    onehot = (flat_expert[:, None] == jnp.arange(experts)[None, :]).astype(jnp.int32)
+    choice_major = jnp.concatenate([expert_choice[:, k] for k in range(choices_each)])
+    onehot = (choice_major[:, None] == jnp.arange(experts)[None, :]).astype(jnp.int32)
     before = jnp.cumsum(onehot, axis=0) - onehot
     slot_index = jnp.sum(before * onehot, axis=1)
-    target = flat_expert * capacity + slot_index
+    target = (choice_major * capacity + slot_index).reshape(choices_each, row_count).T.reshape(-1)
     select = target[None, :] == jnp.arange(experts * capacity)[:, None]
     select_rows = select.astype(jnp.bfloat16)
     lanes = 128
     blocks = model_width // lanes
-    repeated = jnp.repeat(normed, choices_each, axis=0).reshape(-1, blocks, lanes)
-    sendbuf = jnp.einsum(
-        "mr,rab->mab", select_rows, repeated, preferred_element_type=jnp.float32
-    ).astype(jnp.bfloat16)
+    slot_used = jnp.any(select, axis=1)
+    slot_row = jnp.sum(
+        select.astype(jnp.int32) * jnp.arange(row_count * choices_each, dtype=jnp.int32)[None, :],
+        axis=1,
+    ) // choices_each
+    sendbuf = jnp.where(
+        slot_used[:, None, None],
+        normed.reshape(row_count, blocks, lanes)[slot_row],
+        jnp.zeros((), jnp.bfloat16),
+    )
     replicas = groups // experts
     sendbuf = jnp.broadcast_to(
         sendbuf.reshape(experts, 1, capacity, blocks, lanes),
@@ -114,12 +120,16 @@
         .transpose(0, 2, 1, 3)
         .reshape(experts * capacity, heads_here, head_dim)
     )
-    raw_query = queries[target].reshape(row_count, choices_each, heads_here, head_dim)
+    pair_target = target.reshape(row_count, choices_each)
+    raw_query = queries[pair_target]
     query_rot = rotate(raw_query.astype(jnp.float32), cache_length[:, None, None]).astype(
         jnp.bfloat16
     )
+    page_raw = queries[pair_target[page_owner]]
+    page_queries = rotate(page_raw.astype(jnp.float32), page_limit[:, None, None]).astype(
+        jnp.bfloat16
+    )
     score_scale = 1.0 / head_dim**0.5
-    page_queries = query_rot[page_owner]
     head_eye = jnp.eye(heads_here, dtype=jnp.bfloat16)
     spread_queries = page_queries[:, :, :, None, :] * head_eye[None, None, :, :, None]
     scores = (

time: 88.4 us -> 89.9 us (1.017)
  local copies, waits for them, and re-layouts: 7.51 us -> 8.92 us
  other arithmetic: 6.79 us -> 8.16 us
  waiting for transfers between devices: 31.8 us -> 30.7 us
    gather x2 -> x5, local copies, waits for them, and re-layouts: 1.35 us -> 2.75 us  [the longest x3 1.41 us: body(): page_raw = queries[pair_target[page_owner]]]
    all_to_all x1, waiting for transfers between devices: 4.35 us -> 3.25 us  [body(): lax.all_to_all(sendbuf, 'req', split_axis=0, concat_axis=0, tiled=True)]
    unnamed x0 -> x1, other arithmetic: none -> 1.03 us
    select_n x1 -> x4, other arithmetic: 0.01 us -> 1.03 us  [the longest x1 1.01 us: body(): jnp.where(slot_used[:, None, None], normed.reshape(row_count, blocks, lan...]
    convert_element_type x2, other arithmetic: 1.09 us -> 0.1 us  [the longest x1 0.08 us: body(): (choice_major[:, None] == jnp.arange(experts)[None, :]).astype(jnp.int32)]
  transfers between devices with their start and end apart: 3 -> 3, of which waited for: 3 -> 3; matrix products, arithmetic and copies ran while one was open for 9% -> 10% of each run, Pallas kernels for 0% -> 0%
where the time goes in v8:
time: 89.9 us; the launch traced here: 89.2 us
  waiting for transfers between devices  30.7 us (34%)
  matrix products  18 us (20%)
  starting transfers between devices  13.5 us (15%)
  blocking collectives  9.51 us (11%)
  local copies, waits for them, and re-layouts  8.92 us (10%)
  other arithmetic  8.16 us (9%)
    all_to_all x1, waiting for transfers between devices, body(): lax.all_to_all(partial_far.reshape(groups * head_count, capacity * wblock...  20.4 us
    all_to_all x1, blocking collectives, body(): lax.all_to_all(context_buf, 'req', split_axis=0, concat_axis=0, tiled=True)  9.51 us
    all_to_all x1, starting transfers between devices, body(): lax.all_to_all(sendbuf, 'req', split_axis=0, concat_axis=0, tiled=True)  7.26 us
    all_to_all x1, waiting for transfers between devices, body(): lax.all_to_all(queries_far, 'req', split_axis=0, concat_axis=0, tiled=True)  7.03 us
    dot_general x1, matrix products, body(): jnp.einsum('pkjhd,pthd->pkjt', spread_queries, cache_keys, preferred_elem...  5.92 us
    dot_general x1, matrix products, body(): jnp.einsum('pkjt,pthd->pkjhd', weights_rounded, cache_values, preferred_e...  4.76 us
    all_to_all x1, starting transfers between devices, body(): lax.all_to_all(queries_far, 'req', split_axis=0, concat_axis=0, tiled=True)  3.62 us
    all_to_all x1, waiting for transfers between devices, body(): lax.all_to_all(sendbuf, 'req', split_axis=0, concat_axis=0, tiled=True)  3.25 us
  transfers between devices with their start and end apart: 3, of which 3 were waited for; matrix products, arithmetic and copies ran while one was open for 10% of the time, Pallas kernels for 0%

profile of v8, /device:TPU:0, one launch (start us, length us, event | category | flops | bytes accessed | tf_op | source)
XLA Modules:
  0.0 89.2 jit_solution(4273637003729070028)
XLA Ops:
  0.0 0.9 slice_bitcast_fusion.2
  1.9 1.0 %fusion.33 = f32[32]{0:T(128)S(1)} fusion(bf16[32,2048]{1,0:T(8,128)(2,1)} %param.12), kind=kLoop, calls=%fused_computation.39 | loop fusion | flops 196576 | bytes 131200 | tf_op jit(solution)/shard_map/reduce_sum | solution.py:58
  2.9 1.0 %fusion.54 = bf16[4,8,16,128]{3,1,2,0:T(8,128)(2,1)S(1)} fusion(f32[2048]{0:T(1024)} %param.13, f32[32]{0:T(128)S(1)} %add_rsqrt_fusion, bf16[32,2048]{1,0:T(8,128)(2,1)} %param.12), kind=kLoop, calls=%fused_computation.73 | loop fusion | flops 262144 | bytes 270464
  4.3 0.7 gather_fusion.1
  5.0 1.0 %bitcast_select_fusion = bf16[8,192,128]{2,1,0:T(8,128)(2,1)} fusion(pred[8,192]{1,0:T(8,128)(4,1)S(1)} %broadcast_in_dim.58, bf16[8,192,128]{2,1,0:T(8,128)(2,1)S(1)} %bitcast.151), kind=kLoop, calls=%fused_computation.36 | loop fusion | flops 196608 | bytes 787968 | tf_op jit(solution)/shard_map/jit(_where)/select_n | solution.py:75
  6.0 7.3 %all-to-all-start = ((bf16[8,192,128]{2,1,0:T(8,128)(2,1)}), bf16[8,192,128]{2,1,0:T(8,128)(2,1)S(1)}, u32[]{:S(2)}, u32[]{:S(2)}) async-start(bf16[8,192,128]{2,1,0:T(8,128)(2,1)} %bitcast_select_fusion), calls=%async_computation | async-start | bytes 786432 | tf_op jit(solution)/shard_map/all_to_all | solution.py:86
  13.3 0.7 broadcast_compare_fusion
  14.0 0.7 broadcast_subtract_fusion
  14.7 0.4 fusion.31
  15.1 0.6 gather_fusion.2
  15.7 1.4 %gather_fusion = s32[64]{0:T(128)S(1)} fusion(s32[32]{0:T(128)} %param.19, s32[1024]{0:T(1024)S(1)} %pad_clamp_fusion.3), kind=kCustom, calls=%fused_computation | custom fusion | bytes 768 | tf_op jit(solution)/shard_map/gather | solution.py:113
  17.7 3.1 %fusion.4 = f32[32,4,2,128]{3,0,2,1:T(8,128)S(1)} fusion(bf16[2048,4,2,128]{3,2,1,0:T(2,128)(2,1)} %param.14, bf16[32,2048]{1,0:T(8,128)(2,1)S(1)} %copy-done.2, f32[2048]{0:T(1024)S(1)} %copy-done.3, f32[32]{0:T(128)S(1)} %add_rsqrt_fusion), kind=kOutput, calls=%fused_computation.10 | convolution fusion | flops 134479872 | bytes 4464768 | tf_op jit(solution)/shard_map/rf,fhkd->rhkd/dot_general | solution.py:93
  21.1 0.4 select_reduce_fusion
  21.7 3.3 %all-to-all-done = bf16[8,192,128]{2,1,0:T(8,128)(2,1)S(1)} async-done(((bf16[8,192,128]{2,1,0:T(8,128)(2,1)}), bf16[8,192,128]{2,1,0:T(8,128)(2,1)S(1)}, u32[]{:S(2)}, u32[]{:S(2)}) %all-to-all-start) | async-done | bytes 393248 | tf_op jit(solution)/shard_map/all_to_all | solution.py:86
  24.9 0.4 fusion.21
  25.4 0.7 copy.86
  26.0 3.6 %all-to-all-start.1 = ((bf16[8,4,12,128]{3,1,2,0:T(4,128)(2,1)}), bf16[8,4,12,128]{3,1,2,0:T(4,128)(2,1)S(1)}, u32[]{:S(2)}, u32[]{:S(2)}) async-start(bf16[8,4,12,128]{3,1,2,0:T(4,128)(2,1)} %copy.86), calls=%async_computation.1 | async-start | bytes 196608 | tf_op jit(solution)/shard_map/all_to_all | solution.py:117
  29.8 7.0 %all-to-all-done.1 = bf16[8,4,12,128]{3,1,2,0:T(4,128)(2,1)S(1)} async-done(((bf16[8,4,12,128]{3,1,2,0:T(4,128)(2,1)}), bf16[8,4,12,128]{3,1,2,0:T(4,128)(2,1)S(1)}, u32[]{:S(2)}, u32[]{:S(2)}) %all-to-all-start.1) | async-done | bytes 98336 | tf_op jit(solution)/shard_map/all_to_all | solution.py:117
  36.8 0.7 gather_fusion.3
  38.0 5.9 %fusion.69 = (f32[64,2,4]{2,1,0:T(2,128)S(1)}, f32[64,2,4,128]{3,2,1,0:T(4,128)S(1)}) fusion(bf16[64,128,4,128,1]{3,2,1,0,4:T(4,128)(2,1)} %bitcast.163, bf16[4,4]{0,1:T(4,128)(2,1)S(1)} %fusion.63, bf16[64,2,4,128]{3,2,1,0:T(4,128)(2,1)S(1)} %pad_maximum_fusion, pred[64,128]{1,0:T(8,128)(4,1)S(1)} %fusion.59), kind=kOutput, calls=%fused_computation.124 | convolution fusion | flops 68353536 | bytes 8792096 | tf_op jit(solution)/shard_map/pkjhd,pthd->pkjt/dot_general | solution.py:136
  44.1 0.7 gather_fusion.4
  45.1 0.3 fusion.50
  45.6 0.7 gather_fusion.5
  46.3 0.4 fusion.39
  47.0 4.8 %fusion.11 = f32[64,2,4,128]{3,2,1,0:T(4,128)S(1)} fusion(bf16[64,128,4,128,1]{3,2,1,0,4:T(4,128)(2,1)} %bitcast.164, f32[4,4]{0,1:T(4,128)S(1)} %fusion.68, f32[64,2,4,128]{3,2,1,0:T(4,128)S(1)} %get-tuple-element.22, f32[64,2,4]{2,1,0:T(2,128)S(1)} %gather_fusion.5), kind=kOutput, calls=%fused_computation.15 | convolution fusion | flops 67698688 | bytes 8915008 | tf_op jit(solution)/shard_map/pkjt,pthd->pkjhd/dot_general | solution.py:160
  52.1 0.3 convolution_convert_fusion
  52.4 9.5 %all_to_all.20 = bf16[8,4,12,128]{3,1,2,0:T(4,128)(2,1)S(1)} all-to-all(bf16[8,4,12,128]{3,1,2,0:T(4,128)(2,1)S(1)} %bitcast.158), channel_id=1, replica_groups=mesh['req'=8,'head'=4] {'req'}, dimensions={0} | all-to-all | bytes 196608 | tf_op jit(solution)/shard_map/all_to_all | solution.py:180
  61.9 2.1 %fusion.6 = f32[8,12,2048,1]{2,0,3,1:T(8,128)S(1)} fusion(bf16[4,128,2048]{2,1,0:T(8,128)(2,1)} %param.16, bf16[8,4,12,128]{3,1,2,0:T(4,128)(2,1)S(1)} %all_to_all.20), kind=kOutput, calls=%fused_computation.12 | convolution fusion | flops 201326592 | bytes 2981888 | tf_op jit(solution)/shard_map/spnh,phd->snd/dot_general | solution.py:178
  64.0 1.1 %copy.99 = f32[8,4,12,4,128]{4,3,2,1,0:T(4,128)} copy(f32[8,4,12,4,128]{4,0,3,1,2:T(8,128)S(1)} %bitcast.154) | data formatting | bytes 1572864 | tf_op jit(solution)/shard_map/transpose | solution.py:184
  65.1 2.6 %all-to-all-start.3 = ((f32[32,48,128]{2,1,0:T(8,128)}), f32[32,48,128]{2,1,0:T(8,128)S(1)}, u32[]{:S(2)}, u32[]{:S(2)}) async-start(f32[32,48,128]{2,1,0:T(8,128)} %bitcast.45), calls=%async_computation.3 | async-start | bytes 1572864 | tf_op jit(solution)/shard_map/all_to_all | solution.py:195
  67.9 20.4 %all-to-all-done.3 = f32[32,48,128]{2,1,0:T(8,128)S(1)} async-done(((f32[32,48,128]{2,1,0:T(8,128)}), f32[32,48,128]{2,1,0:T(8,128)S(1)}, u32[]{:S(2)}, u32[]{:S(2)}) %all-to-all-start.3) | async-done | bytes 786464 | tf_op jit(solution)/shard_map/all_to_all | solution.py:195
  88.4 0.8 fusion.24
  (75 shorter events, 4.4 us)
Async XLA Ops:
  0.0 24.9 %copy-start = (bf16[4,2048,128]{2,1,0:T(8,128)(2,1)S(1)}, bf16[4,2048,128]{2,1,0:T(8,128)(2,1)}, u32[]{:S(2)}) copy-start(bf16[4,2048,128]{2,1,0:T(8,128)(2,1)} %param.15) | copy-start | bytes 6291460
  0.0 17.7 %copy-start.2 = (bf16[32,2048]{1,0:T(8,128)(2,1)S(1)}, bf16[32,2048]{1,0:T(8,128)(2,1)}, u32[]{:S(2)}) copy-start(bf16[32,2048]{1,0:T(8,128)(2,1)} %param.12) | copy-start | bytes 393220
  0.0 17.7 %copy-start.3 = (f32[2048]{0:T(1024)S(1)}, f32[2048]{0:T(1024)}, u32[]{:S(2)}) copy-start(f32[2048]{0:T(1024)} %param.13) | copy-start | bytes 24580
  0.0 17.2 %copy-start.1 = (s32[32]{0:T(128)S(1)}, s32[32]{0:T(128)}, u32[]{:S(2)}) copy-start(s32[32]{0:T(128)} %param.19) | copy-start | bytes 388
  6.0 19.0 %all-to-all-start = ((bf16[8,192,128]{2,1,0:T(8,128)(2,1)}), bf16[8,192,128]{2,1,0:T(8,128)(2,1)S(1)}, u32[]{:S(2)}, u32[]{:S(2)}) async-start(bf16[8,192,128]{2,1,0:T(8,128)(2,1)} %bitcast_select_fusion), calls=%async_computation | async-start | bytes 786432 | tf_op jit(solution)/shard_map/all_to_all | solution.py:86
  26.0 10.7 %all-to-all-start.1 = ((bf16[8,4,12,128]{3,1,2,0:T(4,128)(2,1)}), bf16[8,4,12,128]{3,1,2,0:T(4,128)(2,1)S(1)}, u32[]{:S(2)}, u32[]{:S(2)}) async-start(bf16[8,4,12,128]{3,1,2,0:T(4,128)(2,1)} %copy.86), calls=%async_computation.1 | async-start | bytes 196608 | tf_op jit(solution)/shard_map/all_to_all | solution.py:117
  61.9 5.9 %copy-start.5 = (s32[32]{0:T(128)S(1)}, s32[32]{0:T(128)}, u32[]{:S(2)}) copy-start(s32[32]{0:T(128)} %param.23) | copy-start | bytes 388
  61.9 5.9 %copy-start.4 = (f32[32,2]{0,1:T(2,128)S(1)}, f32[32,2]{0,1:T(2,128)}, u32[]{:S(2)}) copy-start(f32[32,2]{0,1:T(2,128)} %param.22) | copy-start | bytes 772
  65.1 23.2 %all-to-all-start.3 = ((f32[32,48,128]{2,1,0:T(8,128)}), f32[32,48,128]{2,1,0:T(8,128)S(1)}, u32[]{:S(2)}, u32[]{:S(2)}) async-start(f32[32,48,128]{2,1,0:T(8,128)} %bitcast.45), calls=%async_computation.3 | async-start | bytes 1572864 | tf_op jit(solution)/shard_map/all_to_all | solution.py:195

commit v9 on v7

--- a/solution.py
+++ b/solution.py
@@ -171,9 +171,17 @@
         output_weight,
         preferred_element_type=jnp.float32,
     )
-    partial_far = partial_far.reshape(groups, capacity, head_count, wblocks, lanes).transpose(
-        0, 2, 1, 3, 4
-    )
+    head_index = lax.axis_index("head")
+    held = partial_far.reshape(groups, capacity, head_count, width_here)
+    bit = 1
+    while bit < head_count:
+        pair = held.reshape(groups, capacity, held.shape[2] // 2, 2, width_here)
+        upper = (head_index // bit) % 2 == 1
+        keep = jnp.where(upper, pair[:, :, :, 1], pair[:, :, :, 0])
+        give = jnp.where(upper, pair[:, :, :, 0], pair[:, :, :, 1])
+        got = lax.ppermute(give, "head", [(c, c ^ bit) for c in range(head_count)])
+        held = keep + got
+        bit *= 2
     gate_flat = expert_gate.reshape(-1)
     spread = (
         jnp.where(select, gate_flat[None, :], jnp.float32(0.0))
@@ -183,13 +191,13 @@
     )
     alive_rows = live_mask.astype(jnp.float32)[:, None]
     returned = lax.all_to_all(
-        partial_far.reshape(groups * head_count, capacity * wblocks, lanes),
-        ("req", "head"),
+        held.reshape(groups, capacity * wblocks, lanes),
+        "req",
         split_axis=0,
         concat_axis=0,
         tiled=True,
     )
-    summed = returned.reshape(experts, replicas * head_count, capacity * wblocks, lanes).sum(axis=1)
+    summed = returned.reshape(experts, replicas, capacity * wblocks, lanes).sum(axis=1)
     result = jnp.einsum(
         "rm,mab->rab",
         spread,

time: 88.4 us -> 92.7 us (1.049)
  blocking collectives: 9.51 us -> 0 us
  starting transfers between devices: 13.5 us -> 19.5 us
  other arithmetic: 6.79 us -> 10.2 us
  local copies, waits for them, and re-layouts: 7.51 us -> 9.73 us
  waiting for transfers between devices: 31.8 us -> 32.9 us
    all_to_all x1 -> x0, blocking collectives: 9.51 us -> none  [body(): lax.all_to_all(context_buf, 'req', split_axis=0, concat_axis=0, tiled=True)]
    ppermute x0 -> x2, waiting for transfers between devices: none -> 7.09 us  [body(): got = lax.ppermute(give, 'head', [(c, c ^ bit) for c in range(head_count)])]
    all_to_all x1 -> x2, waiting for transfers between devices: 20.4 us -> 14.4 us  [the longest x1 7.53 us: body(): lax.all_to_all(held.reshape(groups, capacity * wblocks, lanes), 'req', sp...]
    all_to_all x1 -> x2, starting transfers between devices: 2.62 us -> 6.93 us  [the longest x1 3.54 us: body(): lax.all_to_all(context_buf, 'req', split_axis=0, concat_axis=0, tiled=True)]
    slice x0 -> x2, other arithmetic: none -> 1.92 us  [body(): keep = jnp.where(upper, pair[:, :, :, 1], pair[:, :, :, 0])]
    another operation x0 -> x1, local copies, waits for them, and re-layouts: none -> 1.8 us  [body(): pair = held.reshape(groups, capacity, held.shape[2] // 2, 2, width_here)]
    ppermute x0 -> x2, starting transfers between devices: none -> 1.66 us  [body(): got = lax.ppermute(give, 'head', [(c, c ^ bit) for c in range(head_count)])]
    reshape x0 -> x1, other arithmetic: none -> 1.38 us  [body(): pair = held.reshape(groups, capacity, held.shape[2] // 2, 2, width_here)]
  transfers between devices with their start and end apart: 3 -> 6, of which waited for: 3 -> 6; matrix products, arithmetic and copies ran while one was open for 9% -> 8% of each run, Pallas kernels for 0% -> 0%
where the time goes in v9:
time: 92.7 us; the launch traced here: 91.9 us
  waiting for transfers between devices  32.9 us (35%)
  starting transfers between devices  19.5 us (21%)
  matrix products  19.2 us (21%)
  other arithmetic  10.2 us (11%)
  local copies, waits for them, and re-layouts  9.73 us (10%)
    all_to_all x1, waiting for transfers between devices, body(): lax.all_to_all(held.reshape(groups, capacity * wblocks, lanes), 'req', sp...  7.53 us
    all_to_all x1, starting transfers between devices, body(): lax.all_to_all(sendbuf, 'req', split_axis=0, concat_axis=0, tiled=True)  7.25 us
    ppermute x2, waiting for transfers between devices, body(): got = lax.ppermute(give, 'head', [(c, c ^ bit) for c in range(head_count)])  7.09 us
    all_to_all x1, waiting for transfers between devices, body(): lax.all_to_all(queries_far, 'req', split_axis=0, concat_axis=0, tiled=True)  7.03 us
    all_to_all x1, waiting for transfers between devices, body(): lax.all_to_all(context_buf, 'req', split_axis=0, concat_axis=0, tiled=True)  6.87 us
    dot_general x1, matrix products, body(): jnp.einsum('pkjhd,pthd->pkjt', spread_queries, cache_keys, preferred_elem...  5.93 us
    dot_general x1, matrix products, body(): jnp.einsum('pkjt,pthd->pkjhd', weights_rounded, cache_values, preferred_e...  4.74 us
    all_to_all x1, waiting for transfers between devices, body(): lax.all_to_all(sendbuf, 'req', split_axis=0, concat_axis=0, tiled=True)  4.36 us
  transfers between devices with their start and end apart: 6, of which 6 were waited for; matrix products, arithmetic and copies ran while one was open for 8% of the time, Pallas kernels for 0%

profile of v9, /device:TPU:0, one launch (start us, length us, event | category | flops | bytes accessed | tf_op | source)
XLA Modules:
  0.0 91.9 jit_solution(6843387389767031769)
XLA Ops:
  0.0 1.2 %fusion.35 = f32[32]{0:T(128)S(1)} fusion(bf16[32,2048]{1,0:T(8,128)(2,1)} %param.12), kind=kLoop, calls=%fused_computation.43 | loop fusion | flops 196576 | bytes 131200 | tf_op jit(solution)/shard_map/reduce_sum | solution.py:58
  1.2 0.8 copy.124
  2.5 1.0 %fusion.37 = bf16[32,2048]{1,0:T(8,128)(2,1)S(1)} fusion(bf16[32,2048]{1,0:T(8,128)(2,1)} %param.12, f32[2048]{0:T(1024)} %param.13, f32[32]{0:T(128)S(1)} %add_rsqrt_fusion), kind=kLoop, calls=%fused_computation.45 | loop fusion | flops 262144 | bytes 270464 | tf_op jit(solution)/shard_map/convert_element_type | solution.py:60
  4.2 0.9 copy.128
  5.1 7.3 %all-to-all-start = ((bf16[8,192,128]{2,1,0:T(8,128)(2,1)}), bf16[8,192,128]{2,1,0:T(8,128)(2,1)S(1)}, u32[]{:S(2)}, u32[]{:S(2)}) async-start(bf16[8,192,128]{2,1,0:T(8,128)(2,1)} %bitcast.5), calls=%async_computation | async-start | bytes 786432 | tf_op jit(solution)/shard_map/all_to_all | solution.py:80
  12.5 0.7 convert_element_type.100
  13.1 0.7 broadcast_compare_fusion
  13.9 0.7 broadcast_subtract_fusion
  15.0 0.8 gather_fusion
  15.9 3.0 %fusion.4 = f32[32,4,2,128]{3,0,2,1:T(8,128)S(1)} fusion(bf16[2048,4,2,128]{3,2,1,0:T(2,128)(2,1)} %param.14, bf16[32,2048]{1,0:T(8,128)(2,1)S(1)} %fusion.37), kind=kOutput, calls=%fused_computation.8 | convolution fusion | flops 134217728 | bytes 4456448 | tf_op jit(solution)/shard_map/rf,fhkd->rhkd/dot_general | solution.py:87
  19.7 4.4 %all-to-all-done = bf16[8,192,128]{2,1,0:T(8,128)(2,1)S(1)} async-done(((bf16[8,192,128]{2,1,0:T(8,128)(2,1)}), bf16[8,192,128]{2,1,0:T(8,128)(2,1)S(1)}, u32[]{:S(2)}, u32[]{:S(2)}) %all-to-all-start) | async-done | bytes 393248 | tf_op jit(solution)/shard_map/all_to_all | solution.py:80
  24.5 0.7 copy.130
  25.1 3.6 %all-to-all-start.1 = ((bf16[8,4,12,128]{3,1,2,0:T(4,128)(2,1)}), bf16[8,4,12,128]{3,1,2,0:T(4,128)(2,1)S(1)}, u32[]{:S(2)}, u32[]{:S(2)}) async-start(bf16[8,4,12,128]{3,1,2,0:T(4,128)(2,1)} %copy.130), calls=%async_computation.1 | async-start | bytes 196608 | tf_op jit(solution)/shard_map/all_to_all | solution.py:111
  28.8 7.0 %all-to-all-done.1 = bf16[8,4,12,128]{3,1,2,0:T(4,128)(2,1)S(1)} async-done(((bf16[8,4,12,128]{3,1,2,0:T(4,128)(2,1)}), bf16[8,4,12,128]{3,1,2,0:T(4,128)(2,1)S(1)}, u32[]{:S(2)}, u32[]{:S(2)}) %all-to-all-start.1) | async-done | bytes 98336 | tf_op jit(solution)/shard_map/all_to_all | solution.py:111
  36.9 0.7 gather_fusion.2
  37.9 5.9 %fusion.77 = (f32[64,2,4]{2,1,0:T(2,128)S(1)}, f32[64,2,4,128]{3,2,1,0:T(4,128)S(1)}) fusion(bf16[64,128,4,128,1]{3,2,1,0,4:T(4,128)(2,1)} %bitcast.152, bf16[4,4]{0,1:T(4,128)(2,1)S(1)} %fusion.68, bf16[64,2,4,128]{3,2,1,0:T(4,128)(2,1)S(1)} %gather_fusion.2, pred[64,128]{1,0:T(8,128)(4,1)S(1)} %fusion.63), kind=kOutput, calls=%fused_computation.120 | convolution fusion | flops 68353536 | bytes 8792096 | tf_op jit(solution)/shard_map/pkjhd,pthd->pkjt/dot_general | solution.py:126
  44.2 0.7 gather_fusion.3
  45.6 4.7 %fusion.10 = f32[64,2,4,128]{3,2,1,0:T(4,128)S(1)} fusion(bf16[64,128,4,128,1]{3,2,1,0,4:T(4,128)(2,1)} %bitcast.153, f32[4,4]{0,1:T(4,128)S(1)} %fusion.73, f32[64,2,4,128]{3,2,1,0:T(4,128)S(1)} %get-tuple-element.24, f32[64,2,4]{2,1,0:T(2,128)S(1)} %gather_fusion.3), kind=kOutput, calls=%fused_computation.14 | convolution fusion | flops 67698688 | bytes 8915008 | tf_op jit(solution)/shard_map/pkjt,pthd->pkjhd/dot_general | solution.py:150
  50.9 0.7 reshape.395
  51.5 3.5 %all-to-all-start.2 = ((bf16[8,4,12,128]{3,1,2,0:T(4,128)(2,1)}), bf16[8,4,12,128]{3,1,2,0:T(4,128)(2,1)S(1)}, u32[]{:S(2)}, u32[]{:S(2)}) async-start(bf16[8,4,12,128]{3,1,2,0:T(4,128)(2,1)} %bitcast.34), calls=%async_computation.2 | async-start | bytes 196608 | tf_op jit(solution)/shard_map/all_to_all | solution.py:170
  55.1 6.9 %all-to-all-done.2 = bf16[8,4,12,128]{3,1,2,0:T(4,128)(2,1)S(1)} async-done(((bf16[8,4,12,128]{3,1,2,0:T(4,128)(2,1)}), bf16[8,4,12,128]{3,1,2,0:T(4,128)(2,1)S(1)}, u32[]{:S(2)}, u32[]{:S(2)}) %all-to-all-start.2) | async-done | bytes 98336 | tf_op jit(solution)/shard_map/all_to_all | solution.py:170
  62.0 2.9 %convolution_bitcast_fusion = f32[8,12,2048]{2,0,1:T(8,128)} fusion(bf16[4,128,2048]{2,1,0:T(8,128)(2,1)} %param.16, bf16[8,4,12,128]{3,1,2,0:T(4,128)(2,1)S(1)} %all-to-all-done.2), kind=kOutput, calls=%fused_computation.10 | convolution fusion | flops 201326592 | bytes 2981888 | tf_op jit(solution)/shard_map/spnh,phd->snd/dot_general | solution.py:168
  64.9 1.8 %reshape_reshape.11 = f32[8,12,2,2,512]{4,3,2,0,1:T(2,128)S(1)} reshape(f32[8,12,2048]{2,0,1:T(8,128)} %convolution_bitcast_fusion) | data formatting | bytes 1572864 | tf_op jit(solution)/shard_map/reshape;reshape | solution.py:178
  66.7 1.5 %fusion.75 = (f32[8,12,2,1,512]{4,3,2,0,1:T(1,128)S(1)}, f32[8,12,2,1,512]{4,3,2,0,1:T(1,128)S(1)}, f32[8,12,2,1,512]{4,3,2,0,1:T(1,128)}) fusion(f32[8,12,2,2,512]{4,3,2,0,1:T(2,128)S(1)} %reshape_reshape.11, pred[]{:T(512)S(6)} %eq.77), kind=kLoop, calls=%fused_computation.118 | loop fusion | flops 98304 | bytes 1966081 | tf_op jit(solution)/shard_map/slice | solution.py:180
  68.5 1.7 %collective-permute-done = f32[8,12,2,512]{3,2,0,1:T(2,128)S(1)} collective-permute-done((f32[8,12,2,512]{3,2,0,1:T(2,128)S(1)}, f32[8,12,2,512]{3,2,0,1:T(2,128)S(1)}, u32[]{:S(2)}, u32[]{:S(2)}) %collective-permute-start) | collective-permute-done | bytes 393248 | tf_op jit(solution)/shard_map/ppermute | solution.py:182
  70.2 1.4 %fusion.34 = f32[8,12,1,2,512]{4,3,0,1,2:T(2,128)S(1)} fusion(f32[8,12,2,512]{3,2,0,1:T(2,128)S(1)} %collective-permute-done, f32[8,12,2,1,512]{4,3,2,0,1:T(1,128)} %get-tuple-element.9, f32[8,12,2,1,512]{4,3,2,0,1:T(1,128)S(1)} %get-tuple-element.7, pred[]{:T(512)S(6)} %eq.77), kind=kLoop, calls=%fused_computation.38 | loop fusion | flops 196608 | bytes 1572865 | tf_op jit(solution)/shard_map/reshape | solution.py:178
  72.1 1.6 %collective-permute-start.1 = (f32[8,12,1,512]{3,0,1,2:T(8,128)S(1)}, f32[8,12,1,512]{3,0,1,2:T(8,128)S(1)}, u32[]{:S(2)}, u32[]{:S(2)}) collective-permute-start(f32[8,12,1,512]{3,0,1,2:T(8,128)S(1)} %bitcast.149), channel_id=1, source_target_pairs={{0,2},{1,3},{2,0},{3,1},{4,6},{5,7},{6,4},{7,5},{8,10},{9,11},{10,... | collective-permute-start | bytes 589832 | tf_op jit(solution)/shard_map/ppermute | solution.py:182
  73.7 5.4 %collective-permute-done.1 = f32[8,12,1,512]{3,0,1,2:T(8,128)S(1)} collective-permute-done((f32[8,12,1,512]{3,0,1,2:T(8,128)S(1)}, f32[8,12,1,512]{3,0,1,2:T(8,128)S(1)}, u32[]{:S(2)}, u32[]{:S(2)}) %collective-permute-start.1) | collective-permute-done | bytes 196640 | tf_op jit(solution)/shard_map/ppermute | solution.py:182
  79.2 0.7 reshape.397
  79.9 3.4 %all-to-all-start.3 = ((f32[8,48,128]{2,1,0:T(8,128)}), f32[8,48,128]{2,1,0:T(8,128)S(1)}, u32[]{:S(2)}, u32[]{:S(2)}) async-start(f32[8,48,128]{2,1,0:T(8,128)} %reshape.397), calls=%async_computation.3 | async-start | bytes 393216 | tf_op jit(solution)/shard_map/all_to_all | solution.py:193
  83.5 7.5 %all-to-all-done.3 = f32[8,48,128]{2,1,0:T(8,128)S(1)} async-done(((f32[8,48,128]{2,1,0:T(8,128)}), f32[8,48,128]{2,1,0:T(8,128)S(1)}, u32[]{:S(2)}, u32[]{:S(2)}) %all-to-all-start.3) | async-done | bytes 196640 | tf_op jit(solution)/shard_map/all_to_all | solution.py:193
  91.1 0.8 fusion.23
  (65 shorter events, 7.0 us)
Async XLA Ops:
  0.0 24.0 %copy-start = (bf16[4,2048,128]{2,1,0:T(8,128)(2,1)S(1)}, bf16[4,2048,128]{2,1,0:T(8,128)(2,1)}, u32[]{:S(2)}) copy-start(bf16[4,2048,128]{2,1,0:T(8,128)(2,1)} %param.15) | copy-start | bytes 6291460
  0.0 15.0 %copy-start.1 = (s32[32]{0:T(128)S(1)}, s32[32]{0:T(128)}, u32[]{:S(2)}) copy-start(s32[32]{0:T(128)} %param.19) | copy-start | bytes 388
  5.1 18.9 %all-to-all-start = ((bf16[8,192,128]{2,1,0:T(8,128)(2,1)}), bf16[8,192,128]{2,1,0:T(8,128)(2,1)S(1)}, u32[]{:S(2)}, u32[]{:S(2)}) async-start(bf16[8,192,128]{2,1,0:T(8,128)(2,1)} %bitcast.5), calls=%async_computation | async-start | bytes 786432 | tf_op jit(solution)/shard_map/all_to_all | solution.py:80
  25.1 10.7 %all-to-all-start.1 = ((bf16[8,4,12,128]{3,1,2,0:T(4,128)(2,1)}), bf16[8,4,12,128]{3,1,2,0:T(4,128)(2,1)S(1)}, u32[]{:S(2)}, u32[]{:S(2)}) async-start(bf16[8,4,12,128]{3,1,2,0:T(4,128)(2,1)} %copy.130), calls=%async_computation.1 | async-start | bytes 196608 | tf_op jit(solution)/shard_map/all_to_all | solution.py:111
  51.5 10.4 %all-to-all-start.2 = ((bf16[8,4,12,128]{3,1,2,0:T(4,128)(2,1)}), bf16[8,4,12,128]{3,1,2,0:T(4,128)(2,1)S(1)}, u32[]{:S(2)}, u32[]{:S(2)}) async-start(bf16[8,4,12,128]{3,1,2,0:T(4,128)(2,1)} %bitcast.34), calls=%async_computation.2 | async-start | bytes 196608 | tf_op jit(solution)/shard_map/all_to_all | solution.py:170
  66.7 16.6 %copy-start.3 = (s32[32]{0:T(128)S(1)}, s32[32]{0:T(128)}, u32[]{:S(2)}) copy-start(s32[32]{0:T(128)} %param.23) | copy-start | bytes 388
  66.7 16.7 %copy-start.2 = (f32[32,2]{0,1:T(2,128)S(1)}, f32[32,2]{0,1:T(2,128)}, u32[]{:S(2)}) copy-start(f32[32,2]{0,1:T(2,128)} %param.22) | copy-start | bytes 772
  68.4 1.8 %collective-permute-start = (f32[8,12,2,512]{3,2,0,1:T(2,128)S(1)}, f32[8,12,2,512]{3,2,0,1:T(2,128)S(1)}, u32[]{:S(2)}, u32[]{:S(2)}) collective-permute-start(f32[8,12,2,512]{3,2,0,1:T(2,128)S(1)} %bitcast.145), channel_id=1, source_target_pairs={{0,1},{1,0},{2,3},{3,2},{4,5},{5,4},{6,7},{7,6},{8,9},{9,8},{10,11... | collective-permute-start | bytes 1179656 | tf_op jit(solution)/shard_map/ppermute | solution.py:182
  72.1 7.0 %collective-permute-start.1 = (f32[8,12,1,512]{3,0,1,2:T(8,128)S(1)}, f32[8,12,1,512]{3,0,1,2:T(8,128)S(1)}, u32[]{:S(2)}, u32[]{:S(2)}) collective-permute-start(f32[8,12,1,512]{3,0,1,2:T(8,128)S(1)} %bitcast.149), channel_id=1, source_target_pairs={{0,2},{1,3},{2,0},{3,1},{4,6},{5,7},{6,4},{7,5},{8,10},{9,11},{10,... | collective-permute-start | bytes 589832 | tf_op jit(solution)/shard_map/ppermute | solution.py:182
  79.9 11.1 %all-to-all-start.3 = ((f32[8,48,128]{2,1,0:T(8,128)}), f32[8,48,128]{2,1,0:T(8,128)S(1)}, u32[]{:S(2)}, u32[]{:S(2)}) async-start(f32[8,48,128]{2,1,0:T(8,128)} %reshape.397), calls=%async_computation.3 | async-start | bytes 393216 | tf_op jit(solution)/shard_map/all_to_all | solution.py:193

commit v10 on v7

--- a/solution.py
+++ b/solution.py
@@ -114,12 +114,19 @@
         .transpose(0, 2, 1, 3)
         .reshape(experts * capacity, heads_here, head_dim)
     )
-    raw_query = queries[target].reshape(row_count, choices_each, heads_here, head_dim)
-    query_rot = rotate(raw_query.astype(jnp.float32), cache_length[:, None, None]).astype(
+    page_slots = target.reshape(row_count, choices_each)[page_owner]
+    key_page = key_new[page_owner]
+    value_page = value_new[page_owner]
+    same_owner = (
+        page_taken[:, None] & page_taken[None, :] & (page_owner[:, None] == page_owner[None, :])
+    )
+    leader = jnp.any(local_ids[:, :1] == jnp.arange(pages_here)[None, :], axis=0)
+    leader_float = leader.astype(jnp.float32)[:, None, None]
+    page_raw = queries[page_slots]
+    page_queries = rotate(page_raw.astype(jnp.float32), page_limit[:, None, None]).astype(
         jnp.bfloat16
     )
     score_scale = 1.0 / head_dim**0.5
-    page_queries = query_rot[page_owner]
     head_eye = jnp.eye(heads_here, dtype=jnp.bfloat16)
     spread_queries = page_queries[:, :, :, None, :] * head_eye[None, None, :, :, None]
     scores = (
@@ -130,20 +137,20 @@
     )
     scores = jnp.where(in_range[:, None, None, :], scores, -jnp.inf)
     fresh_score = (
-        jnp.einsum("rkhd,rhd->rkh", query_rot, key_new, preferred_element_type=jnp.float32)
+        jnp.einsum("pkhd,phd->pkh", page_queries, key_page, preferred_element_type=jnp.float32)
         * score_scale
     )
     page_top = jnp.max(scores, axis=3)
-    owned_top = jnp.max(jnp.where(owned_pages[:, :, None, None], page_top[None], -jnp.inf), axis=1)
-    row_top = jnp.maximum(owned_top, fresh_score)
-    weights = jnp.exp(scores - row_top[page_owner][..., None])
+    owner_top = jnp.max(jnp.where(same_owner[:, :, None, None], page_top[None], -jnp.inf), axis=1)
+    row_top = jnp.maximum(owner_top, fresh_score)
+    weights = jnp.exp(scores - row_top[..., None])
     fresh_weight = jnp.exp(fresh_score - row_top)
     owned_float = owned_pages.astype(jnp.float32)
-    denominator = (
-        jnp.einsum(
-            "rp,pkh->rkh", owned_float, jnp.sum(weights, axis=3), precision=lax.Precision.HIGHEST
-        )
-        + fresh_weight
+    denominator = jnp.einsum(
+        "rp,pkh->rkh",
+        owned_float,
+        jnp.sum(weights, axis=3) + leader_float * fresh_weight,
+        precision=lax.Precision.HIGHEST,
     )
     weights_rounded = weights.astype(jnp.bfloat16)
     fresh_rounded = lax.optimization_barrier(fresh_weight.astype(jnp.bfloat16)).astype(jnp.float32)
@@ -151,10 +158,12 @@
         "pkjt,pthd->pkjhd", weights_rounded, cache_values, preferred_element_type=jnp.float32
     )
     page_context = jnp.sum(page_context * head_eye.astype(jnp.float32)[None, None, :, :, None], axis=3)
+    page_context = page_context + (leader_float * fresh_rounded)[..., None] * value_page.astype(
+        jnp.float32
+    )[:, None]
     accumulated = jnp.einsum(
         "rp,pkhd->rkhd", owned_float, page_context, precision=lax.Precision.HIGHEST
     )
-    accumulated = accumulated + fresh_rounded[..., None] * value_new.astype(jnp.float32)[:, None]
     context = (accumulated / denominator[..., None]).astype(jnp.bfloat16)
     context_flat = context.reshape(row_count * choices_each, heads_here * head_dim)
     context_buf = jnp.dot(select_rows, context_flat, preferred_element_type=jnp.float32).astype(

time: 88.4 us -> 87.7 us (level)
  other arithmetic: 6.79 us -> 5.51 us
  local copies, waits for them, and re-layouts: 7.51 us -> 8.75 us
    gather x3 -> x5, local copies, waits for them, and re-layouts: 2.01 us -> 2.73 us  [the longest x1 0.74 us: body(): page_raw = queries[page_slots]]
where the time goes in v10:
time: 87.7 us; the launch traced here: 87.1 us
  waiting for transfers between devices  31 us (35%)
  matrix products  18.5 us (21%)
  starting transfers between devices  13.5 us (15%)
  blocking collectives  9.51 us (11%)
  local copies, waits for them, and re-layouts  8.75 us (10%)
  other arithmetic  5.51 us (6%)
    all_to_all x1, waiting for transfers between devices, body(): lax.all_to_all(partial_far.reshape(groups * head_count, capacity * wblock...  20.5 us
    all_to_all x1, blocking collectives, body(): lax.all_to_all(context_buf, 'req', split_axis=0, concat_axis=0, tiled=True)  9.51 us
    all_to_all x1, starting transfers between devices, body(): lax.all_to_all(sendbuf, 'req', split_axis=0, concat_axis=0, tiled=True)  7.25 us
    all_to_all x1, waiting for transfers between devices, body(): lax.all_to_all(queries_far, 'req', split_axis=0, concat_axis=0, tiled=True)  7.03 us
    dot_general x1, matrix products, body(): jnp.einsum('pkjhd,pthd->pkjt', spread_queries, cache_keys, preferred_elem...  5.91 us
    dot_general x1, matrix products, body(): jnp.einsum('pkjt,pthd->pkjhd', weights_rounded, cache_values, preferred_e...  4.76 us
    all_to_all x1, starting transfers between devices, body(): lax.all_to_all(queries_far, 'req', split_axis=0, concat_axis=0, tiled=True)  3.62 us
    all_to_all x1, waiting for transfers between devices, body(): lax.all_to_all(sendbuf, 'req', split_axis=0, concat_axis=0, tiled=True)  3.47 us
  transfers between devices with their start and end apart: 3, of which 3 were waited for; matrix products, arithmetic and copies ran while one was open for 9% of the time, Pallas kernels for 0%

profile of v10, /device:TPU:0, one launch (start us, length us, event | category | flops | bytes accessed | tf_op | source)
XLA Modules:
  0.0 87.1 jit_solution(6575285269014037272)
XLA Ops:
  0.0 0.9 %copy.135 = s32[32,2]{1,0:T(8,128)S(1)} copy(s32[32,2]{0,1:T(2,128)} %param.21) | data formatting | bytes 512 | tf_op args[9]
  1.4 1.0 %fusion.32 = f32[32]{0:T(128)S(1)} fusion(bf16[32,2048]{1,0:T(8,128)(2,1)} %param.12), kind=kLoop, calls=%fused_computation.37 | loop fusion | flops 196576 | bytes 131200 | tf_op jit(solution)/shard_map/reduce_sum | solution.py:58
  2.5 1.0 %fusion.34 = bf16[32,2048]{1,0:T(8,128)(2,1)S(1)} fusion(bf16[32,2048]{1,0:T(8,128)(2,1)} %param.12, f32[2048]{0:T(1024)} %param.13, f32[32]{0:T(128)S(1)} %add_rsqrt_fusion), kind=kLoop, calls=%fused_computation.39 | loop fusion | flops 262144 | bytes 270464 | tf_op jit(solution)/shard_map/convert_element_type | solution.py:60
  3.8 0.4 convolution_convert_fusion
  4.2 0.9 %copy.138 = bf16[96,16,128]{2,1,0:T(8,128)(2,1)} copy(bf16[96,16,128]{2,0,1:T(8,128)(2,1)S(1)} %convolution_convert_fusion) | data formatting | bytes 786432 | tf_op jit(solution)/shard_map/convert_element_type | solution.py:73
  5.1 7.3 %all-to-all-start = ((bf16[8,192,128]{2,1,0:T(8,128)(2,1)}), bf16[8,192,128]{2,1,0:T(8,128)(2,1)S(1)}, u32[]{:S(2)}, u32[]{:S(2)}) async-start(bf16[8,192,128]{2,1,0:T(8,128)(2,1)} %bitcast.5), calls=%async_computation | async-start | bytes 786432 | tf_op jit(solution)/shard_map/all_to_all | solution.py:80
  12.5 3.0 %fusion.4 = f32[32,4,2,128]{3,0,2,1:T(8,128)S(1)} fusion(bf16[2048,4,2,128]{3,2,1,0:T(2,128)(2,1)} %param.14, bf16[32,2048]{1,0:T(8,128)(2,1)S(1)} %fusion.34), kind=kOutput, calls=%fused_computation.9 | convolution fusion | flops 134217728 | bytes 4456448 | tf_op jit(solution)/shard_map/rf,fhkd->rhkd/dot_general | solution.py:87
  15.7 0.4 fusion.30
  16.3 0.8 gather_fusion
  17.1 0.6 gather_fusion.1
  18.4 0.7 gather_fusion.3
  19.2 0.7 gather_fusion.4
  19.9 0.4 select_reduce_fusion
  20.6 3.5 %all-to-all-done = bf16[8,192,128]{2,1,0:T(8,128)(2,1)S(1)} async-done(((bf16[8,192,128]{2,1,0:T(8,128)(2,1)}), bf16[8,192,128]{2,1,0:T(8,128)(2,1)S(1)}, u32[]{:S(2)}, u32[]{:S(2)}) %all-to-all-start) | async-done | bytes 393248 | tf_op jit(solution)/shard_map/all_to_all | solution.py:80
  24.0 0.4 fusion.21
  24.5 0.7 copy.140
  25.1 3.6 %all-to-all-start.1 = ((bf16[8,4,12,128]{3,1,2,0:T(4,128)(2,1)}), bf16[8,4,12,128]{3,1,2,0:T(4,128)(2,1)S(1)}, u32[]{:S(2)}, u32[]{:S(2)}) async-start(bf16[8,4,12,128]{3,1,2,0:T(4,128)(2,1)} %copy.140), calls=%async_computation.1 | async-start | bytes 196608 | tf_op jit(solution)/shard_map/all_to_all | solution.py:111
  28.9 7.0 %all-to-all-done.1 = bf16[8,4,12,128]{3,1,2,0:T(4,128)(2,1)S(1)} async-done(((bf16[8,4,12,128]{3,1,2,0:T(4,128)(2,1)}), bf16[8,4,12,128]{3,1,2,0:T(4,128)(2,1)S(1)}, u32[]{:S(2)}, u32[]{:S(2)}) %all-to-all-start.1) | async-done | bytes 98336 | tf_op jit(solution)/shard_map/all_to_all | solution.py:111
  35.9 0.7 gather_fusion.2
  36.7 0.2 subtract_convert_fusion
  37.1 5.9 %fusion.67 = (f32[64,2,4]{2,1,0:T(2,128)S(1)}, f32[64,2,4,128]{3,2,1,0:T(4,128)S(1)}) fusion(bf16[64,128,4,128,1]{3,2,1,0,4:T(4,128)(2,1)} %bitcast.131, bf16[4,4]{0,1:T(4,128)(2,1)S(1)} %fusion.63, bf16[64,2,4,128]{3,2,1,0:T(4,128)(2,1)S(1)} %pad_maximum_fusion, pred[64,128]{1,0:T(8,128)(4,1)S(1)} %fusion.57), kind=kOutput, calls=%fused_computation.112 | convolution fusion | flops 68353536 | bytes 8792096 | tf_op jit(solution)/shard_map/pkjhd,pthd->pkjt/dot_general | solution.py:133
  43.1 0.4 fusion.47
  43.9 0.4 fusion.39
  44.7 4.8 %fusion.11 = f32[64,2,4,128]{3,2,1,0:T(4,128)S(1)} fusion(bf16[64,128,4,128,1]{3,2,1,0,4:T(4,128)(2,1)} %bitcast.132, f32[4,4]{0,1:T(4,128)S(1)} %fusion.66, f32[64,2,4,128]{3,2,1,0:T(4,128)S(1)} %get-tuple-element.18, f32[64,2,4]{2,1,0:T(2,128)S(1)} %copy.148), kind=kOutput, calls=%fused_computation.15 | convolution fusion | flops 67698688 | bytes 8915008 | tf_op jit(solution)/shard_map/pkjt,pthd->pkjhd/dot_general | solution.py:157
  49.7 0.3 fusion.22
  50.0 0.3 convolution_convert_fusion.1
  50.3 9.5 %all_to_all.20 = bf16[8,4,12,128]{3,1,2,0:T(4,128)(2,1)S(1)} all-to-all(bf16[8,4,12,128]{3,1,2,0:T(4,128)(2,1)S(1)} %bitcast.126), channel_id=1, replica_groups=mesh['req'=8,'head'=4] {'req'}, dimensions={0} | all-to-all | bytes 196608 | tf_op jit(solution)/shard_map/all_to_all | solution.py:179
  59.8 2.1 %fusion.6 = f32[8,12,2048,1]{2,0,3,1:T(8,128)S(1)} fusion(bf16[4,128,2048]{2,1,0:T(8,128)(2,1)} %param.16, bf16[8,4,12,128]{3,1,2,0:T(4,128)(2,1)S(1)} %all_to_all.20), kind=kOutput, calls=%fused_computation.11 | convolution fusion | flops 201326592 | bytes 2981888 | tf_op jit(solution)/shard_map/spnh,phd->snd/dot_general | solution.py:177
  61.9 1.1 %copy.157 = f32[8,4,12,4,128]{4,3,2,1,0:T(4,128)} copy(f32[8,4,12,4,128]{4,0,3,1,2:T(8,128)S(1)} %bitcast.121) | data formatting | bytes 1572864 | tf_op jit(solution)/shard_map/transpose | solution.py:183
  63.0 2.6 %all-to-all-start.3 = ((f32[32,48,128]{2,1,0:T(8,128)}), f32[32,48,128]{2,1,0:T(8,128)S(1)}, u32[]{:S(2)}, u32[]{:S(2)}) async-start(f32[32,48,128]{2,1,0:T(8,128)} %bitcast.38), calls=%async_computation.3 | async-start | bytes 1572864 | tf_op jit(solution)/shard_map/all_to_all | solution.py:194
  65.8 20.5 %all-to-all-done.3 = f32[32,48,128]{2,1,0:T(8,128)S(1)} async-done(((f32[32,48,128]{2,1,0:T(8,128)}), f32[32,48,128]{2,1,0:T(8,128)S(1)}, u32[]{:S(2)}, u32[]{:S(2)}) %all-to-all-start.3) | async-done | bytes 786464 | tf_op jit(solution)/shard_map/all_to_all | solution.py:194
  86.3 0.8 fusion.23
  (72 shorter events, 3.9 us)
Async XLA Ops:
  0.0 24.0 %copy-start = (bf16[4,2048,128]{2,1,0:T(8,128)(2,1)S(1)}, bf16[4,2048,128]{2,1,0:T(8,128)(2,1)}, u32[]{:S(2)}) copy-start(bf16[4,2048,128]{2,1,0:T(8,128)(2,1)} %param.15) | copy-start | bytes 6291460
  1.1 14.4 %copy-start.1 = (s32[32]{0:T(128)S(1)}, s32[32]{0:T(128)}, u32[]{:S(2)}) copy-start(s32[32]{0:T(128)} %param.19) | copy-start | bytes 388
  1.2 14.4 %copy-start.2 = (s32[32,32]{1,0:T(8,128)S(1)}, s32[32,32]{1,0:T(8,128)}, u32[]{:S(2)}) copy-start(s32[32,32]{1,0:T(8,128)} %param.20) | copy-start | bytes 12292
  1.4 14.8 %copy-start.3 = (s32[32,2]{0,1:T(2,128)S(1)}, s32[32,2]{0,1:T(2,128)}, u32[]{:S(2)}) copy-start(s32[32,2]{0,1:T(2,128)} %param.21) | copy-start | bytes 772
  5.1 18.9 %all-to-all-start = ((bf16[8,192,128]{2,1,0:T(8,128)(2,1)}), bf16[8,192,128]{2,1,0:T(8,128)(2,1)S(1)}, u32[]{:S(2)}, u32[]{:S(2)}) async-start(bf16[8,192,128]{2,1,0:T(8,128)(2,1)} %bitcast.5), calls=%async_computation | async-start | bytes 786432 | tf_op jit(solution)/shard_map/all_to_all | solution.py:80
  25.1 10.7 %all-to-all-start.1 = ((bf16[8,4,12,128]{3,1,2,0:T(4,128)(2,1)}), bf16[8,4,12,128]{3,1,2,0:T(4,128)(2,1)S(1)}, u32[]{:S(2)}, u32[]{:S(2)}) async-start(bf16[8,4,12,128]{3,1,2,0:T(4,128)(2,1)} %copy.140), calls=%async_computation.1 | async-start | bytes 196608 | tf_op jit(solution)/shard_map/all_to_all | solution.py:111
  59.8 5.8 %copy-start.5 = (s32[32]{0:T(128)S(1)}, s32[32]{0:T(128)}, u32[]{:S(2)}) copy-start(s32[32]{0:T(128)} %param.23) | copy-start | bytes 388
  59.8 5.8 %copy-start.4 = (f32[32,2]{0,1:T(2,128)S(1)}, f32[32,2]{0,1:T(2,128)}, u32[]{:S(2)}) copy-start(f32[32,2]{0,1:T(2,128)} %param.22) | copy-start | bytes 772
  63.0 23.2 %all-to-all-start.3 = ((f32[32,48,128]{2,1,0:T(8,128)}), f32[32,48,128]{2,1,0:T(8,128)S(1)}, u32[]{:S(2)}, u32[]{:S(2)}) async-start(f32[32,48,128]{2,1,0:T(8,128)} %bitcast.38), calls=%async_computation.3 | async-start | bytes 1572864 | tf_op jit(solution)/shard_map/all_to_all | solution.py:194

commit v11 on v10

--- a/solution.py
+++ b/solution.py
@@ -174,10 +174,10 @@
     head_count = lax.axis_size("head")
     width_here = model_width // head_count
     wblocks = width_here // lanes
-    partial_far = jnp.einsum(
-        "spnh,phd->snd",
-        lax.all_to_all(context_buf, "req", split_axis=0, concat_axis=0, tiled=True),
-        output_weight,
+    context_far = lax.all_to_all(context_buf, "req", split_axis=0, concat_axis=0, tiled=True)
+    partial_far = jnp.dot(
+        context_far.transpose(0, 2, 1, 3).reshape(groups * capacity, pairs_here * head_dim),
+        output_weight.reshape(pairs_here * head_dim, model_width),
         preferred_element_type=jnp.float32,
     )
     partial_far = partial_far.reshape(groups, capacity, head_count, wblocks, lanes).transpose(

time: 87.7 us -> 90.1 us (1.027)
  blocking collectives: 9.51 us -> 0 us
  local copies, waits for them, and re-layouts: 8.75 us -> 13.5 us
  starting transfers between devices: 13.5 us -> 17.1 us
  waiting for transfers between devices: 31 us -> 34.1 us
    all_to_all x1 -> x0, blocking collectives: 9.51 us -> none  [body(): lax.all_to_all(context_buf, 'req', split_axis=0, concat_axis=0, tiled=True)]
    dot_general x0 -> x1, local copies, waits for them, and re-layouts: none -> 3.94 us  [body(): jnp.dot(context_far.transpose(0, 2, 1, 3).reshape(groups * capacity, pair...]
    all_to_all x0 -> x1, starting transfers between devices: none -> 3.36 us  [body(): lax.all_to_all(context_buf, 'req', split_axis=0, concat_axis=0, tiled=True)]
    all_to_all x0 -> x1, waiting for transfers between devices: none -> 3.11 us  [body(): lax.all_to_all(context_buf, 'req', split_axis=0, concat_axis=0, tiled=True)]
  transfers between devices with their start and end apart: 3 -> 4, of which waited for: 3 -> 4; matrix products, arithmetic and copies ran while one was open for 9% -> 14% of each run, Pallas kernels for 0% -> 0%
where the time goes in v11:
time: 90.1 us; the launch traced here: 89.4 us
  waiting for transfers between devices  34.1 us (38%)
  matrix products  18.8 us (21%)
  starting transfers between devices  17.1 us (19%)
  local copies, waits for them, and re-layouts  13.5 us (15%)
  other arithmetic  5.51 us (6%)
    all_to_all x1, waiting for transfers between devices, body(): lax.all_to_all(partial_far.reshape(groups * head_count, capacity * wblock...  20.5 us
    all_to_all x1, starting transfers between devices, body(): lax.all_to_all(sendbuf, 'req', split_axis=0, concat_axis=0, tiled=True)  7.25 us
    all_to_all x1, waiting for transfers between devices, body(): lax.all_to_all(queries_far, 'req', split_axis=0, concat_axis=0, tiled=True)  7.03 us
    dot_general x1, matrix products, body(): jnp.einsum('pkjhd,pthd->pkjt', spread_queries, cache_keys, preferred_elem...  5.91 us
    dot_general x1, matrix products, body(): jnp.einsum('pkjt,pthd->pkjhd', weights_rounded, cache_values, preferred_e...  4.76 us
    dot_general x1, local copies, waits for them, and re-layouts, body(): jnp.dot(context_far.transpose(0, 2, 1, 3).reshape(groups * capacity, pair...  3.94 us
    all_to_all x1, starting transfers between devices, body(): lax.all_to_all(queries_far, 'req', split_axis=0, concat_axis=0, tiled=True)  3.62 us
    all_to_all x1, waiting for transfers between devices, body(): lax.all_to_all(sendbuf, 'req', split_axis=0, concat_axis=0, tiled=True)  3.48 us
  transfers between devices with their start and end apart: 4, of which 4 were waited for; matrix products, arithmetic and copies ran while one was open for 14% of the time, Pallas kernels for 0%

profile of v11, /device:TPU:0, one launch (start us, length us, event | category | flops | bytes accessed | tf_op | source)
XLA Modules:
  0.0 89.4 jit_solution(15724642887797323351)
XLA Ops:
  0.0 0.9 %copy.140 = s32[32,2]{1,0:T(8,128)S(1)} copy(s32[32,2]{0,1:T(2,128)} %param.21) | data formatting | bytes 512 | tf_op args[9]
  1.4 1.0 %fusion.30 = f32[32]{0:T(128)S(1)} fusion(bf16[32,2048]{1,0:T(8,128)(2,1)} %param.12), kind=kLoop, calls=%fused_computation.36 | loop fusion | flops 196576 | bytes 131200 | tf_op jit(solution)/shard_map/reduce_sum | solution.py:58
  2.5 1.0 %fusion.32 = bf16[32,2048]{1,0:T(8,128)(2,1)S(1)} fusion(bf16[32,2048]{1,0:T(8,128)(2,1)} %param.12, f32[2048]{0:T(1024)} %param.13, f32[32]{0:T(128)S(1)} %add_rsqrt_fusion), kind=kLoop, calls=%fused_computation.38 | loop fusion | flops 262144 | bytes 270464 | tf_op jit(solution)/shard_map/convert_element_type | solution.py:60
  3.8 0.4 convolution_convert_fusion
  4.2 0.9 copy.143
  5.1 7.3 %all-to-all-start = ((bf16[8,192,128]{2,1,0:T(8,128)(2,1)}), bf16[8,192,128]{2,1,0:T(8,128)(2,1)S(1)}, u32[]{:S(2)}, u32[]{:S(2)}) async-start(bf16[8,192,128]{2,1,0:T(8,128)(2,1)} %bitcast.5), calls=%async_computation | async-start | bytes 786432 | tf_op jit(solution)/shard_map/all_to_all | solution.py:80
  12.5 3.0 %fusion.4 = f32[32,4,2,128]{3,0,2,1:T(8,128)S(1)} fusion(bf16[2048,4,2,128]{3,2,1,0:T(2,128)(2,1)} %param.14, bf16[32,2048]{1,0:T(8,128)(2,1)S(1)} %fusion.32), kind=kOutput, calls=%fused_computation.9 | convolution fusion | flops 134217728 | bytes 4456448 | tf_op jit(solution)/shard_map/rf,fhkd->rhkd/dot_general | solution.py:87
  15.7 0.4 fusion.28
  16.3 0.8 gather_fusion
  17.1 0.6 gather_fusion.1
  18.4 0.7 gather_fusion.3
  19.2 0.7 gather_fusion.4
  19.9 0.4 select_reduce_fusion
  20.5 3.5 %all-to-all-done = bf16[8,192,128]{2,1,0:T(8,128)(2,1)S(1)} async-done(((bf16[8,192,128]{2,1,0:T(8,128)(2,1)}), bf16[8,192,128]{2,1,0:T(8,128)(2,1)S(1)}, u32[]{:S(2)}, u32[]{:S(2)}) %all-to-all-start) | async-done | bytes 393248 | tf_op jit(solution)/shard_map/all_to_all | solution.py:80
  24.0 0.4 fusion.19
  24.5 0.7 copy.145
  25.1 3.6 %all-to-all-start.1 = ((bf16[8,4,12,128]{3,1,2,0:T(4,128)(2,1)}), bf16[8,4,12,128]{3,1,2,0:T(4,128)(2,1)S(1)}, u32[]{:S(2)}, u32[]{:S(2)}) async-start(bf16[8,4,12,128]{3,1,2,0:T(4,128)(2,1)} %copy.145), calls=%async_computation.1 | async-start | bytes 196608 | tf_op jit(solution)/shard_map/all_to_all | solution.py:111
  28.9 7.0 %all-to-all-done.1 = bf16[8,4,12,128]{3,1,2,0:T(4,128)(2,1)S(1)} async-done(((bf16[8,4,12,128]{3,1,2,0:T(4,128)(2,1)}), bf16[8,4,12,128]{3,1,2,0:T(4,128)(2,1)S(1)}, u32[]{:S(2)}, u32[]{:S(2)}) %all-to-all-start.1) | async-done | bytes 98336 | tf_op jit(solution)/shard_map/all_to_all | solution.py:111
  35.9 0.7 gather_fusion.2
  37.1 5.9 %fusion.65 = (f32[64,2,4]{2,1,0:T(2,128)S(1)}, f32[64,2,4,128]{3,2,1,0:T(4,128)S(1)}) fusion(bf16[64,128,4,128,1]{3,2,1,0,4:T(4,128)(2,1)} %bitcast.140, bf16[4,4]{0,1:T(4,128)(2,1)S(1)} %fusion.61, bf16[64,2,4,128]{3,2,1,0:T(4,128)(2,1)S(1)} %pad_maximum_fusion, pred[64,128]{1,0:T(8,128)(4,1)S(1)} %fusion.55), kind=kOutput, calls=%fused_computation.112 | convolution fusion | flops 68353536 | bytes 8792096 | tf_op jit(solution)/shard_map/pkjhd,pthd->pkjt/dot_general | solution.py:133
  43.1 0.4 fusion.46
  43.9 0.4 fusion.37
  44.7 4.8 %fusion.9 = f32[64,2,4,128]{3,2,1,0:T(4,128)S(1)} fusion(bf16[64,128,4,128,1]{3,2,1,0,4:T(4,128)(2,1)} %bitcast.141, f32[4,4]{0,1:T(4,128)S(1)} %fusion.64, f32[64,2,4,128]{3,2,1,0:T(4,128)S(1)} %get-tuple-element.18, f32[64,2,4]{2,1,0:T(2,128)S(1)} %copy.153), kind=kOutput, calls=%fused_computation.14 | convolution fusion | flops 67698688 | bytes 8915008 | tf_op jit(solution)/shard_map/pkjt,pthd->pkjhd/dot_general | solution.py:157
  50.3 0.7 reshape.406
  51.0 3.4 %all-to-all-start.2 = ((bf16[8,4,12,128]{3,1,2,0:T(4,128)(2,1)}), bf16[8,4,12,128]{3,1,2,0:T(4,128)(2,1)S(1)}, u32[]{:S(2)}, u32[]{:S(2)}) async-start(bf16[8,4,12,128]{3,1,2,0:T(4,128)(2,1)} %bitcast.33), calls=%async_computation.2 | async-start | bytes 196608 | tf_op jit(solution)/shard_map/all_to_all | solution.py:177
  54.3 3.9 %copy.161 = bf16[2048,512]{1,0:T(8,128)(2,1)} copy(bf16[2048,512]{0,1:T(8,128)(2,1)} %bitcast.130) | data formatting | bytes 4194304 | tf_op jit(solution)/shard_map/dot_general | solution.py:178
  58.3 3.1 %all-to-all-done.2 = bf16[8,4,12,128]{3,1,2,0:T(4,128)(2,1)S(1)} async-done(((bf16[8,4,12,128]{3,1,2,0:T(4,128)(2,1)}), bf16[8,4,12,128]{3,1,2,0:T(4,128)(2,1)S(1)}, u32[]{:S(2)}, u32[]{:S(2)}) %all-to-all-start.2) | async-done | bytes 98336 | tf_op jit(solution)/shard_map/all_to_all | solution.py:177
  61.4 2.4 %convolution_bitcast_fusion = f32[8,4,12,4,128]{4,2,3,1,0:T(8,128)S(1)} fusion(bf16[4,4,128,512,1]{3,2,1,0,4:T(8,128)(2,1)} %bitcast.129, bf16[8,12,512,1,1]{2,0,1,4,3:T(8,128)(2,1)S(1)} %bitcast.132), kind=kOutput, calls=%fused_computation.11 | convolution fusion | flops 201326592 | bytes 2981888 | tf_op jit(solution)/shard_map/dot_general | solution.py:178
  63.8 1.2 %copy.163 = f32[8,4,12,4,128]{4,3,2,1,0:T(4,128)} copy(f32[8,4,12,4,128]{4,2,3,1,0:T(8,128)S(1)} %convolution_bitcast_fusion) | data formatting | bytes 1572864 | tf_op jit(solution)/shard_map/transpose | solution.py:183
  65.0 2.9 %all-to-all-start.3 = ((f32[32,48,128]{2,1,0:T(8,128)}), f32[32,48,128]{2,1,0:T(8,128)S(1)}, u32[]{:S(2)}, u32[]{:S(2)}) async-start(f32[32,48,128]{2,1,0:T(8,128)} %bitcast.42), calls=%async_computation.3 | async-start | bytes 1572864 | tf_op jit(solution)/shard_map/all_to_all | solution.py:194
  68.0 20.5 %all-to-all-done.3 = f32[32,48,128]{2,1,0:T(8,128)S(1)} async-done(((f32[32,48,128]{2,1,0:T(8,128)}), f32[32,48,128]{2,1,0:T(8,128)S(1)}, u32[]{:S(2)}, u32[]{:S(2)}) %all-to-all-start.3) | async-done | bytes 786464 | tf_op jit(solution)/shard_map/all_to_all | solution.py:194
  88.6 0.8 fusion.21
  (75 shorter events, 4.7 us)
Async XLA Ops:
  0.0 24.0 %copy-start = (bf16[4,2048,128]{2,1,0:T(8,128)(2,1)S(1)}, bf16[4,2048,128]{2,1,0:T(8,128)(2,1)}, u32[]{:S(2)}) copy-start(bf16[4,2048,128]{2,1,0:T(8,128)(2,1)} %param.15) | copy-start | bytes 6291460
  1.1 14.4 %copy-start.1 = (s32[32]{0:T(128)S(1)}, s32[32]{0:T(128)}, u32[]{:S(2)}) copy-start(s32[32]{0:T(128)} %param.19) | copy-start | bytes 388
  1.2 14.4 %copy-start.2 = (s32[32,32]{1,0:T(8,128)S(1)}, s32[32,32]{1,0:T(8,128)}, u32[]{:S(2)}) copy-start(s32[32,32]{1,0:T(8,128)} %param.20) | copy-start | bytes 12292
  1.4 14.8 %copy-start.3 = (s32[32,2]{0,1:T(2,128)S(1)}, s32[32,2]{0,1:T(2,128)}, u32[]{:S(2)}) copy-start(s32[32,2]{0,1:T(2,128)} %param.21) | copy-start | bytes 772
  5.1 18.9 %all-to-all-start = ((bf16[8,192,128]{2,1,0:T(8,128)(2,1)}), bf16[8,192,128]{2,1,0:T(8,128)(2,1)S(1)}, u32[]{:S(2)}, u32[]{:S(2)}) async-start(bf16[8,192,128]{2,1,0:T(8,128)(2,1)} %bitcast.5), calls=%async_computation | async-start | bytes 786432 | tf_op jit(solution)/shard_map/all_to_all | solution.py:80
  25.1 10.7 %all-to-all-start.1 = ((bf16[8,4,12,128]{3,1,2,0:T(4,128)(2,1)}), bf16[8,4,12,128]{3,1,2,0:T(4,128)(2,1)S(1)}, u32[]{:S(2)}, u32[]{:S(2)}) async-start(bf16[8,4,12,128]{3,1,2,0:T(4,128)(2,1)} %copy.145), calls=%async_computation.1 | async-start | bytes 196608 | tf_op jit(solution)/shard_map/all_to_all | solution.py:111
  51.0 10.4 %all-to-all-start.2 = ((bf16[8,4,12,128]{3,1,2,0:T(4,128)(2,1)}), bf16[8,4,12,128]{3,1,2,0:T(4,128)(2,1)S(1)}, u32[]{:S(2)}, u32[]{:S(2)}) async-start(bf16[8,4,12,128]{3,1,2,0:T(4,128)(2,1)} %bitcast.33), calls=%async_computation.2 | async-start | bytes 196608 | tf_op jit(solution)/shard_map/all_to_all | solution.py:177
  58.3 9.6 %copy-start.5 = (s32[32]{0:T(128)S(1)}, s32[32]{0:T(128)}, u32[]{:S(2)}) copy-start(s32[32]{0:T(128)} %param.23) | copy-start | bytes 388
  58.3 9.6 %copy-start.4 = (f32[32,2]{0,1:T(2,128)S(1)}, f32[32,2]{0,1:T(2,128)}, u32[]{:S(2)}) copy-start(f32[32,2]{0,1:T(2,128)} %param.22) | copy-start | bytes 772
  65.0 23.5 %all-to-all-start.3 = ((f32[32,48,128]{2,1,0:T(8,128)}), f32[32,48,128]{2,1,0:T(8,128)S(1)}, u32[]{:S(2)}, u32[]{:S(2)}) async-start(f32[32,48,128]{2,1,0:T(8,128)} %bitcast.42), calls=%async_computation.3 | async-start | bytes 1572864 | tf_op jit(solution)/shard_map/all_to_all | solution.py:194

commit v12 on v10

--- a/solution.py
+++ b/solution.py
@@ -53,11 +53,8 @@
     experts = AEXP
     capacity = CAP
     as_float = tokens.astype(jnp.float32)
-    normed = (
-        as_float
-        * lax.rsqrt(jnp.mean(as_float * as_float, axis=-1, keepdims=True) + eps)
-        * norm_gain
-    ).astype(jnp.bfloat16)
+    row_scale = lax.rsqrt(jnp.mean(as_float * as_float, axis=-1, keepdims=True) + eps)
+    normed = (as_float * row_scale * norm_gain).astype(jnp.bfloat16)
     flat_expert = expert_choice.reshape(-1)
     onehot = (flat_expert[:, None] == jnp.arange(experts)[None, :]).astype(jnp.int32)
     before = jnp.cumsum(onehot, axis=0) - onehot
@@ -67,9 +64,14 @@
     select_rows = select.astype(jnp.bfloat16)
     lanes = 128
     blocks = model_width // lanes
-    repeated = jnp.repeat(normed, choices_each, axis=0).reshape(-1, blocks, lanes)
-    sendbuf = jnp.einsum(
-        "mr,rab->mab", select_rows, repeated, preferred_element_type=jnp.float32
+    repeated = jnp.repeat(tokens, choices_each, axis=0).reshape(-1, blocks, lanes)
+    picked = jnp.einsum("mr,rab->mab", select_rows, repeated, preferred_element_type=jnp.float32)
+    slot_scale = jnp.sum(
+        jnp.where(select, jnp.repeat(row_scale[:, 0], choices_each)[None, :], jnp.float32(0.0)),
+        axis=1,
+    )
+    sendbuf = (
+        picked * slot_scale[:, None, None] * norm_gain.reshape(blocks, lanes)[None]
     ).astype(jnp.bfloat16)
     replicas = groups // experts
     sendbuf = jnp.broadcast_to(

time: 87.7 us -> 88.7 us (1.011)
  local copies, waits for them, and re-layouts: 8.75 us -> 9.85 us
  other arithmetic: 5.51 us -> 4.58 us
  matrix products: 18.5 us -> 19.4 us
    broadcast_in_dim x1 -> x3, local copies, waits for them, and re-layouts: 0.15 us -> 1.25 us  [the longest x1 1.06 us: body(): jnp.repeat(tokens, choices_each, axis=0).reshape(-1, blocks, lanes)]
    convert_element_type x1 -> x0, other arithmetic: 1.01 us -> none  [body(): normed = (as_float * lax.rsqrt(jnp.mean(as_float * as_float, axis=-1, kee...]
  transfers between devices with their start and end apart: 3 -> 3, of which waited for: 3 -> 3; matrix products, arithmetic and copies ran while one was open for 9% -> 10% of each run, Pallas kernels for 0% -> 0%
where the time goes in v12:
time: 88.7 us; the launch traced here: 88 us
  waiting for transfers between devices  30.8 us (35%)
  matrix products  19.4 us (22%)
  starting transfers between devices  13.5 us (15%)
  local copies, waits for them, and re-layouts  9.85 us (11%)
  blocking collectives  9.51 us (11%)
  other arithmetic  4.58 us (5%)
    all_to_all x1, waiting for transfers between devices, body(): lax.all_to_all(partial_far.reshape(groups * head_count, capacity * wblock...  20.5 us
    all_to_all x1, blocking collectives, body(): lax.all_to_all(context_buf, 'req', split_axis=0, concat_axis=0, tiled=True)  9.51 us
    all_to_all x1, starting transfers between devices, body(): lax.all_to_all(sendbuf, 'req', split_axis=0, concat_axis=0, tiled=True)  7.25 us
    all_to_all x1, waiting for transfers between devices, body(): lax.all_to_all(queries_far, 'req', split_axis=0, concat_axis=0, tiled=True)  7.03 us
    dot_general x1, matrix products, body(): jnp.einsum('pkjhd,pthd->pkjt', spread_queries, cache_keys, preferred_elem...  5.93 us
    dot_general x1, matrix products, body(): jnp.einsum('pkjt,pthd->pkjhd', weights_rounded, cache_values, preferred_e...  4.76 us
    all_to_all x1, starting transfers between devices, body(): lax.all_to_all(queries_far, 'req', split_axis=0, concat_axis=0, tiled=True)  3.62 us
    all_to_all x1, waiting for transfers between devices, body(): lax.all_to_all(sendbuf, 'req', split_axis=0, concat_axis=0, tiled=True)  3.34 us
  transfers between devices with their start and end apart: 3, of which 3 were waited for; matrix products, arithmetic and copies ran while one was open for 10% of the time, Pallas kernels for 0%

profile of v12, /device:TPU:0, one launch (start us, length us, event | category | flops | bytes accessed | tf_op | source)
XLA Modules:
  0.0 88.0 jit_solution(12951181122922911469)
XLA Ops:
  0.0 0.9 %copy.135 = s32[32,2]{1,0:T(8,128)S(1)} copy(s32[32,2]{0,1:T(2,128)} %param.21) | data formatting | bytes 512 | tf_op args[9]
  1.4 1.0 %fusion.34 = f32[32]{0:T(128)S(1)} fusion(bf16[32,2048]{1,0:T(8,128)(2,1)} %param.12), kind=kLoop, calls=%fused_computation.39 | loop fusion | flops 196576 | bytes 131200 | tf_op jit(solution)/shard_map/reduce_sum | solution.py:56
  2.7 1.1 %broadcast_in_dim.50 = bf16[32,2,2048]{2,1,0:T(2,128)(2,1)S(1)} broadcast(bf16[32,2048]{1,0:T(8,128)(2,1)} %param.12), dimensions={0,2} | broadcast | bytes 393216 | tf_op jit(solution)/shard_map/broadcast_in_dim | solution.py:67
  4.0 1.1 %fusion.9 = bf16[96,16,128]{2,0,1:T(8,128)(2,1)S(1)} fusion(f32[16,128]{1,0:T(8,128)} %bitcast.134, f32[96]{0:T(128)S(1)} %select_reduce_fusion.2, bf16[64,16,128]{2,1,0:T(8,128)(2,1)S(1)} %reshape_reshape.6, s32[64]{0:T(128)S(1)} %multiply_add_fusion.3), kind=kOutput, calls=%fused_computation.15 | convolution fusion | flops 25761792 | bytes 664192 | tf_op jit(solution)/shard_map/mr,rab->mab/dot_general | solution.py:68
  5.1 0.9 %copy.138 = bf16[96,16,128]{2,1,0:T(8,128)(2,1)} copy(bf16[96,16,128]{2,0,1:T(8,128)(2,1)S(1)} %fusion.9) | data formatting | bytes 786432 | tf_op jit(solution)/shard_map/convert_element_type | solution.py:75
  6.0 7.3 %all-to-all-start = ((bf16[8,192,128]{2,1,0:T(8,128)(2,1)}), bf16[8,192,128]{2,1,0:T(8,128)(2,1)S(1)}, u32[]{:S(2)}, u32[]{:S(2)}) async-start(bf16[8,192,128]{2,1,0:T(8,128)(2,1)} %bitcast.6), calls=%async_computation | async-start | bytes 786432 | tf_op jit(solution)/shard_map/all_to_all | solution.py:82
  13.4 3.2 %fusion.4 = f32[32,4,2,128]{3,0,2,1:T(8,128)S(1)} fusion(bf16[2048,4,2,128]{3,2,1,0:T(2,128)(2,1)} %param.14, bf16[32,2048]{1,0:T(8,128)(2,1)} %param.12, f32[2048]{0:T(1024)} %param.13, f32[32]{0:T(128)S(1)} %add_rsqrt_fusion), kind=kOutput, calls=%fused_computation.9 | convolution fusion | flops 134479872 | bytes 4464768 | tf_op jit(solution)/shard_map/rf,fhkd->rhkd/dot_general | solution.py:89
  16.8 0.4 fusion.32
  17.4 0.8 gather_fusion
  18.1 0.6 gather_fusion.1
  19.4 0.7 gather_fusion.3
  20.2 0.7 gather_fusion.4
  20.9 0.4 select_reduce_fusion
  21.6 3.3 %all-to-all-done = bf16[8,192,128]{2,1,0:T(8,128)(2,1)S(1)} async-done(((bf16[8,192,128]{2,1,0:T(8,128)(2,1)}), bf16[8,192,128]{2,1,0:T(8,128)(2,1)S(1)}, u32[]{:S(2)}, u32[]{:S(2)}) %all-to-all-start) | async-done | bytes 393248 | tf_op jit(solution)/shard_map/all_to_all | solution.py:82
  24.9 0.4 fusion.23
  25.4 0.7 copy.140
  26.0 3.6 %all-to-all-start.1 = ((bf16[8,4,12,128]{3,1,2,0:T(4,128)(2,1)}), bf16[8,4,12,128]{3,1,2,0:T(4,128)(2,1)S(1)}, u32[]{:S(2)}, u32[]{:S(2)}) async-start(bf16[8,4,12,128]{3,1,2,0:T(4,128)(2,1)} %copy.140), calls=%async_computation.1 | async-start | bytes 196608 | tf_op jit(solution)/shard_map/all_to_all | solution.py:113
  29.7 7.0 %all-to-all-done.1 = bf16[8,4,12,128]{3,1,2,0:T(4,128)(2,1)S(1)} async-done(((bf16[8,4,12,128]{3,1,2,0:T(4,128)(2,1)}), bf16[8,4,12,128]{3,1,2,0:T(4,128)(2,1)S(1)}, u32[]{:S(2)}, u32[]{:S(2)}) %all-to-all-start.1) | async-done | bytes 98336 | tf_op jit(solution)/shard_map/all_to_all | solution.py:113
  36.8 0.7 gather_fusion.2
  37.6 0.2 subtract_convert_fusion
  38.0 0.4 fusion.52
  38.5 5.9 %fusion.72 = (f32[64,2,4]{2,1,0:T(2,128)S(1)}, f32[64,2,4,128]{3,2,1,0:T(4,128)S(1)}) fusion(bf16[64,128,4,128,1]{3,2,1,0,4:T(4,128)(2,1)} %bitcast.132, bf16[4,4]{0,1:T(4,128)(2,1)S(1)} %fusion.68, bf16[64,2,4,128]{3,2,1,0:T(4,128)(2,1)S(1)} %pad_maximum_fusion, pred[64,128]{1,0:T(8,128)(4,1)S(1)} %fusion.62), kind=kOutput, calls=%fused_computation.117 | convolution fusion | flops 68353536 | bytes 8792096 | tf_op jit(solution)/shard_map/pkjhd,pthd->pkjt/dot_general | solution.py:135
  44.8 0.4 fusion.41
  45.6 4.8 %fusion.13 = f32[64,2,4,128]{3,2,1,0:T(4,128)S(1)} fusion(bf16[64,128,4,128,1]{3,2,1,0,4:T(4,128)(2,1)} %bitcast.133, f32[4,4]{0,1:T(4,128)S(1)} %fusion.71, f32[64,2,4,128]{3,2,1,0:T(4,128)S(1)} %get-tuple-element.18, f32[64,2,4]{2,1,0:T(2,128)S(1)} %copy.148), kind=kOutput, calls=%fused_computation.17 | convolution fusion | flops 67698688 | bytes 8915008 | tf_op jit(solution)/shard_map/pkjt,pthd->pkjhd/dot_general | solution.py:159
  50.6 0.3 fusion.24
  50.9 0.3 convolution_convert_fusion
  51.2 9.5 %all_to_all.20 = bf16[8,4,12,128]{3,1,2,0:T(4,128)(2,1)S(1)} all-to-all(bf16[8,4,12,128]{3,1,2,0:T(4,128)(2,1)S(1)} %bitcast.127), channel_id=1, replica_groups=mesh['req'=8,'head'=4] {'req'}, dimensions={0} | all-to-all | bytes 196608 | tf_op jit(solution)/shard_map/all_to_all | solution.py:181
  60.7 2.1 %fusion.6 = f32[8,12,2048,1]{2,0,3,1:T(8,128)S(1)} fusion(bf16[4,128,2048]{2,1,0:T(8,128)(2,1)} %param.16, bf16[8,4,12,128]{3,1,2,0:T(4,128)(2,1)S(1)} %all_to_all.20), kind=kOutput, calls=%fused_computation.11 | convolution fusion | flops 201326592 | bytes 2981888 | tf_op jit(solution)/shard_map/spnh,phd->snd/dot_general | solution.py:179
  62.8 1.1 %copy.157 = f32[8,4,12,4,128]{4,3,2,1,0:T(4,128)} copy(f32[8,4,12,4,128]{4,0,3,1,2:T(8,128)S(1)} %bitcast.122) | data formatting | bytes 1572864 | tf_op jit(solution)/shard_map/transpose | solution.py:185
  63.9 2.6 %all-to-all-start.3 = ((f32[32,48,128]{2,1,0:T(8,128)}), f32[32,48,128]{2,1,0:T(8,128)S(1)}, u32[]{:S(2)}, u32[]{:S(2)}) async-start(f32[32,48,128]{2,1,0:T(8,128)} %bitcast.39), calls=%async_computation.3 | async-start | bytes 1572864 | tf_op jit(solution)/shard_map/all_to_all | solution.py:196
  66.7 20.5 %all-to-all-done.3 = f32[32,48,128]{2,1,0:T(8,128)S(1)} async-done(((f32[32,48,128]{2,1,0:T(8,128)}), f32[32,48,128]{2,1,0:T(8,128)S(1)}, u32[]{:S(2)}, u32[]{:S(2)}) %all-to-all-start.3) | async-done | bytes 786464 | tf_op jit(solution)/shard_map/all_to_all | solution.py:196
  87.2 0.8 fusion.25
  (74 shorter events, 4.1 us)
Async XLA Ops:
  0.0 24.9 %copy-start = (bf16[4,2048,128]{2,1,0:T(8,128)(2,1)S(1)}, bf16[4,2048,128]{2,1,0:T(8,128)(2,1)}, u32[]{:S(2)}) copy-start(bf16[4,2048,128]{2,1,0:T(8,128)(2,1)} %param.15) | copy-start | bytes 6291460
  1.1 15.5 %copy-start.1 = (s32[32]{0:T(128)S(1)}, s32[32]{0:T(128)}, u32[]{:S(2)}) copy-start(s32[32]{0:T(128)} %param.19) | copy-start | bytes 388
  1.1 15.5 %copy-start.2 = (s32[32,32]{1,0:T(8,128)S(1)}, s32[32,32]{1,0:T(8,128)}, u32[]{:S(2)}) copy-start(s32[32,32]{1,0:T(8,128)} %param.20) | copy-start | bytes 12292
  1.4 15.9 %copy-start.3 = (s32[32,2]{0,1:T(2,128)S(1)}, s32[32,2]{0,1:T(2,128)}, u32[]{:S(2)}) copy-start(s32[32,2]{0,1:T(2,128)} %param.21) | copy-start | bytes 772
  6.0 18.9 %all-to-all-start = ((bf16[8,192,128]{2,1,0:T(8,128)(2,1)}), bf16[8,192,128]{2,1,0:T(8,128)(2,1)S(1)}, u32[]{:S(2)}, u32[]{:S(2)}) async-start(bf16[8,192,128]{2,1,0:T(8,128)(2,1)} %bitcast.6), calls=%async_computation | async-start | bytes 786432 | tf_op jit(solution)/shard_map/all_to_all | solution.py:82
  26.0 10.7 %all-to-all-start.1 = ((bf16[8,4,12,128]{3,1,2,0:T(4,128)(2,1)}), bf16[8,4,12,128]{3,1,2,0:T(4,128)(2,1)S(1)}, u32[]{:S(2)}, u32[]{:S(2)}) async-start(bf16[8,4,12,128]{3,1,2,0:T(4,128)(2,1)} %copy.140), calls=%async_computation.1 | async-start | bytes 196608 | tf_op jit(solution)/shard_map/all_to_all | solution.py:113
  60.7 5.8 %copy-start.5 = (s32[32]{0:T(128)S(1)}, s32[32]{0:T(128)}, u32[]{:S(2)}) copy-start(s32[32]{0:T(128)} %param.23) | copy-start | bytes 388
  60.7 5.8 %copy-start.4 = (f32[32,2]{0,1:T(2,128)S(1)}, f32[32,2]{0,1:T(2,128)}, u32[]{:S(2)}) copy-start(f32[32,2]{0,1:T(2,128)} %param.22) | copy-start | bytes 772
  63.9 23.2 %all-to-all-start.3 = ((f32[32,48,128]{2,1,0:T(8,128)}), f32[32,48,128]{2,1,0:T(8,128)S(1)}, u32[]{:S(2)}, u32[]{:S(2)}) async-start(f32[32,48,128]{2,1,0:T(8,128)} %bitcast.39), calls=%async_computation.3 | async-start | bytes 1572864 | tf_op jit(solution)/shard_map/all_to_all | solution.py:196

commit v13 on v10

--- a/solution.py
+++ b/solution.py
@@ -1,6 +1,7 @@
 import jax
 import jax.numpy as jnp
 from jax import lax
+from jax.experimental import pallas as pl
 from jax.sharding import PartitionSpec as P
 
 AEXP = 8
@@ -23,6 +24,12 @@
         [first_half * cosine - second * sine_part, second * cosine + first_half * sine_part],
         axis=-1,
     )
+
+
+def norm_kernel(tokens_ref, gain_ref, out_ref):
+    as_float = tokens_ref[...].astype(jnp.float32)
+    mean_square = jnp.mean(as_float * as_float, axis=-1, keepdims=True)
+    out_ref[...] = (as_float * lax.rsqrt(mean_square + eps) * gain_ref[...]).astype(out_ref.dtype)
 
 
 def body(
@@ -52,12 +59,9 @@
     max_pages = page_table.shape[1]
     experts = AEXP
     capacity = CAP
-    as_float = tokens.astype(jnp.float32)
-    normed = (
-        as_float
-        * lax.rsqrt(jnp.mean(as_float * as_float, axis=-1, keepdims=True) + eps)
-        * norm_gain
-    ).astype(jnp.bfloat16)
+    normed = pl.pallas_call(
+        norm_kernel, out_shape=jax.ShapeDtypeStruct(tokens.shape, jnp.bfloat16)
+    )(tokens, norm_gain.reshape(1, -1))
     flat_expert = expert_choice.reshape(-1)
     onehot = (flat_expert[:, None] == jnp.arange(experts)[None, :]).astype(jnp.int32)
     before = jnp.cumsum(onehot, axis=0) - onehot

time: 87.7 us -> 88.2 us (level)
  other arithmetic: 5.51 us -> 3.44 us
  Pallas kernels: 0 us -> 1.69 us
  local copies, waits for them, and re-layouts: 8.75 us -> 9.65 us
    pallas_call x0 -> x1, Pallas kernels: none -> 1.69 us  [body(): pl.pallas_call(norm_kernel, out_shape=jax.ShapeDtypeStruct(tokens.shape,...]
    reduce_sum x1 -> x0, other arithmetic: 1.04 us -> none  [body(): jnp.mean(as_float * as_float, axis=-1, keepdims=True) + eps]
    convert_element_type x1 -> x0, other arithmetic: 1.01 us -> none  [body(): normed = (as_float * lax.rsqrt(jnp.mean(as_float * as_float, axis=-1, kee...]
    broadcast_in_dim x1, local copies, waits for them, and re-layouts: 0.15 us -> 1.05 us  [body(): jnp.repeat(normed, choices_each, axis=0).reshape(-1, blocks, lanes)]
where the time goes in v13:
time: 88.2 us; the launch traced here: 87.7 us
  waiting for transfers between devices  30.9 us (35%)
  matrix products  18.6 us (21%)
  starting transfers between devices  13.5 us (15%)
  local copies, waits for them, and re-layouts  9.65 us (11%)
  blocking collectives  9.51 us (11%)
  other arithmetic  3.44 us (4%)
  Pallas kernels  1.69 us (2%)
    all_to_all x1, waiting for transfers between devices, body(): lax.all_to_all(partial_far.reshape(groups * head_count, capacity * wblock...  20.5 us
    all_to_all x1, blocking collectives, body(): lax.all_to_all(context_buf, 'req', split_axis=0, concat_axis=0, tiled=True)  9.51 us
    all_to_all x1, starting transfers between devices, body(): lax.all_to_all(sendbuf, 'req', split_axis=0, concat_axis=0, tiled=True)  7.26 us
    all_to_all x1, waiting for transfers between devices, body(): lax.all_to_all(queries_far, 'req', split_axis=0, concat_axis=0, tiled=True)  7.03 us
    dot_general x1, matrix products, body(): jnp.einsum('pkjhd,pthd->pkjt', spread_queries, cache_keys, preferred_elem...  5.91 us
    dot_general x1, matrix products, body(): jnp.einsum('pkjt,pthd->pkjhd', weights_rounded, cache_values, preferred_e...  4.76 us
    all_to_all x1, starting transfers between devices, body(): lax.all_to_all(queries_far, 'req', split_axis=0, concat_axis=0, tiled=True)  3.62 us
    all_to_all x1, waiting for transfers between devices, body(): lax.all_to_all(sendbuf, 'req', split_axis=0, concat_axis=0, tiled=True)  3.4 us
  transfers between devices with their start and end apart: 3, of which 3 were waited for; matrix products, arithmetic and copies ran while one was open for 9% of the time, Pallas kernels for 0%

profile of v13, /device:TPU:0, one launch (start us, length us, event | category | flops | bytes accessed | tf_op | source)
XLA Modules:
  0.0 87.7 jit_solution(17006380860908466733)
XLA Ops:
  0.0 0.9 %copy.135 = s32[32,2]{1,0:T(8,128)S(1)} copy(s32[32,2]{0,1:T(2,128)} %param.21) | data formatting | bytes 512 | tf_op args[9]
  1.4 1.7 %shard_map.118 = bf16[32,2048]{1,0:T(8,128)(2,1)} custom-call(bf16[32,2048]{1,0:T(8,128)(2,1)} %tokens_ref.1, f32[1,2048]{1,0:T(1,128)} %bitcast.131), custom_call_target="tpu_custom_call" | custom-call | tf_op jit(solution)/shard_map/pallas_call | solution.py:62
  3.1 1.1 %broadcast_in_dim.34 = bf16[32,2,2048]{2,1,0:T(2,128)(2,1)S(1)} broadcast(bf16[32,2048]{1,0:T(8,128)(2,1)} %shard_map.118), dimensions={0,2} | broadcast | bytes 393216 | tf_op jit(solution)/shard_map/broadcast_in_dim | solution.py:74
  4.3 0.4 convolution_convert_fusion
  4.7 0.9 %copy.138 = bf16[96,16,128]{2,1,0:T(8,128)(2,1)} copy(bf16[96,16,128]{2,0,1:T(8,128)(2,1)S(1)} %convolution_convert_fusion) | data formatting | bytes 786432 | tf_op jit(solution)/shard_map/convert_element_type | solution.py:77
  5.6 7.3 %all-to-all-start = ((bf16[8,192,128]{2,1,0:T(8,128)(2,1)}), bf16[8,192,128]{2,1,0:T(8,128)(2,1)S(1)}, u32[]{:S(2)}, u32[]{:S(2)}) async-start(bf16[8,192,128]{2,1,0:T(8,128)(2,1)} %bitcast.6), calls=%async_computation | async-start | bytes 786432 | tf_op jit(solution)/shard_map/all_to_all | solution.py:84
  13.0 3.1 %fusion.4 = f32[32,4,2,128]{3,0,2,1:T(8,128)S(1)} fusion(bf16[2048,4,2,128]{3,2,1,0:T(2,128)(2,1)} %param.14, bf16[32,2048]{1,0:T(8,128)(2,1)} %shard_map.118), kind=kOutput, calls=%fused_computation.9 | convolution fusion | flops 134217728 | bytes 4456448 | tf_op jit(solution)/shard_map/rf,fhkd->rhkd/dot_general | solution.py:91
  16.3 0.4 fusion.30
  16.9 0.8 gather_fusion
  17.7 0.6 gather_fusion.1
  19.0 0.7 gather_fusion.3
  19.8 0.7 gather_fusion.4
  20.5 0.4 select_reduce_fusion
  21.1 3.4 %all-to-all-done = bf16[8,192,128]{2,1,0:T(8,128)(2,1)S(1)} async-done(((bf16[8,192,128]{2,1,0:T(8,128)(2,1)}), bf16[8,192,128]{2,1,0:T(8,128)(2,1)S(1)}, u32[]{:S(2)}, u32[]{:S(2)}) %all-to-all-start) | async-done | bytes 393248 | tf_op jit(solution)/shard_map/all_to_all | solution.py:84
  24.5 0.4 fusion.21
  25.0 0.7 copy.140
  25.7 3.6 %all-to-all-start.1 = ((bf16[8,4,12,128]{3,1,2,0:T(4,128)(2,1)}), bf16[8,4,12,128]{3,1,2,0:T(4,128)(2,1)S(1)}, u32[]{:S(2)}, u32[]{:S(2)}) async-start(bf16[8,4,12,128]{3,1,2,0:T(4,128)(2,1)} %copy.140), calls=%async_computation.1 | async-start | bytes 196608 | tf_op jit(solution)/shard_map/all_to_all | solution.py:115
  29.4 7.0 %all-to-all-done.1 = bf16[8,4,12,128]{3,1,2,0:T(4,128)(2,1)S(1)} async-done(((bf16[8,4,12,128]{3,1,2,0:T(4,128)(2,1)}), bf16[8,4,12,128]{3,1,2,0:T(4,128)(2,1)S(1)}, u32[]{:S(2)}, u32[]{:S(2)}) %all-to-all-start.1) | async-done | bytes 98336 | tf_op jit(solution)/shard_map/all_to_all | solution.py:115
  36.4 0.7 gather_fusion.2
  37.2 0.2 subtract_convert_fusion
  37.6 5.9 %fusion.64 = (f32[64,2,4]{2,1,0:T(2,128)S(1)}, f32[64,2,4,128]{3,2,1,0:T(4,128)S(1)}) fusion(bf16[64,128,4,128,1]{3,2,1,0,4:T(4,128)(2,1)} %bitcast.133, bf16[4,4]{0,1:T(4,128)(2,1)S(1)} %fusion.60, bf16[64,2,4,128]{3,2,1,0:T(4,128)(2,1)S(1)} %pad_maximum_fusion, pred[64,128]{1,0:T(8,128)(4,1)S(1)} %fusion.54), kind=kOutput, calls=%fused_computation.106 | convolution fusion | flops 68353536 | bytes 8792096 | tf_op jit(solution)/shard_map/pkjhd,pthd->pkjt/dot_general | solution.py:137
  43.6 0.4 fusion.44
  44.4 0.4 fusion.36
  45.2 4.8 %fusion.11 = f32[64,2,4,128]{3,2,1,0:T(4,128)S(1)} fusion(bf16[64,128,4,128,1]{3,2,1,0,4:T(4,128)(2,1)} %bitcast.134, f32[4,4]{0,1:T(4,128)S(1)} %fusion.63, f32[64,2,4,128]{3,2,1,0:T(4,128)S(1)} %get-tuple-element.18, f32[64,2,4]{2,1,0:T(2,128)S(1)} %copy.148), kind=kOutput, calls=%fused_computation.15 | convolution fusion | flops 67698688 | bytes 8915008 | tf_op jit(solution)/shard_map/pkjt,pthd->pkjhd/dot_general | solution.py:161
  50.2 0.3 fusion.22
  50.5 0.3 convolution_convert_fusion.1
  50.9 9.5 %all_to_all.20 = bf16[8,4,12,128]{3,1,2,0:T(4,128)(2,1)S(1)} all-to-all(bf16[8,4,12,128]{3,1,2,0:T(4,128)(2,1)S(1)} %bitcast.127), channel_id=1, replica_groups=mesh['req'=8,'head'=4] {'req'}, dimensions={0} | all-to-all | bytes 196608 | tf_op jit(solution)/shard_map/all_to_all | solution.py:183
  60.4 2.1 %fusion.6 = f32[8,12,2048,1]{2,0,3,1:T(8,128)S(1)} fusion(bf16[4,128,2048]{2,1,0:T(8,128)(2,1)} %param.16, bf16[8,4,12,128]{3,1,2,0:T(4,128)(2,1)S(1)} %all_to_all.20), kind=kOutput, calls=%fused_computation.11 | convolution fusion | flops 201326592 | bytes 2981888 | tf_op jit(solution)/shard_map/spnh,phd->snd/dot_general | solution.py:181
  62.5 1.1 %copy.157 = f32[8,4,12,4,128]{4,3,2,1,0:T(4,128)} copy(f32[8,4,12,4,128]{4,0,3,1,2:T(8,128)S(1)} %bitcast.122) | data formatting | bytes 1572864 | tf_op jit(solution)/shard_map/transpose | solution.py:187
  63.5 2.6 %all-to-all-start.3 = ((f32[32,48,128]{2,1,0:T(8,128)}), f32[32,48,128]{2,1,0:T(8,128)S(1)}, u32[]{:S(2)}, u32[]{:S(2)}) async-start(f32[32,48,128]{2,1,0:T(8,128)} %bitcast.39), calls=%async_computation.3 | async-start | bytes 1572864 | tf_op jit(solution)/shard_map/all_to_all | solution.py:198
  66.3 20.5 %all-to-all-done.3 = f32[32,48,128]{2,1,0:T(8,128)S(1)} async-done(((f32[32,48,128]{2,1,0:T(8,128)}), f32[32,48,128]{2,1,0:T(8,128)S(1)}, u32[]{:S(2)}, u32[]{:S(2)}) %all-to-all-start.3) | async-done | bytes 786464 | tf_op jit(solution)/shard_map/all_to_all | solution.py:198
  86.8 0.8 fusion.23
  (70 shorter events, 3.8 us)
Async XLA Ops:
  0.0 24.5 %copy-start = (bf16[4,2048,128]{2,1,0:T(8,128)(2,1)S(1)}, bf16[4,2048,128]{2,1,0:T(8,128)(2,1)}, u32[]{:S(2)}) copy-start(bf16[4,2048,128]{2,1,0:T(8,128)(2,1)} %param.15) | copy-start | bytes 6291460
  0.0 16.1 %copy-start.1 = (s32[32]{0:T(128)S(1)}, s32[32]{0:T(128)}, u32[]{:S(2)}) copy-start(s32[32]{0:T(128)} %param.19) | copy-start | bytes 388
  0.0 16.2 %copy-start.2 = (s32[32,32]{1,0:T(8,128)S(1)}, s32[32,32]{1,0:T(8,128)}, u32[]{:S(2)}) copy-start(s32[32,32]{1,0:T(8,128)} %param.20) | copy-start | bytes 12292
  1.1 15.7 %copy-start.3 = (s32[32,2]{0,1:T(2,128)S(1)}, s32[32,2]{0,1:T(2,128)}, u32[]{:S(2)}) copy-start(s32[32,2]{0,1:T(2,128)} %param.21) | copy-start | bytes 772
  5.6 19.0 %all-to-all-start = ((bf16[8,192,128]{2,1,0:T(8,128)(2,1)}), bf16[8,192,128]{2,1,0:T(8,128)(2,1)S(1)}, u32[]{:S(2)}, u32[]{:S(2)}) async-start(bf16[8,192,128]{2,1,0:T(8,128)(2,1)} %bitcast.6), calls=%async_computation | async-start | bytes 786432 | tf_op jit(solution)/shard_map/all_to_all | solution.py:84
  25.7 10.7 %all-to-all-start.1 = ((bf16[8,4,12,128]{3,1,2,0:T(4,128)(2,1)}), bf16[8,4,12,128]{3,1,2,0:T(4,128)(2,1)S(1)}, u32[]{:S(2)}, u32[]{:S(2)}) async-start(bf16[8,4,12,128]{3,1,2,0:T(4,128)(2,1)} %copy.140), calls=%async_computation.1 | async-start | bytes 196608 | tf_op jit(solution)/shard_map/all_to_all | solution.py:115
  60.4 5.8 %copy-start.5 = (s32[32]{0:T(128)S(1)}, s32[32]{0:T(128)}, u32[]{:S(2)}) copy-start(s32[32]{0:T(128)} %param.23) | copy-start | bytes 388
  60.4 5.8 %copy-start.4 = (f32[32,2]{0,1:T(2,128)S(1)}, f32[32,2]{0,1:T(2,128)}, u32[]{:S(2)}) copy-start(f32[32,2]{0,1:T(2,128)} %param.22) | copy-start | bytes 772
  63.5 23.2 %all-to-all-start.3 = ((f32[32,48,128]{2,1,0:T(8,128)}), f32[32,48,128]{2,1,0:T(8,128)S(1)}, u32[]{:S(2)}, u32[]{:S(2)}) async-start(f32[32,48,128]{2,1,0:T(8,128)} %bitcast.39), calls=%async_computation.3 | async-start | bytes 1572864 | tf_op jit(solution)/shard_map/all_to_all | solution.py:198

commit v14 on v13

--- a/solution.py
+++ b/solution.py
@@ -71,9 +71,14 @@
     select_rows = select.astype(jnp.bfloat16)
     lanes = 128
     blocks = model_width // lanes
-    repeated = jnp.repeat(normed, choices_each, axis=0).reshape(-1, blocks, lanes)
+    select_tokens = jnp.any(
+        select.reshape(experts * capacity, row_count, choices_each), axis=2
+    ).astype(jnp.bfloat16)
     sendbuf = jnp.einsum(
-        "mr,rab->mab", select_rows, repeated, preferred_element_type=jnp.float32
+        "mr,rab->mab",
+        select_tokens,
+        normed.reshape(row_count, blocks, lanes),
+        preferred_element_type=jnp.float32,
     ).astype(jnp.bfloat16)
     replicas = groups // experts
     sendbuf = jnp.broadcast_to(

time: 88.2 us -> 89.7 us (1.017)
  other arithmetic: 3.44 us -> 6.24 us
  waiting for transfers between devices: 30.9 us -> 29.1 us
  local copies, waits for them, and re-layouts: 9.65 us -> 8.43 us
  starting transfers between devices: 13.5 us -> 14.4 us
    all_to_all x1, waiting for transfers between devices: 3.4 us -> 1.5 us  [body(): lax.all_to_all(sendbuf, 'req', split_axis=0, concat_axis=0, tiled=True)]
    broadcast_in_dim x1 -> x0, local copies, waits for them, and re-layouts: 1.05 us -> none  [body(): jnp.repeat(normed, choices_each, axis=0).reshape(-1, blocks, lanes)]
  transfers between devices with their start and end apart: 3 -> 3, of which waited for: 3 -> 3; matrix products, arithmetic and copies ran while one was open for 9% -> 11% of each run, Pallas kernels for 0% -> 0%
where the time goes in v14:
time: 89.7 us; the launch traced here: 89 us
  waiting for transfers between devices  29.1 us (32%)
  matrix products  19.3 us (22%)
  starting transfers between devices  14.4 us (16%)
  blocking collectives  9.51 us (11%)
  local copies, waits for them, and re-layouts  8.43 us (9%)
  other arithmetic  6.24 us (7%)
  Pallas kernels  1.69 us (2%)
    all_to_all x1, waiting for transfers between devices, body(): lax.all_to_all(partial_far.reshape(groups * head_count, capacity * wblock...  20.5 us
    all_to_all x1, blocking collectives, body(): lax.all_to_all(context_buf, 'req', split_axis=0, concat_axis=0, tiled=True)  9.51 us
    all_to_all x1, starting transfers between devices, body(): lax.all_to_all(sendbuf, 'req', split_axis=0, concat_axis=0, tiled=True)  7.25 us
    all_to_all x1, waiting for transfers between devices, body(): lax.all_to_all(queries_far, 'req', split_axis=0, concat_axis=0, tiled=True)  7.12 us
    dot_general x1, matrix products, body(): jnp.einsum('pkjhd,pthd->pkjt', spread_queries, cache_keys, preferred_elem...  5.92 us
    dot_general x1, matrix products, body(): jnp.einsum('pkjt,pthd->pkjhd', weights_rounded, cache_values, preferred_e...  4.77 us
    all_to_all x1, starting transfers between devices, body(): lax.all_to_all(queries_far, 'req', split_axis=0, concat_axis=0, tiled=True)  4.51 us
    dot_general x1, matrix products, body(): jnp.einsum('rf,fhkd->rhkd', normed, key_value_weight, preferred_element_t...  3.09 us
  transfers between devices with their start and end apart: 3, of which 3 were waited for; matrix products, arithmetic and copies ran while one was open for 11% of the time, Pallas kernels for 0%

profile of v14, /device:TPU:0, one launch (start us, length us, event | category | flops | bytes accessed | tf_op | source)
XLA Modules:
  0.0 89.0 jit_solution(13398829152005002691)
XLA Ops:
  0.0 0.9 %copy.136 = s32[32,2]{1,0:T(8,128)S(1)} copy(s32[32,2]{0,1:T(2,128)} %param.21) | data formatting | bytes 512 | tf_op args[9]
  1.6 0.7 multiply_add_fusion.2
  2.4 1.7 %shard_map.118 = bf16[32,2048]{1,0:T(8,128)(2,1)} custom-call(bf16[32,2048]{1,0:T(8,128)(2,1)} %tokens_ref.1, f32[1,2048]{1,0:T(1,128)} %bitcast.138), custom_call_target="tpu_custom_call" | custom-call | tf_op jit(solution)/shard_map/pallas_call | solution.py:62
  4.0 1.2 %convolution_convert_fusion = bf16[96,16,128]{2,0,1:T(8,128)(2,1)S(1)} fusion(pred[96,32]{0,1:T(8,128)(4,1)S(1)} %fusion.52, bf16[32,2048]{1,0:T(8,128)(2,1)} %shard_map.118), kind=kOutput, calls=%fused_computation.13 | convolution fusion | flops 12779520 | bytes 527360 | tf_op jit(solution)/shard_map/mr,rab->mab/dot_general | solution.py:77
  5.3 0.9 %copy.139 = bf16[96,16,128]{2,1,0:T(8,128)(2,1)} copy(bf16[96,16,128]{2,0,1:T(8,128)(2,1)S(1)} %convolution_convert_fusion) | data formatting | bytes 786432 | tf_op jit(solution)/shard_map/convert_element_type | solution.py:82
  6.2 7.3 %all-to-all-start = ((bf16[8,192,128]{2,1,0:T(8,128)(2,1)}), bf16[8,192,128]{2,1,0:T(8,128)(2,1)S(1)}, u32[]{:S(2)}, u32[]{:S(2)}) async-start(bf16[8,192,128]{2,1,0:T(8,128)(2,1)} %bitcast.6), calls=%async_computation | async-start | bytes 786432 | tf_op jit(solution)/shard_map/all_to_all | solution.py:89
  13.5 0.7 broadcast_subtract_fusion
  14.2 0.7 broadcast_compare_fusion
  15.0 0.4 fusion.30
  15.3 0.4 select_reduce_fusion
  15.7 0.7 convert_element_type.104
  16.5 3.1 %fusion.4 = f32[32,4,2,128]{3,0,2,1:T(8,128)S(1)} fusion(bf16[2048,4,2,128]{3,2,1,0:T(2,128)(2,1)} %param.14, bf16[32,2048]{1,0:T(8,128)(2,1)} %shard_map.118), kind=kOutput, calls=%fused_computation.9 | convolution fusion | flops 134217728 | bytes 4456448 | tf_op jit(solution)/shard_map/rf,fhkd->rhkd/dot_general | solution.py:96
  19.6 0.6 gather_fusion.1
  21.0 0.8 gather_fusion
  21.8 0.7 gather_fusion.3
  22.5 0.7 gather_fusion.4
  23.6 1.5 %all-to-all-done = bf16[8,192,128]{2,1,0:T(8,128)(2,1)S(1)} async-done(((bf16[8,192,128]{2,1,0:T(8,128)(2,1)}), bf16[8,192,128]{2,1,0:T(8,128)(2,1)S(1)}, u32[]{:S(2)}, u32[]{:S(2)}) %all-to-all-start) | async-done | bytes 393248 | tf_op jit(solution)/shard_map/all_to_all | solution.py:89
  25.1 0.4 fusion.21
  25.6 0.7 copy.141
  26.2 4.5 %all-to-all-start.1 = ((bf16[8,4,12,128]{3,1,2,0:T(4,128)(2,1)}), bf16[8,4,12,128]{3,1,2,0:T(4,128)(2,1)S(1)}, u32[]{:S(2)}, u32[]{:S(2)}) async-start(bf16[8,4,12,128]{3,1,2,0:T(4,128)(2,1)} %copy.141), calls=%async_computation.1 | async-start | bytes 196608 | tf_op jit(solution)/shard_map/all_to_all | solution.py:120
  30.7 7.1 %all-to-all-done.1 = bf16[8,4,12,128]{3,1,2,0:T(4,128)(2,1)S(1)} async-done(((bf16[8,4,12,128]{3,1,2,0:T(4,128)(2,1)}), bf16[8,4,12,128]{3,1,2,0:T(4,128)(2,1)S(1)}, u32[]{:S(2)}, u32[]{:S(2)}) %all-to-all-start.1) | async-done | bytes 98336 | tf_op jit(solution)/shard_map/all_to_all | solution.py:120
  37.9 0.7 gather_fusion.2
  39.1 5.9 %fusion.64 = (f32[64,2,4]{2,1,0:T(2,128)S(1)}, f32[64,2,4,128]{3,2,1,0:T(4,128)S(1)}) fusion(bf16[64,128,4,128,1]{3,2,1,0,4:T(4,128)(2,1)} %bitcast.140, bf16[4,4]{0,1:T(4,128)(2,1)S(1)} %fusion.60, bf16[64,2,4,128]{3,2,1,0:T(4,128)(2,1)S(1)} %pad_maximum_fusion, pred[64,128]{1,0:T(8,128)(4,1)S(1)} %fusion.54), kind=kOutput, calls=%fused_computation.107 | convolution fusion | flops 68353536 | bytes 8792096 | tf_op jit(solution)/shard_map/pkjhd,pthd->pkjt/dot_general | solution.py:142
  45.1 0.4 fusion.45
  45.9 0.4 fusion.35
  46.7 4.8 %fusion.11 = f32[64,2,4,128]{3,2,1,0:T(4,128)S(1)} fusion(bf16[64,128,4,128,1]{3,2,1,0,4:T(4,128)(2,1)} %bitcast.141, f32[4,4]{0,1:T(4,128)S(1)} %fusion.63, f32[64,2,4,128]{3,2,1,0:T(4,128)S(1)} %get-tuple-element.18, f32[64,2,4]{2,1,0:T(2,128)S(1)} %copy.149), kind=kOutput, calls=%fused_computation.15 | convolution fusion | flops 67698688 | bytes 8915008 | tf_op jit(solution)/shard_map/pkjt,pthd->pkjhd/dot_general | solution.py:166
  52.2 9.5 %all_to_all.20 = bf16[8,4,12,128]{3,1,2,0:T(4,128)(2,1)S(1)} all-to-all(bf16[8,4,12,128]{3,1,2,0:T(4,128)(2,1)S(1)} %bitcast.134), channel_id=1, replica_groups=mesh['req'=8,'head'=4] {'req'}, dimensions={0} | all-to-all | bytes 196608 | tf_op jit(solution)/shard_map/all_to_all | solution.py:188
  61.7 2.1 %fusion.6 = f32[8,12,2048,1]{2,0,3,1:T(8,128)S(1)} fusion(bf16[4,128,2048]{2,1,0:T(8,128)(2,1)} %param.16, bf16[8,4,12,128]{3,1,2,0:T(4,128)(2,1)S(1)} %all_to_all.20), kind=kOutput, calls=%fused_computation.11 | convolution fusion | flops 201326592 | bytes 2981888 | tf_op jit(solution)/shard_map/spnh,phd->snd/dot_general | solution.py:186
  63.8 1.1 %copy.158 = f32[8,4,12,4,128]{4,3,2,1,0:T(4,128)} copy(f32[8,4,12,4,128]{4,0,3,1,2:T(8,128)S(1)} %bitcast.129) | data formatting | bytes 1572864 | tf_op jit(solution)/shard_map/transpose | solution.py:192
  64.9 2.6 %all-to-all-start.3 = ((f32[32,48,128]{2,1,0:T(8,128)}), f32[32,48,128]{2,1,0:T(8,128)S(1)}, u32[]{:S(2)}, u32[]{:S(2)}) async-start(f32[32,48,128]{2,1,0:T(8,128)} %bitcast.39), calls=%async_computation.3 | async-start | bytes 1572864 | tf_op jit(solution)/shard_map/all_to_all | solution.py:203
  67.6 20.5 %all-to-all-done.3 = f32[32,48,128]{2,1,0:T(8,128)S(1)} async-done(((f32[32,48,128]{2,1,0:T(8,128)}), f32[32,48,128]{2,1,0:T(8,128)S(1)}, u32[]{:S(2)}, u32[]{:S(2)}) %all-to-all-start.3) | async-done | bytes 786464 | tf_op jit(solution)/shard_map/all_to_all | solution.py:203
  88.2 0.8 fusion.23
  (65 shorter events, 4.3 us)
Async XLA Ops:
  0.0 25.1 %copy-start = (bf16[4,2048,128]{2,1,0:T(8,128)(2,1)S(1)}, bf16[4,2048,128]{2,1,0:T(8,128)(2,1)}, u32[]{:S(2)}) copy-start(bf16[4,2048,128]{2,1,0:T(8,128)(2,1)} %param.15) | copy-start | bytes 6291460
  0.0 21.0 %copy-start.1 = (s32[32]{0:T(128)S(1)}, s32[32]{0:T(128)}, u32[]{:S(2)}) copy-start(s32[32]{0:T(128)} %param.19) | copy-start | bytes 388
  6.2 18.9 %all-to-all-start = ((bf16[8,192,128]{2,1,0:T(8,128)(2,1)}), bf16[8,192,128]{2,1,0:T(8,128)(2,1)S(1)}, u32[]{:S(2)}, u32[]{:S(2)}) async-start(bf16[8,192,128]{2,1,0:T(8,128)(2,1)} %bitcast.6), calls=%async_computation | async-start | bytes 786432 | tf_op jit(solution)/shard_map/all_to_all | solution.py:89
  26.2 11.6 %all-to-all-start.1 = ((bf16[8,4,12,128]{3,1,2,0:T(4,128)(2,1)}), bf16[8,4,12,128]{3,1,2,0:T(4,128)(2,1)S(1)}, u32[]{:S(2)}, u32[]{:S(2)}) async-start(bf16[8,4,12,128]{3,1,2,0:T(4,128)(2,1)} %copy.141), calls=%async_computation.1 | async-start | bytes 196608 | tf_op jit(solution)/shard_map/all_to_all | solution.py:120
  61.7 5.8 %copy-start.3 = (s32[32]{0:T(128)S(1)}, s32[32]{0:T(128)}, u32[]{:S(2)}) copy-start(s32[32]{0:T(128)} %param.23) | copy-start | bytes 388
  61.7 5.8 %copy-start.2 = (f32[32,2]{0,1:T(2,128)S(1)}, f32[32,2]{0,1:T(2,128)}, u32[]{:S(2)}) copy-start(f32[32,2]{0,1:T(2,128)} %param.22) | copy-start | bytes 772
  64.9 23.2 %all-to-all-start.3 = ((f32[32,48,128]{2,1,0:T(8,128)}), f32[32,48,128]{2,1,0:T(8,128)S(1)}, u32[]{:S(2)}, u32[]{:S(2)}) async-start(f32[32,48,128]{2,1,0:T(8,128)} %bitcast.39), calls=%async_computation.3 | async-start | bytes 1572864 | tf_op jit(solution)/shard_map/all_to_all | solution.py:203

commit v15 on v10

--- a/solution.py
+++ b/solution.py
@@ -67,9 +67,14 @@
     select_rows = select.astype(jnp.bfloat16)
     lanes = 128
     blocks = model_width // lanes
-    repeated = jnp.repeat(normed, choices_each, axis=0).reshape(-1, blocks, lanes)
+    select_tokens = jnp.any(
+        select.reshape(experts * capacity, row_count, choices_each), axis=2
+    ).astype(jnp.bfloat16)
     sendbuf = jnp.einsum(
-        "mr,rab->mab", select_rows, repeated, preferred_element_type=jnp.float32
+        "mr,rab->mab",
+        select_tokens,
+        normed.reshape(row_count, blocks, lanes),
+        preferred_element_type=jnp.float32,
     ).astype(jnp.bfloat16)
     replicas = groups // experts
     sendbuf = jnp.broadcast_to(

time: 87.7 us -> 89.1 us (1.016)
  waiting for transfers between devices: 31 us -> 29 us
  other arithmetic: 5.51 us -> 7.29 us
  starting transfers between devices: 13.5 us -> 14.4 us
  matrix products: 18.5 us -> 19.4 us
    all_to_all x1, waiting for transfers between devices: 3.47 us -> 1.44 us  [body(): lax.all_to_all(sendbuf, 'req', split_axis=0, concat_axis=0, tiled=True)]
    convert_element_type x1 -> x0, other arithmetic: 1.01 us -> none  [body(): normed = (as_float * lax.rsqrt(jnp.mean(as_float * as_float, axis=-1, kee...]
    all_to_all x1, starting transfers between devices: 3.62 us -> 4.57 us  [body(): lax.all_to_all(queries_far, 'req', split_axis=0, concat_axis=0, tiled=True)]
  transfers between devices with their start and end apart: 3 -> 3, of which waited for: 3 -> 3; matrix products, arithmetic and copies ran while one was open for 9% -> 12% of each run, Pallas kernels for 0% -> 0%
where the time goes in v15:
time: 89.1 us; the launch traced here: 88.5 us
  waiting for transfers between devices  29 us (33%)
  matrix products  19.4 us (22%)
  starting transfers between devices  14.4 us (16%)
  blocking collectives  9.51 us (11%)
  local copies, waits for them, and re-layouts  8.43 us (9%)
  other arithmetic  7.29 us (8%)
    all_to_all x1, waiting for transfers between devices, body(): lax.all_to_all(partial_far.reshape(groups * head_count, capacity * wblock...  20.5 us
    all_to_all x1, blocking collectives, body(): lax.all_to_all(context_buf, 'req', split_axis=0, concat_axis=0, tiled=True)  9.51 us
    all_to_all x1, starting transfers between devices, body(): lax.all_to_all(sendbuf, 'req', split_axis=0, concat_axis=0, tiled=True)  7.25 us
    all_to_all x1, waiting for transfers between devices, body(): lax.all_to_all(queries_far, 'req', split_axis=0, concat_axis=0, tiled=True)  7.12 us
    dot_general x1, matrix products, body(): jnp.einsum('pkjhd,pthd->pkjt', spread_queries, cache_keys, preferred_elem...  5.92 us
    dot_general x1, matrix products, body(): jnp.einsum('pkjt,pthd->pkjhd', weights_rounded, cache_values, preferred_e...  4.77 us
    all_to_all x1, starting transfers between devices, body(): lax.all_to_all(queries_far, 'req', split_axis=0, concat_axis=0, tiled=True)  4.57 us
    dot_general x1, matrix products, body(): jnp.einsum('rf,fhkd->rhkd', normed, key_value_weight, preferred_element_t...  3.15 us
  transfers between devices with their start and end apart: 3, of which 3 were waited for; matrix products, arithmetic and copies ran while one was open for 12% of the time, Pallas kernels for 0%

profile of v15, /device:TPU:0, one launch (start us, length us, event | category | flops | bytes accessed | tf_op | source)
XLA Modules:
  0.0 88.5 jit_solution(11587609479119328375)
XLA Ops:
  0.0 0.9 %copy.136 = s32[32,2]{1,0:T(8,128)S(1)} copy(s32[32,2]{0,1:T(2,128)} %param.21) | data formatting | bytes 512 | tf_op args[9]
  1.6 0.7 multiply_add_fusion.2
  2.4 1.0 %fusion.32 = f32[32]{0:T(128)S(1)} fusion(bf16[32,2048]{1,0:T(8,128)(2,1)} %param.12), kind=kLoop, calls=%fused_computation.37 | loop fusion | flops 196576 | bytes 131200 | tf_op jit(solution)/shard_map/reduce_sum | solution.py:58
  3.4 1.3 %convolution_convert_fusion = bf16[96,16,128]{2,0,1:T(8,128)(2,1)S(1)} fusion(pred[96,32]{0,1:T(8,128)(4,1)S(1)} %fusion.57, f32[2048]{0:T(1024)} %param.13, f32[32]{0:T(128)S(1)} %add_rsqrt_fusion, bf16[32,2048]{1,0:T(8,128)(2,1)} %param.12), kind=kOutput, calls=%fused_computation.13 | convolution fusion | flops 13041664 | bytes 535680 | tf_op jit(solution)/shard_map/mr,rab->mab/dot_general | solution.py:73
  4.7 0.9 %copy.139 = bf16[96,16,128]{2,1,0:T(8,128)(2,1)} copy(bf16[96,16,128]{2,0,1:T(8,128)(2,1)S(1)} %convolution_convert_fusion) | data formatting | bytes 786432 | tf_op jit(solution)/shard_map/convert_element_type | solution.py:78
  5.6 7.3 %all-to-all-start = ((bf16[8,192,128]{2,1,0:T(8,128)(2,1)}), bf16[8,192,128]{2,1,0:T(8,128)(2,1)S(1)}, u32[]{:S(2)}, u32[]{:S(2)}) async-start(bf16[8,192,128]{2,1,0:T(8,128)(2,1)} %bitcast.5), calls=%async_computation | async-start | bytes 786432 | tf_op jit(solution)/shard_map/all_to_all | solution.py:85
  12.9 0.7 broadcast_subtract_fusion
  13.6 0.7 broadcast_compare_fusion
  14.4 0.4 fusion.30
  14.7 0.4 select_reduce_fusion
  15.1 0.7 convert_element_type.112
  15.9 3.2 %fusion.4 = f32[32,4,2,128]{3,0,2,1:T(8,128)S(1)} fusion(bf16[2048,4,2,128]{3,2,1,0:T(2,128)(2,1)} %param.14, bf16[32,2048]{1,0:T(8,128)(2,1)} %param.12, f32[2048]{0:T(1024)} %param.13, f32[32]{0:T(128)S(1)} %add_rsqrt_fusion), kind=kOutput, calls=%fused_computation.9 | convolution fusion | flops 134479872 | bytes 4464768 | tf_op jit(solution)/shard_map/rf,fhkd->rhkd/dot_general | solution.py:92
  19.1 0.6 gather_fusion.1
  20.5 0.8 gather_fusion
  21.3 0.7 gather_fusion.3
  22.0 0.7 gather_fusion.4
  23.1 1.4 %all-to-all-done = bf16[8,192,128]{2,1,0:T(8,128)(2,1)S(1)} async-done(((bf16[8,192,128]{2,1,0:T(8,128)(2,1)}), bf16[8,192,128]{2,1,0:T(8,128)(2,1)S(1)}, u32[]{:S(2)}, u32[]{:S(2)}) %all-to-all-start) | async-done | bytes 393248 | tf_op jit(solution)/shard_map/all_to_all | solution.py:85
  24.5 0.4 fusion.21
  25.0 0.7 copy.141
  25.6 4.6 %all-to-all-start.1 = ((bf16[8,4,12,128]{3,1,2,0:T(4,128)(2,1)}), bf16[8,4,12,128]{3,1,2,0:T(4,128)(2,1)S(1)}, u32[]{:S(2)}, u32[]{:S(2)}) async-start(bf16[8,4,12,128]{3,1,2,0:T(4,128)(2,1)} %copy.141), calls=%async_computation.1 | async-start | bytes 196608 | tf_op jit(solution)/shard_map/all_to_all | solution.py:116
  30.2 7.1 %all-to-all-done.1 = bf16[8,4,12,128]{3,1,2,0:T(4,128)(2,1)S(1)} async-done(((bf16[8,4,12,128]{3,1,2,0:T(4,128)(2,1)}), bf16[8,4,12,128]{3,1,2,0:T(4,128)(2,1)S(1)}, u32[]{:S(2)}, u32[]{:S(2)}) %all-to-all-start.1) | async-done | bytes 98336 | tf_op jit(solution)/shard_map/all_to_all | solution.py:116
  37.3 0.7 gather_fusion.2
  38.5 5.9 %fusion.69 = (f32[64,2,4]{2,1,0:T(2,128)S(1)}, f32[64,2,4,128]{3,2,1,0:T(4,128)S(1)}) fusion(bf16[64,128,4,128,1]{3,2,1,0,4:T(4,128)(2,1)} %bitcast.138, bf16[4,4]{0,1:T(4,128)(2,1)S(1)} %fusion.65, bf16[64,2,4,128]{3,2,1,0:T(4,128)(2,1)S(1)} %pad_maximum_fusion, pred[64,128]{1,0:T(8,128)(4,1)S(1)} %fusion.59), kind=kOutput, calls=%fused_computation.114 | convolution fusion | flops 68353536 | bytes 8792096 | tf_op jit(solution)/shard_map/pkjhd,pthd->pkjt/dot_general | solution.py:138
  44.5 0.4 fusion.48
  45.4 0.4 fusion.38
  46.2 4.8 %fusion.11 = f32[64,2,4,128]{3,2,1,0:T(4,128)S(1)} fusion(bf16[64,128,4,128,1]{3,2,1,0,4:T(4,128)(2,1)} %bitcast.139, f32[4,4]{0,1:T(4,128)S(1)} %fusion.68, f32[64,2,4,128]{3,2,1,0:T(4,128)S(1)} %get-tuple-element.18, f32[64,2,4]{2,1,0:T(2,128)S(1)} %copy.149), kind=kOutput, calls=%fused_computation.15 | convolution fusion | flops 67698688 | bytes 8915008 | tf_op jit(solution)/shard_map/pkjt,pthd->pkjhd/dot_general | solution.py:162
  51.7 9.5 %all_to_all.20 = bf16[8,4,12,128]{3,1,2,0:T(4,128)(2,1)S(1)} all-to-all(bf16[8,4,12,128]{3,1,2,0:T(4,128)(2,1)S(1)} %bitcast.133), channel_id=1, replica_groups=mesh['req'=8,'head'=4] {'req'}, dimensions={0} | all-to-all | bytes 196608 | tf_op jit(solution)/shard_map/all_to_all | solution.py:184
  61.2 2.1 %fusion.6 = f32[8,12,2048,1]{2,0,3,1:T(8,128)S(1)} fusion(bf16[4,128,2048]{2,1,0:T(8,128)(2,1)} %param.16, bf16[8,4,12,128]{3,1,2,0:T(4,128)(2,1)S(1)} %all_to_all.20), kind=kOutput, calls=%fused_computation.11 | convolution fusion | flops 201326592 | bytes 2981888 | tf_op jit(solution)/shard_map/spnh,phd->snd/dot_general | solution.py:182
  63.3 1.1 %copy.158 = f32[8,4,12,4,128]{4,3,2,1,0:T(4,128)} copy(f32[8,4,12,4,128]{4,0,3,1,2:T(8,128)S(1)} %bitcast.128) | data formatting | bytes 1572864 | tf_op jit(solution)/shard_map/transpose | solution.py:188
  64.3 2.6 %all-to-all-start.3 = ((f32[32,48,128]{2,1,0:T(8,128)}), f32[32,48,128]{2,1,0:T(8,128)S(1)}, u32[]{:S(2)}, u32[]{:S(2)}) async-start(f32[32,48,128]{2,1,0:T(8,128)} %bitcast.38), calls=%async_computation.3 | async-start | bytes 1572864 | tf_op jit(solution)/shard_map/all_to_all | solution.py:199
  67.1 20.5 %all-to-all-done.3 = f32[32,48,128]{2,1,0:T(8,128)S(1)} async-done(((f32[32,48,128]{2,1,0:T(8,128)}), f32[32,48,128]{2,1,0:T(8,128)S(1)}, u32[]{:S(2)}, u32[]{:S(2)}) %all-to-all-start.3) | async-done | bytes 786464 | tf_op jit(solution)/shard_map/all_to_all | solution.py:199
  87.6 0.8 fusion.23
  (66 shorter events, 4.3 us)
Async XLA Ops:
  0.0 24.5 %copy-start = (bf16[4,2048,128]{2,1,0:T(8,128)(2,1)S(1)}, bf16[4,2048,128]{2,1,0:T(8,128)(2,1)}, u32[]{:S(2)}) copy-start(bf16[4,2048,128]{2,1,0:T(8,128)(2,1)} %param.15) | copy-start | bytes 6291460
  0.0 20.5 %copy-start.1 = (s32[32]{0:T(128)S(1)}, s32[32]{0:T(128)}, u32[]{:S(2)}) copy-start(s32[32]{0:T(128)} %param.19) | copy-start | bytes 388
  5.6 18.9 %all-to-all-start = ((bf16[8,192,128]{2,1,0:T(8,128)(2,1)}), bf16[8,192,128]{2,1,0:T(8,128)(2,1)S(1)}, u32[]{:S(2)}, u32[]{:S(2)}) async-start(bf16[8,192,128]{2,1,0:T(8,128)(2,1)} %bitcast.5), calls=%async_computation | async-start | bytes 786432 | tf_op jit(solution)/shard_map/all_to_all | solution.py:85
  25.6 11.7 %all-to-all-start.1 = ((bf16[8,4,12,128]{3,1,2,0:T(4,128)(2,1)}), bf16[8,4,12,128]{3,1,2,0:T(4,128)(2,1)S(1)}, u32[]{:S(2)}, u32[]{:S(2)}) async-start(bf16[8,4,12,128]{3,1,2,0:T(4,128)(2,1)} %copy.141), calls=%async_computation.1 | async-start | bytes 196608 | tf_op jit(solution)/shard_map/all_to_all | solution.py:116
  61.2 5.8 %copy-start.3 = (s32[32]{0:T(128)S(1)}, s32[32]{0:T(128)}, u32[]{:S(2)}) copy-start(s32[32]{0:T(128)} %param.23) | copy-start | bytes 388
  61.2 5.8 %copy-start.2 = (f32[32,2]{0,1:T(2,128)S(1)}, f32[32,2]{0,1:T(2,128)}, u32[]{:S(2)}) copy-start(f32[32,2]{0,1:T(2,128)} %param.22) | copy-start | bytes 772
  64.3 23.2 %all-to-all-start.3 = ((f32[32,48,128]{2,1,0:T(8,128)}), f32[32,48,128]{2,1,0:T(8,128)S(1)}, u32[]{:S(2)}, u32[]{:S(2)}) async-start(f32[32,48,128]{2,1,0:T(8,128)} %bitcast.38), calls=%async_computation.3 | async-start | bytes 1572864 | tf_op jit(solution)/shard_map/all_to_all | solution.py:199

commit v16 on v10

--- a/solution.py
+++ b/solution.py
@@ -199,12 +199,8 @@
         tiled=True,
     )
     summed = returned.reshape(experts, replicas * head_count, capacity * wblocks, lanes).sum(axis=1)
-    result = jnp.einsum(
-        "rm,mab->rab",
-        spread,
-        summed.reshape(experts * capacity, wblocks, lanes),
-        precision=lax.Precision.HIGHEST,
-    ).reshape(row_count, width_here)
+    picked_rows = summed.reshape(experts * capacity, width_here)[target.reshape(row_count, choices_each)]
+    result = jnp.sum(picked_rows * expert_gate[:, :, None], axis=1)
     return (result * alive_rows).astype(jnp.bfloat16)
 
 

time: 87.7 us -> 88.6 us (1.010)
  local copies, waits for them, and re-layouts: 8.75 us -> 9.78 us
  transfers between devices with their start and end apart: 3 -> 3, of which waited for: 3 -> 3; matrix products, arithmetic and copies ran while one was open for 9% -> 10% of each run, Pallas kernels for 0% -> 0%
where the time goes in v16:
time: 88.6 us; the launch traced here: 88 us
  waiting for transfers between devices  30.8 us (35%)
  matrix products  17.7 us (20%)
  starting transfers between devices  13.5 us (15%)
  local copies, waits for them, and re-layouts  9.78 us (11%)
  blocking collectives  9.51 us (11%)
  other arithmetic  6.35 us (7%)
    all_to_all x1, waiting for transfers between devices, body(): lax.all_to_all(partial_far.reshape(groups * head_count, capacity * wblock...  20.3 us
    all_to_all x1, blocking collectives, body(): lax.all_to_all(context_buf, 'req', split_axis=0, concat_axis=0, tiled=True)  9.51 us
    all_to_all x1, starting transfers between devices, body(): lax.all_to_all(sendbuf, 'req', split_axis=0, concat_axis=0, tiled=True)  7.25 us
    all_to_all x1, waiting for transfers between devices, body(): lax.all_to_all(queries_far, 'req', split_axis=0, concat_axis=0, tiled=True)  7.03 us
    dot_general x1, matrix products, body(): jnp.einsum('pkjhd,pthd->pkjt', spread_queries, cache_keys, preferred_elem...  5.91 us
    dot_general x1, matrix products, body(): jnp.einsum('pkjt,pthd->pkjhd', weights_rounded, cache_values, preferred_e...  4.76 us
    all_to_all x1, starting transfers between devices, body(): lax.all_to_all(queries_far, 'req', split_axis=0, concat_axis=0, tiled=True)  3.62 us
    all_to_all x1, waiting for transfers between devices, body(): lax.all_to_all(sendbuf, 'req', split_axis=0, concat_axis=0, tiled=True)  3.48 us
  transfers between devices with their start and end apart: 3, of which 3 were waited for; matrix products, arithmetic and copies ran while one was open for 10% of the time, Pallas kernels for 0%

profile of v16, /device:TPU:0, one launch (start us, length us, event | category | flops | bytes accessed | tf_op | source)
XLA Modules:
  0.0 88.0 jit_solution(12503446964445348239)
XLA Ops:
  0.0 0.9 %copy.135 = s32[32,2]{1,0:T(8,128)S(1)} copy(s32[32,2]{0,1:T(2,128)} %param.21) | data formatting | bytes 512 | tf_op args[9]
  1.4 1.0 %fusion.31 = f32[32]{0:T(128)S(1)} fusion(bf16[32,2048]{1,0:T(8,128)(2,1)} %param.12), kind=kLoop, calls=%fused_computation.36 | loop fusion | flops 196576 | bytes 131200 | tf_op jit(solution)/shard_map/reduce_sum | solution.py:58
  2.5 1.0 %fusion.33 = bf16[32,2048]{1,0:T(8,128)(2,1)S(1)} fusion(bf16[32,2048]{1,0:T(8,128)(2,1)} %param.12, f32[2048]{0:T(1024)} %param.13, f32[32]{0:T(128)S(1)} %add_rsqrt_fusion), kind=kLoop, calls=%fused_computation.38 | loop fusion | flops 262144 | bytes 270464 | tf_op jit(solution)/shard_map/convert_element_type | solution.py:60
  3.8 0.4 convolution_convert_fusion
  4.2 0.9 %copy.137 = bf16[96,16,128]{2,1,0:T(8,128)(2,1)} copy(bf16[96,16,128]{2,0,1:T(8,128)(2,1)S(1)} %convolution_convert_fusion) | data formatting | bytes 786432 | tf_op jit(solution)/shard_map/convert_element_type | solution.py:73
  5.1 7.3 %all-to-all-start = ((bf16[8,192,128]{2,1,0:T(8,128)(2,1)}), bf16[8,192,128]{2,1,0:T(8,128)(2,1)S(1)}, u32[]{:S(2)}, u32[]{:S(2)}) async-start(bf16[8,192,128]{2,1,0:T(8,128)(2,1)} %bitcast.5), calls=%async_computation | async-start | bytes 786432 | tf_op jit(solution)/shard_map/all_to_all | solution.py:80
  12.5 3.0 %fusion.4 = f32[32,4,2,128]{3,0,2,1:T(8,128)S(1)} fusion(bf16[2048,4,2,128]{3,2,1,0:T(2,128)(2,1)} %param.14, bf16[32,2048]{1,0:T(8,128)(2,1)S(1)} %fusion.33), kind=kOutput, calls=%fused_computation.10 | convolution fusion | flops 134217728 | bytes 4456448 | tf_op jit(solution)/shard_map/rf,fhkd->rhkd/dot_general | solution.py:87
  15.7 0.4 fusion.29
  16.3 0.8 gather_fusion
  17.1 0.6 gather_fusion.1
  18.4 0.7 gather_fusion.3
  19.2 0.7 gather_fusion.4
  19.9 0.4 select_reduce_fusion
  20.5 3.5 %all-to-all-done = bf16[8,192,128]{2,1,0:T(8,128)(2,1)S(1)} async-done(((bf16[8,192,128]{2,1,0:T(8,128)(2,1)}), bf16[8,192,128]{2,1,0:T(8,128)(2,1)S(1)}, u32[]{:S(2)}, u32[]{:S(2)}) %all-to-all-start) | async-done | bytes 393248 | tf_op jit(solution)/shard_map/all_to_all | solution.py:80
  24.0 0.4 fusion.21
  24.5 0.7 copy.139
  25.1 3.6 %all-to-all-start.1 = ((bf16[8,4,12,128]{3,1,2,0:T(4,128)(2,1)}), bf16[8,4,12,128]{3,1,2,0:T(4,128)(2,1)S(1)}, u32[]{:S(2)}, u32[]{:S(2)}) async-start(bf16[8,4,12,128]{3,1,2,0:T(4,128)(2,1)} %copy.139), calls=%async_computation.1 | async-start | bytes 196608 | tf_op jit(solution)/shard_map/all_to_all | solution.py:111
  28.9 7.0 %all-to-all-done.1 = bf16[8,4,12,128]{3,1,2,0:T(4,128)(2,1)S(1)} async-done(((bf16[8,4,12,128]{3,1,2,0:T(4,128)(2,1)}), bf16[8,4,12,128]{3,1,2,0:T(4,128)(2,1)S(1)}, u32[]{:S(2)}, u32[]{:S(2)}) %all-to-all-start.1) | async-done | bytes 98336 | tf_op jit(solution)/shard_map/all_to_all | solution.py:111
  35.9 0.7 gather_fusion.2
  37.1 5.9 %fusion.64 = (f32[64,2,4]{2,1,0:T(2,128)S(1)}, f32[64,2,4,128]{3,2,1,0:T(4,128)S(1)}) fusion(bf16[64,128,4,128,1]{3,2,1,0,4:T(4,128)(2,1)} %bitcast.120, bf16[4,4]{0,1:T(4,128)(2,1)S(1)} %fusion.60, bf16[64,2,4,128]{3,2,1,0:T(4,128)(2,1)S(1)} %pad_maximum_fusion, pred[64,128]{1,0:T(8,128)(4,1)S(1)} %fusion.54), kind=kOutput, calls=%fused_computation.111 | convolution fusion | flops 68353536 | bytes 8792096 | tf_op jit(solution)/shard_map/pkjhd,pthd->pkjt/dot_general | solution.py:133
  43.1 0.4 fusion.44
  43.9 0.4 fusion.38
  44.7 4.8 %fusion.11 = f32[64,2,4,128]{3,2,1,0:T(4,128)S(1)} fusion(bf16[64,128,4,128,1]{3,2,1,0,4:T(4,128)(2,1)} %bitcast.121, f32[4,4]{0,1:T(4,128)S(1)} %fusion.63, f32[64,2,4,128]{3,2,1,0:T(4,128)S(1)} %get-tuple-element.20, f32[64,2,4]{2,1,0:T(2,128)S(1)} %copy.148), kind=kOutput, calls=%fused_computation.16 | convolution fusion | flops 67698688 | bytes 8915008 | tf_op jit(solution)/shard_map/pkjt,pthd->pkjhd/dot_general | solution.py:157
  49.7 0.3 fusion.22
  50.0 0.3 convolution_convert_fusion.1
  50.3 9.5 %all_to_all.20 = bf16[8,4,12,128]{3,1,2,0:T(4,128)(2,1)S(1)} all-to-all(bf16[8,4,12,128]{3,1,2,0:T(4,128)(2,1)S(1)} %bitcast.115), channel_id=1, replica_groups=mesh['req'=8,'head'=4] {'req'}, dimensions={0} | all-to-all | bytes 196608 | tf_op jit(solution)/shard_map/all_to_all | solution.py:179
  59.9 2.1 %fusion.6 = f32[8,12,2048,1]{2,0,3,1:T(8,128)S(1)} fusion(bf16[4,128,2048]{2,1,0:T(8,128)(2,1)} %param.16, bf16[8,4,12,128]{3,1,2,0:T(4,128)(2,1)S(1)} %all_to_all.20), kind=kOutput, calls=%fused_computation.12 | convolution fusion | flops 201326592 | bytes 2981888 | tf_op jit(solution)/shard_map/spnh,phd->snd/dot_general | solution.py:177
  61.9 1.1 %copy.157 = f32[8,4,12,4,128]{4,3,2,1,0:T(4,128)} copy(f32[8,4,12,4,128]{4,0,3,1,2:T(8,128)S(1)} %bitcast.111) | data formatting | bytes 1572864 | tf_op jit(solution)/shard_map/transpose | solution.py:183
  63.0 2.6 %all-to-all-start.3 = ((f32[32,48,128]{2,1,0:T(8,128)}), f32[32,48,128]{2,1,0:T(8,128)S(1)}, u32[]{:S(2)}, u32[]{:S(2)}) async-start(f32[32,48,128]{2,1,0:T(8,128)} %bitcast.38), calls=%async_computation.3 | async-start | bytes 1572864 | tf_op jit(solution)/shard_map/all_to_all | solution.py:194
  66.0 20.3 %all-to-all-done.3 = f32[32,48,128]{2,1,0:T(8,128)S(1)} async-done(((f32[32,48,128]{2,1,0:T(8,128)}), f32[32,48,128]{2,1,0:T(8,128)S(1)}, u32[]{:S(2)}, u32[]{:S(2)}) %all-to-all-start.3) | async-done | bytes 786464 | tf_op jit(solution)/shard_map/all_to_all | solution.py:194
  86.3 0.7 gather_fusion.5
  87.3 0.7 multiply_convert_fusion
  (79 shorter events, 4.7 us)
Async XLA Ops:
  0.0 24.0 %copy-start = (bf16[4,2048,128]{2,1,0:T(8,128)(2,1)S(1)}, bf16[4,2048,128]{2,1,0:T(8,128)(2,1)}, u32[]{:S(2)}) copy-start(bf16[4,2048,128]{2,1,0:T(8,128)(2,1)} %param.15) | copy-start | bytes 6291460
  1.1 14.4 %copy-start.1 = (s32[32]{0:T(128)S(1)}, s32[32]{0:T(128)}, u32[]{:S(2)}) copy-start(s32[32]{0:T(128)} %param.19) | copy-start | bytes 388
  1.2 14.4 %copy-start.2 = (s32[32,32]{1,0:T(8,128)S(1)}, s32[32,32]{1,0:T(8,128)}, u32[]{:S(2)}) copy-start(s32[32,32]{1,0:T(8,128)} %param.20) | copy-start | bytes 12292
  1.4 14.8 %copy-start.3 = (s32[32,2]{0,1:T(2,128)S(1)}, s32[32,2]{0,1:T(2,128)}, u32[]{:S(2)}) copy-start(s32[32,2]{0,1:T(2,128)} %param.21) | copy-start | bytes 772
  5.1 18.9 %all-to-all-start = ((bf16[8,192,128]{2,1,0:T(8,128)(2,1)}), bf16[8,192,128]{2,1,0:T(8,128)(2,1)S(1)}, u32[]{:S(2)}, u32[]{:S(2)}) async-start(bf16[8,192,128]{2,1,0:T(8,128)(2,1)} %bitcast.5), calls=%async_computation | async-start | bytes 786432 | tf_op jit(solution)/shard_map/all_to_all | solution.py:80
  25.1 10.7 %all-to-all-start.1 = ((bf16[8,4,12,128]{3,1,2,0:T(4,128)(2,1)}), bf16[8,4,12,128]{3,1,2,0:T(4,128)(2,1)S(1)}, u32[]{:S(2)}, u32[]{:S(2)}) async-start(bf16[8,4,12,128]{3,1,2,0:T(4,128)(2,1)} %copy.139), calls=%async_computation.1 | async-start | bytes 196608 | tf_op jit(solution)/shard_map/all_to_all | solution.py:111
  59.9 6.0 %copy-start.4 = (f32[32,2]{0,1:T(2,128)S(1)}, f32[32,2]{0,1:T(2,128)}, u32[]{:S(2)}) copy-start(f32[32,2]{0,1:T(2,128)} %param.22) | copy-start | bytes 772
  59.9 6.1 %copy-start.5 = (s32[32]{0:T(128)S(1)}, s32[32]{0:T(128)}, u32[]{:S(2)}) copy-start(s32[32]{0:T(128)} %param.23) | copy-start | bytes 388
  63.0 23.2 %all-to-all-start.3 = ((f32[32,48,128]{2,1,0:T(8,128)}), f32[32,48,128]{2,1,0:T(8,128)S(1)}, u32[]{:S(2)}, u32[]{:S(2)}) async-start(f32[32,48,128]{2,1,0:T(8,128)} %bitcast.38), calls=%async_computation.3 | async-start | bytes 1572864 | tf_op jit(solution)/shard_map/all_to_all | solution.py:194

commit v17 on v10

--- a/solution.py
+++ b/solution.py
@@ -58,11 +58,11 @@
         * lax.rsqrt(jnp.mean(as_float * as_float, axis=-1, keepdims=True) + eps)
         * norm_gain
     ).astype(jnp.bfloat16)
-    flat_expert = expert_choice.reshape(-1)
-    onehot = (flat_expert[:, None] == jnp.arange(experts)[None, :]).astype(jnp.int32)
+    choice_major = expert_choice.T.reshape(-1)
+    onehot = (choice_major[:, None] == jnp.arange(experts)[None, :]).astype(jnp.int32)
     before = jnp.cumsum(onehot, axis=0) - onehot
     slot_index = jnp.sum(before * onehot, axis=1)
-    target = flat_expert * capacity + slot_index
+    target = (choice_major * capacity + slot_index).reshape(choices_each, row_count).T.reshape(-1)
     select = target[None, :] == jnp.arange(experts * capacity)[:, None]
     select_rows = select.astype(jnp.bfloat16)
     lanes = 128

time: 87.7 us -> 88.7 us (1.011)
  other arithmetic: 5.51 us -> 7.56 us
  waiting for transfers between devices: 31 us -> 29.9 us
    all_to_all x1, waiting for transfers between devices: 3.47 us -> 2.41 us  [body(): lax.all_to_all(sendbuf, 'req', split_axis=0, concat_axis=0, tiled=True)]
    unnamed x13 -> x8, local copies, waits for them, and re-layouts: 0.94 us -> 0.02 us
    eq x1 -> x2, local copies, waits for them, and re-layouts: 0.1 us -> 1.02 us  [the longest x1 0.92 us: body(): choice_major[:, None] == jnp.arange(experts)[None, :]]
  transfers between devices with their start and end apart: 3 -> 3, of which waited for: 3 -> 3; matrix products, arithmetic and copies ran while one was open for 9% -> 11% of each run, Pallas kernels for 0% -> 0%
where the time goes in v17:
time: 88.7 us; the launch traced here: 88 us
  waiting for transfers between devices  29.9 us (34%)
  matrix products  18.5 us (21%)
  starting transfers between devices  13.5 us (15%)
  blocking collectives  9.51 us (11%)
  local copies, waits for them, and re-layouts  8.65 us (10%)
  other arithmetic  7.56 us (9%)
    all_to_all x1, waiting for transfers between devices, body(): lax.all_to_all(partial_far.reshape(groups * head_count, capacity * wblock...  20.5 us
    all_to_all x1, blocking collectives, body(): lax.all_to_all(context_buf, 'req', split_axis=0, concat_axis=0, tiled=True)  9.51 us
    all_to_all x1, starting transfers between devices, body(): lax.all_to_all(sendbuf, 'req', split_axis=0, concat_axis=0, tiled=True)  7.25 us
    all_to_all x1, waiting for transfers between devices, body(): lax.all_to_all(queries_far, 'req', split_axis=0, concat_axis=0, tiled=True)  7.03 us
    dot_general x1, matrix products, body(): jnp.einsum('pkjhd,pthd->pkjt', spread_queries, cache_keys, preferred_elem...  5.92 us
    dot_general x1, matrix products, body(): jnp.einsum('pkjt,pthd->pkjhd', weights_rounded, cache_values, preferred_e...  4.76 us
    all_to_all x1, starting transfers between devices, body(): lax.all_to_all(queries_far, 'req', split_axis=0, concat_axis=0, tiled=True)  3.62 us
    dot_general x1, matrix products, body(): jnp.einsum('rf,fhkd->rhkd', normed, key_value_weight, preferred_element_t...  3.01 us
  transfers between devices with their start and end apart: 3, of which 3 were waited for; matrix products, arithmetic and copies ran while one was open for 11% of the time, Pallas kernels for 0%

profile of v17, /device:TPU:0, one launch (start us, length us, event | category | flops | bytes accessed | tf_op | source)
XLA Modules:
  0.0 88.0 jit_solution(6168851433842993594)
XLA Ops:
  0.0 0.9 %eq.94 = s32[64]{0:T(128)S(1)} reshape(s32[2,32]{1,0:T(2,128)} %bitcast.135) | data formatting | bytes 512 | tf_op jit(solution)/shard_map/eq | solution.py:62
  1.4 0.7 add_bitcast_fusion
  2.3 1.0 %fusion.32 = f32[32]{0:T(128)S(1)} fusion(bf16[32,2048]{1,0:T(8,128)(2,1)} %param.12), kind=kLoop, calls=%fused_computation.37 | loop fusion | flops 196576 | bytes 131200 | tf_op jit(solution)/shard_map/reduce_sum | solution.py:58
  3.3 1.0 %fusion.34 = bf16[32,2048]{1,0:T(8,128)(2,1)S(1)} fusion(bf16[32,2048]{1,0:T(8,128)(2,1)} %param.12, f32[2048]{0:T(1024)} %param.13, f32[32]{0:T(128)S(1)} %add_rsqrt_fusion), kind=kLoop, calls=%fused_computation.39 | loop fusion | flops 262144 | bytes 270464 | tf_op jit(solution)/shard_map/convert_element_type | solution.py:60
  4.7 0.4 convolution_convert_fusion
  5.0 0.9 %copy.137 = bf16[96,16,128]{2,1,0:T(8,128)(2,1)} copy(bf16[96,16,128]{2,0,1:T(8,128)(2,1)S(1)} %convolution_convert_fusion) | data formatting | bytes 786432 | tf_op jit(solution)/shard_map/convert_element_type | solution.py:73
  5.9 7.3 %all-to-all-start = ((bf16[8,192,128]{2,1,0:T(8,128)(2,1)}), bf16[8,192,128]{2,1,0:T(8,128)(2,1)S(1)}, u32[]{:S(2)}, u32[]{:S(2)}) async-start(bf16[8,192,128]{2,1,0:T(8,128)(2,1)} %bitcast.7), calls=%async_computation | async-start | bytes 786432 | tf_op jit(solution)/shard_map/all_to_all | solution.py:80
  13.2 0.7 broadcast_subtract_fusion
  13.9 0.7 broadcast_compare_fusion
  14.6 0.4 fusion.30
  15.0 0.6 gather_fusion.1
  15.7 0.8 gather_fusion
  16.6 3.0 %fusion.4 = f32[32,4,2,128]{3,0,2,1:T(8,128)S(1)} fusion(bf16[2048,4,2,128]{3,2,1,0:T(2,128)(2,1)} %param.14, bf16[32,2048]{1,0:T(8,128)(2,1)S(1)} %fusion.34), kind=kOutput, calls=%fused_computation.9 | convolution fusion | flops 134217728 | bytes 4456448 | tf_op jit(solution)/shard_map/rf,fhkd->rhkd/dot_general | solution.py:87
  20.3 0.7 gather_fusion.3
  21.1 0.7 gather_fusion.4
  21.8 0.4 select_reduce_fusion
  22.5 2.4 %all-to-all-done = bf16[8,192,128]{2,1,0:T(8,128)(2,1)S(1)} async-done(((bf16[8,192,128]{2,1,0:T(8,128)(2,1)}), bf16[8,192,128]{2,1,0:T(8,128)(2,1)S(1)}, u32[]{:S(2)}, u32[]{:S(2)}) %all-to-all-start) | async-done | bytes 393248 | tf_op jit(solution)/shard_map/all_to_all | solution.py:80
  24.9 0.4 fusion.21
  25.3 0.7 copy.139
  26.0 3.6 %all-to-all-start.1 = ((bf16[8,4,12,128]{3,1,2,0:T(4,128)(2,1)}), bf16[8,4,12,128]{3,1,2,0:T(4,128)(2,1)S(1)}, u32[]{:S(2)}, u32[]{:S(2)}) async-start(bf16[8,4,12,128]{3,1,2,0:T(4,128)(2,1)} %copy.139), calls=%async_computation.1 | async-start | bytes 196608 | tf_op jit(solution)/shard_map/all_to_all | solution.py:111
  29.7 7.0 %all-to-all-done.1 = bf16[8,4,12,128]{3,1,2,0:T(4,128)(2,1)S(1)} async-done(((bf16[8,4,12,128]{3,1,2,0:T(4,128)(2,1)}), bf16[8,4,12,128]{3,1,2,0:T(4,128)(2,1)S(1)}, u32[]{:S(2)}, u32[]{:S(2)}) %all-to-all-start.1) | async-done | bytes 98336 | tf_op jit(solution)/shard_map/all_to_all | solution.py:111
  36.7 0.7 gather_fusion.2
  38.0 5.9 %fusion.67 = (f32[64,2,4]{2,1,0:T(2,128)S(1)}, f32[64,2,4,128]{3,2,1,0:T(4,128)S(1)}) fusion(bf16[64,128,4,128,1]{3,2,1,0,4:T(4,128)(2,1)} %bitcast.136, bf16[4,4]{0,1:T(4,128)(2,1)S(1)} %fusion.63, bf16[64,2,4,128]{3,2,1,0:T(4,128)(2,1)S(1)} %pad_maximum_fusion, pred[64,128]{1,0:T(8,128)(4,1)S(1)} %fusion.57), kind=kOutput, calls=%fused_computation.111 | convolution fusion | flops 68353536 | bytes 8792096 | tf_op jit(solution)/shard_map/pkjhd,pthd->pkjt/dot_general | solution.py:133
  44.0 0.4 fusion.47
  44.8 0.4 fusion.39
  45.6 4.8 %fusion.11 = f32[64,2,4,128]{3,2,1,0:T(4,128)S(1)} fusion(bf16[64,128,4,128,1]{3,2,1,0,4:T(4,128)(2,1)} %bitcast.137, f32[4,4]{0,1:T(4,128)S(1)} %fusion.66, f32[64,2,4,128]{3,2,1,0:T(4,128)S(1)} %get-tuple-element.18, f32[64,2,4]{2,1,0:T(2,128)S(1)} %copy.147), kind=kOutput, calls=%fused_computation.15 | convolution fusion | flops 67698688 | bytes 8915008 | tf_op jit(solution)/shard_map/pkjt,pthd->pkjhd/dot_general | solution.py:157
  51.2 9.5 %all_to_all.20 = bf16[8,4,12,128]{3,1,2,0:T(4,128)(2,1)S(1)} all-to-all(bf16[8,4,12,128]{3,1,2,0:T(4,128)(2,1)S(1)} %bitcast.130), channel_id=1, replica_groups=mesh['req'=8,'head'=4] {'req'}, dimensions={0} | all-to-all | bytes 196608 | tf_op jit(solution)/shard_map/all_to_all | solution.py:179
  60.7 2.1 %fusion.6 = f32[8,12,2048,1]{2,0,3,1:T(8,128)S(1)} fusion(bf16[4,128,2048]{2,1,0:T(8,128)(2,1)} %param.16, bf16[8,4,12,128]{3,1,2,0:T(4,128)(2,1)S(1)} %all_to_all.20), kind=kOutput, calls=%fused_computation.11 | convolution fusion | flops 201326592 | bytes 2981888 | tf_op jit(solution)/shard_map/spnh,phd->snd/dot_general | solution.py:177
  62.8 1.1 %copy.156 = f32[8,4,12,4,128]{4,3,2,1,0:T(4,128)} copy(f32[8,4,12,4,128]{4,0,3,1,2:T(8,128)S(1)} %bitcast.125) | data formatting | bytes 1572864 | tf_op jit(solution)/shard_map/transpose | solution.py:183
  63.9 2.6 %all-to-all-start.3 = ((f32[32,48,128]{2,1,0:T(8,128)}), f32[32,48,128]{2,1,0:T(8,128)S(1)}, u32[]{:S(2)}, u32[]{:S(2)}) async-start(f32[32,48,128]{2,1,0:T(8,128)} %bitcast.40), calls=%async_computation.3 | async-start | bytes 1572864 | tf_op jit(solution)/shard_map/all_to_all | solution.py:194
  66.6 20.5 %all-to-all-done.3 = f32[32,48,128]{2,1,0:T(8,128)S(1)} async-done(((f32[32,48,128]{2,1,0:T(8,128)}), f32[32,48,128]{2,1,0:T(8,128)S(1)}, u32[]{:S(2)}, u32[]{:S(2)}) %all-to-all-start.3) | async-done | bytes 786464 | tf_op jit(solution)/shard_map/all_to_all | solution.py:194
  87.2 0.8 fusion.23
  (66 shorter events, 4.5 us)
Async XLA Ops:
  0.0 24.9 %copy-start = (bf16[4,2048,128]{2,1,0:T(8,128)(2,1)S(1)}, bf16[4,2048,128]{2,1,0:T(8,128)(2,1)}, u32[]{:S(2)}) copy-start(bf16[4,2048,128]{2,1,0:T(8,128)(2,1)} %param.15) | copy-start | bytes 6291460
  0.0 15.6 %copy-start.1 = (s32[32]{0:T(128)S(1)}, s32[32]{0:T(128)}, u32[]{:S(2)}) copy-start(s32[32]{0:T(128)} %param.19) | copy-start | bytes 388
  5.9 18.9 %all-to-all-start = ((bf16[8,192,128]{2,1,0:T(8,128)(2,1)}), bf16[8,192,128]{2,1,0:T(8,128)(2,1)S(1)}, u32[]{:S(2)}, u32[]{:S(2)}) async-start(bf16[8,192,128]{2,1,0:T(8,128)(2,1)} %bitcast.7), calls=%async_computation | async-start | bytes 786432 | tf_op jit(solution)/shard_map/all_to_all | solution.py:80
  26.0 10.7 %all-to-all-start.1 = ((bf16[8,4,12,128]{3,1,2,0:T(4,128)(2,1)}), bf16[8,4,12,128]{3,1,2,0:T(4,128)(2,1)S(1)}, u32[]{:S(2)}, u32[]{:S(2)}) async-start(bf16[8,4,12,128]{3,1,2,0:T(4,128)(2,1)} %copy.139), calls=%async_computation.1 | async-start | bytes 196608 | tf_op jit(solution)/shard_map/all_to_all | solution.py:111
  60.7 5.8 %copy-start.3 = (s32[32]{0:T(128)S(1)}, s32[32]{0:T(128)}, u32[]{:S(2)}) copy-start(s32[32]{0:T(128)} %param.23) | copy-start | bytes 388
  60.7 5.8 %copy-start.2 = (f32[32,2]{0,1:T(2,128)S(1)}, f32[32,2]{0,1:T(2,128)}, u32[]{:S(2)}) copy-start(f32[32,2]{0,1:T(2,128)} %param.22) | copy-start | bytes 772
  63.9 23.2 %all-to-all-start.3 = ((f32[32,48,128]{2,1,0:T(8,128)}), f32[32,48,128]{2,1,0:T(8,128)S(1)}, u32[]{:S(2)}, u32[]{:S(2)}) async-start(f32[32,48,128]{2,1,0:T(8,128)} %bitcast.40), calls=%async_computation.3 | async-start | bytes 1572864 | tf_op jit(solution)/shard_map/all_to_all | solution.py:194

commit v18 on v10

--- a/solution.py
+++ b/solution.py
@@ -146,12 +146,7 @@
     weights = jnp.exp(scores - row_top[..., None])
     fresh_weight = jnp.exp(fresh_score - row_top)
     owned_float = owned_pages.astype(jnp.float32)
-    denominator = jnp.einsum(
-        "rp,pkh->rkh",
-        owned_float,
-        jnp.sum(weights, axis=3) + leader_float * fresh_weight,
-        precision=lax.Precision.HIGHEST,
-    )
+    page_denominator = jnp.sum(weights, axis=3) + leader_float * fresh_weight
     weights_rounded = weights.astype(jnp.bfloat16)
     fresh_rounded = lax.optimization_barrier(fresh_weight.astype(jnp.bfloat16)).astype(jnp.float32)
     page_context = jnp.einsum(
@@ -161,9 +156,14 @@
     page_context = page_context + (leader_float * fresh_rounded)[..., None] * value_page.astype(
         jnp.float32
     )[:, None]
-    accumulated = jnp.einsum(
-        "rp,pkhd->rkhd", owned_float, page_context, precision=lax.Precision.HIGHEST
-    )
+    both = jnp.einsum(
+        "rp,pkhd->rkhd",
+        owned_float,
+        jnp.concatenate([page_context, page_denominator[..., None]], axis=3),
+        precision=lax.Precision.HIGHEST,
+    )
+    accumulated = both[..., :head_dim]
+    denominator = both[..., head_dim]
     context = (accumulated / denominator[..., None]).astype(jnp.bfloat16)
     context_flat = context.reshape(row_count * choices_each, heads_here * head_dim)
     context_buf = jnp.dot(select_rows, context_flat, preferred_element_type=jnp.float32).astype(

time: 87.7 us -> 88.9 us (1.014)
  other arithmetic: 5.51 us -> 7.59 us
  waiting for transfers between devices: 31 us -> 29 us
  starting transfers between devices: 13.5 us -> 14.4 us
    all_to_all x1, waiting for transfers between devices: 3.47 us -> 1.48 us  [body(): lax.all_to_all(sendbuf, 'req', split_axis=0, concat_axis=0, tiled=True)]
    all_to_all x1, starting transfers between devices: 3.62 us -> 4.54 us  [body(): lax.all_to_all(queries_far, 'req', split_axis=0, concat_axis=0, tiled=True)]
  transfers between devices with their start and end apart: 3 -> 3, of which waited for: 3 -> 3; matrix products, arithmetic and copies ran while one was open for 9% -> 12% of each run, Pallas kernels for 0% -> 0%
where the time goes in v18:
time: 88.9 us; the launch traced here: 88.2 us
  waiting for transfers between devices  29 us (33%)
  matrix products  18.4 us (21%)
  starting transfers between devices  14.4 us (16%)
  blocking collectives  9.51 us (11%)
  local copies, waits for them, and re-layouts  8.88 us (10%)
  other arithmetic  7.59 us (9%)
    all_to_all x1, waiting for transfers between devices, body(): lax.all_to_all(partial_far.reshape(groups * head_count, capacity * wblock...  20.5 us
    all_to_all x1, blocking collectives, body(): lax.all_to_all(context_buf, 'req', split_axis=0, concat_axis=0, tiled=True)  9.51 us
    all_to_all x1, starting transfers between devices, body(): lax.all_to_all(sendbuf, 'req', split_axis=0, concat_axis=0, tiled=True)  7.25 us
    all_to_all x1, waiting for transfers between devices, body(): lax.all_to_all(queries_far, 'req', split_axis=0, concat_axis=0, tiled=True)  7.03 us
    dot_general x1, matrix products, body(): jnp.einsum('pkjhd,pthd->pkjt', spread_queries, cache_keys, preferred_elem...  5.92 us
    dot_general x1, matrix products, body(): jnp.einsum('pkjt,pthd->pkjhd', weights_rounded, cache_values, preferred_e...  4.74 us
    all_to_all x1, starting transfers between devices, body(): lax.all_to_all(queries_far, 'req', split_axis=0, concat_axis=0, tiled=True)  4.54 us
    dot_general x1, matrix products, body(): jnp.einsum('rf,fhkd->rhkd', normed, key_value_weight, preferred_element_t...  3.01 us
  transfers between devices with their start and end apart: 3, of which 3 were waited for; matrix products, arithmetic and copies ran while one was open for 12% of the time, Pallas kernels for 0%

profile of v18, /device:TPU:0, one launch (start us, length us, event | category | flops | bytes accessed | tf_op | source)
XLA Modules:
  0.0 88.2 jit_solution(907130953835919392)
XLA Ops:
  0.0 0.9 %copy.142 = s32[32,2]{1,0:T(8,128)S(1)} copy(s32[32,2]{0,1:T(2,128)} %param.21) | data formatting | bytes 512 | tf_op args[9]
  1.4 1.0 %fusion.35 = f32[32]{0:T(128)S(1)} fusion(bf16[32,2048]{1,0:T(8,128)(2,1)} %param.12), kind=kLoop, calls=%fused_computation.39 | loop fusion | flops 196576 | bytes 131200 | tf_op jit(solution)/shard_map/reduce_sum | solution.py:58
  2.5 1.0 %fusion.37 = bf16[32,2048]{1,0:T(8,128)(2,1)S(1)} fusion(bf16[32,2048]{1,0:T(8,128)(2,1)} %param.12, f32[2048]{0:T(1024)} %param.13, f32[32]{0:T(128)S(1)} %add_rsqrt_fusion), kind=kLoop, calls=%fused_computation.41 | loop fusion | flops 262144 | bytes 270464 | tf_op jit(solution)/shard_map/convert_element_type | solution.py:60
  3.8 0.4 convolution_convert_fusion
  4.2 0.9 %copy.145 = bf16[96,16,128]{2,1,0:T(8,128)(2,1)} copy(bf16[96,16,128]{2,0,1:T(8,128)(2,1)S(1)} %convolution_convert_fusion) | data formatting | bytes 786432 | tf_op jit(solution)/shard_map/convert_element_type | solution.py:73
  5.1 7.3 %all-to-all-start = ((bf16[8,192,128]{2,1,0:T(8,128)(2,1)}), bf16[8,192,128]{2,1,0:T(8,128)(2,1)S(1)}, u32[]{:S(2)}, u32[]{:S(2)}) async-start(bf16[8,192,128]{2,1,0:T(8,128)(2,1)} %bitcast.5), calls=%async_computation | async-start | bytes 786432 | tf_op jit(solution)/shard_map/all_to_all | solution.py:80
  12.5 0.7 broadcast_subtract_fusion
  13.2 0.7 broadcast_compare_fusion
  13.9 0.4 fusion.33
  14.3 0.4 select_reduce_fusion
  14.6 0.7 convert_element_type.111
  15.4 3.0 %fusion.4 = f32[32,4,2,128]{3,0,2,1:T(8,128)S(1)} fusion(bf16[2048,4,2,128]{3,2,1,0:T(2,128)(2,1)} %param.14, bf16[32,2048]{1,0:T(8,128)(2,1)S(1)} %fusion.37), kind=kOutput, calls=%fused_computation.9 | convolution fusion | flops 134217728 | bytes 4456448 | tf_op jit(solution)/shard_map/rf,fhkd->rhkd/dot_general | solution.py:87
  18.7 0.6 gather_fusion.1
  20.1 0.8 gather_fusion
  20.9 0.7 gather_fusion.3
  21.6 0.7 gather_fusion.4
  22.5 1.5 %all-to-all-done = bf16[8,192,128]{2,1,0:T(8,128)(2,1)S(1)} async-done(((bf16[8,192,128]{2,1,0:T(8,128)(2,1)}), bf16[8,192,128]{2,1,0:T(8,128)(2,1)S(1)}, u32[]{:S(2)}, u32[]{:S(2)}) %all-to-all-start) | async-done | bytes 393248 | tf_op jit(solution)/shard_map/all_to_all | solution.py:80
  24.0 0.4 fusion.21
  24.5 0.7 copy.147
  25.1 4.5 %all-to-all-start.1 = ((bf16[8,4,12,128]{3,1,2,0:T(4,128)(2,1)}), bf16[8,4,12,128]{3,1,2,0:T(4,128)(2,1)S(1)}, u32[]{:S(2)}, u32[]{:S(2)}) async-start(bf16[8,4,12,128]{3,1,2,0:T(4,128)(2,1)} %copy.147), calls=%async_computation.1 | async-start | bytes 196608 | tf_op jit(solution)/shard_map/all_to_all | solution.py:111
  29.8 7.0 %all-to-all-done.1 = bf16[8,4,12,128]{3,1,2,0:T(4,128)(2,1)S(1)} async-done(((bf16[8,4,12,128]{3,1,2,0:T(4,128)(2,1)}), bf16[8,4,12,128]{3,1,2,0:T(4,128)(2,1)S(1)}, u32[]{:S(2)}, u32[]{:S(2)}) %all-to-all-start.1) | async-done | bytes 98336 | tf_op jit(solution)/shard_map/all_to_all | solution.py:111
  36.8 0.7 gather_fusion.2
  38.0 5.9 %fusion.71 = (f32[64,2,4]{2,1,0:T(2,128)S(1)}, f32[64,2,4,128]{3,2,1,0:T(4,128)S(1)}) fusion(bf16[64,128,4,128,1]{3,2,1,0,4:T(4,128)(2,1)} %bitcast.127, bf16[4,4]{0,1:T(4,128)(2,1)S(1)} %fusion.66, bf16[64,2,4,128]{3,2,1,0:T(4,128)(2,1)S(1)} %pad_maximum_fusion, pred[64,128]{1,0:T(8,128)(4,1)S(1)} %fusion.60), kind=kOutput, calls=%fused_computation.118 | convolution fusion | flops 68353536 | bytes 8792096 | tf_op jit(solution)/shard_map/pkjhd,pthd->pkjt/dot_general | solution.py:133
  44.0 0.4 fusion.50
  44.9 0.4 fusion.41
  45.6 4.7 %fusion.11 = f32[64,2,4,128]{3,2,1,0:T(4,128)S(1)} fusion(bf16[64,128,4,128,1]{3,2,1,0,4:T(4,128)(2,1)} %bitcast.128, f32[4,4]{0,1:T(4,128)S(1)} %fusion.69, f32[64,2,4,128]{3,2,1,0:T(4,128)S(1)} %get-tuple-element.18, f32[64,2,4]{2,1,0:T(2,128)S(1)} %copy.155), kind=kOutput, calls=%fused_computation.15 | convolution fusion | flops 67698688 | bytes 8915008 | tf_op jit(solution)/shard_map/pkjt,pthd->pkjhd/dot_general | solution.py:152
  51.4 9.5 %all_to_all.20 = bf16[8,4,12,128]{3,1,2,0:T(4,128)(2,1)S(1)} all-to-all(bf16[8,4,12,128]{3,1,2,0:T(4,128)(2,1)S(1)} %bitcast.124), channel_id=1, replica_groups=mesh['req'=8,'head'=4] {'req'}, dimensions={0} | all-to-all | bytes 196608 | tf_op jit(solution)/shard_map/all_to_all | solution.py:179
  60.9 2.1 %fusion.6 = f32[8,12,2048,1]{2,0,3,1:T(8,128)S(1)} fusion(bf16[4,128,2048]{2,1,0:T(8,128)(2,1)} %param.16, bf16[8,4,12,128]{3,1,2,0:T(4,128)(2,1)S(1)} %all_to_all.20), kind=kOutput, calls=%fused_computation.11 | convolution fusion | flops 201326592 | bytes 2981888 | tf_op jit(solution)/shard_map/spnh,phd->snd/dot_general | solution.py:177
  63.0 1.1 %copy.165 = f32[8,4,12,4,128]{4,3,2,1,0:T(4,128)} copy(f32[8,4,12,4,128]{4,0,3,1,2:T(8,128)S(1)} %bitcast.119) | data formatting | bytes 1572864 | tf_op jit(solution)/shard_map/transpose | solution.py:183
  64.1 2.6 %all-to-all-start.3 = ((f32[32,48,128]{2,1,0:T(8,128)}), f32[32,48,128]{2,1,0:T(8,128)S(1)}, u32[]{:S(2)}, u32[]{:S(2)}) async-start(f32[32,48,128]{2,1,0:T(8,128)} %bitcast.37), calls=%async_computation.3 | async-start | bytes 1572864 | tf_op jit(solution)/shard_map/all_to_all | solution.py:194
  66.8 20.5 %all-to-all-done.3 = f32[32,48,128]{2,1,0:T(8,128)S(1)} async-done(((f32[32,48,128]{2,1,0:T(8,128)}), f32[32,48,128]{2,1,0:T(8,128)S(1)}, u32[]{:S(2)}, u32[]{:S(2)}) %all-to-all-start.3) | async-done | bytes 786464 | tf_op jit(solution)/shard_map/all_to_all | solution.py:194
  87.4 0.8 fusion.22
  (71 shorter events, 4.8 us)
Async XLA Ops:
  0.0 24.0 %copy-start = (bf16[4,2048,128]{2,1,0:T(8,128)(2,1)S(1)}, bf16[4,2048,128]{2,1,0:T(8,128)(2,1)}, u32[]{:S(2)}) copy-start(bf16[4,2048,128]{2,1,0:T(8,128)(2,1)} %param.15) | copy-start | bytes 6291460
  1.4 17.2 %copy-start.2 = (s32[32,2]{0,1:T(2,128)S(1)}, s32[32,2]{0,1:T(2,128)}, u32[]{:S(2)}) copy-start(s32[32,2]{0,1:T(2,128)} %param.21) | copy-start | bytes 772
  3.6 16.4 %copy-start.1 = (s32[32]{0:T(128)S(1)}, s32[32]{0:T(128)}, u32[]{:S(2)}) copy-start(s32[32]{0:T(128)} %param.19) | copy-start | bytes 388
  5.1 18.9 %all-to-all-start = ((bf16[8,192,128]{2,1,0:T(8,128)(2,1)}), bf16[8,192,128]{2,1,0:T(8,128)(2,1)S(1)}, u32[]{:S(2)}, u32[]{:S(2)}) async-start(bf16[8,192,128]{2,1,0:T(8,128)(2,1)} %bitcast.5), calls=%async_computation | async-start | bytes 786432 | tf_op jit(solution)/shard_map/all_to_all | solution.py:80
  25.1 11.7 %all-to-all-start.1 = ((bf16[8,4,12,128]{3,1,2,0:T(4,128)(2,1)}), bf16[8,4,12,128]{3,1,2,0:T(4,128)(2,1)S(1)}, u32[]{:S(2)}, u32[]{:S(2)}) async-start(bf16[8,4,12,128]{3,1,2,0:T(4,128)(2,1)} %copy.147), calls=%async_computation.1 | async-start | bytes 196608 | tf_op jit(solution)/shard_map/all_to_all | solution.py:111
  60.9 5.8 %copy-start.4 = (s32[32]{0:T(128)S(1)}, s32[32]{0:T(128)}, u32[]{:S(2)}) copy-start(s32[32]{0:T(128)} %param.23) | copy-start | bytes 388
  60.9 5.8 %copy-start.3 = (f32[32,2]{0,1:T(2,128)S(1)}, f32[32,2]{0,1:T(2,128)}, u32[]{:S(2)}) copy-start(f32[32,2]{0,1:T(2,128)} %param.22) | copy-start | bytes 772
  64.1 23.2 %all-to-all-start.3 = ((f32[32,48,128]{2,1,0:T(8,128)}), f32[32,48,128]{2,1,0:T(8,128)S(1)}, u32[]{:S(2)}, u32[]{:S(2)}) async-start(f32[32,48,128]{2,1,0:T(8,128)} %bitcast.37), calls=%async_computation.3 | async-start | bytes 1572864 | tf_op jit(solution)/shard_map/all_to_all | solution.py:194
